TPU v7x, 256 devices: a whole 4x4x8 slice. The times are simulated.
256 devices in a mesh: sec: 2 (over y_hi), gx: 16 (over y_lo, z), gy: 8 (over x, core).
Axes of the slice: x: 4, y: 4 (y_hi: 2, y_lo: 2; y = y_hi * 2 + y_lo), z: 8, core: 2. Of those that a mesh axis runs over, the one named last changes fastest.
Arguments:
- ocean_velocity: float32 [2, 8, 1024, 2048], P(None, None, 'gx', ('sec', 'gy')), may hold values from -6 to 6
- wind_stress: float32 [2, 1024, 2048], P(None, 'gx', ('sec', 'gy')), may hold values from -6 to 6
- level_counts: int32 [1024, 2048], P('gx', ('sec', 'gy')), may hold values from 1 to 8
- floe_position: float32 [16, 16, 2, 2048], P('gx', ('sec', 'gy')), may hold values from 0 to 4
- floe_velocity: float32 [16, 16, 2, 2048], P('gx', ('sec', 'gy')), may hold values from -3 to 3
- floe_radius: float32 [16, 16, 2048], P('gx', ('sec', 'gy')), may hold values from 0.5 to 1.5
- floe_mass: float32 [16, 16, 2048], P('gx', ('sec', 'gy')), may hold values from 0.5 to 5
- floe_polygon: float32 [16, 16, 32, 2048], P('gx', ('sec', 'gy')), may hold values from -2 to 2
- remap_cells: int32 [16, 16, 2048], P('gx', ('sec', 'gy')), may hold values from 0 to 131071, as said below
- contact_count: int32 [16, 16], P('gx', ('sec', 'gy')), may hold values from 8 to 64, as said below
- contact_list: int32 [16, 16, 3, 64], P('gx', ('sec', 'gy')), may hold values from 0 to 15, as said below
- move_index: int32 [16, 16, 8, 128], P('gx', ('sec', 'gy')), may hold values from 0 to 2047, as said below
- move_count: int32 [16, 16, 8], P('gx', ('sec', 'gy')), may hold values from 42 to 128, as said below
Outputs:
- ocean_next: float32 [2, 8, 1024, 2048], P(None, None, 'gx', ('sec', 'gy'))
- floe_next: float32 [16, 16, 4, 2048], P('gx', ('sec', 'gy'))
- arrivals: float32 [16, 16, 8, 38, 128], P('gx', ('sec', 'gy'))
Inputs may be any that keep to these rules, and one draw needn't show every extreme that they name: `contact_list`: row 0 of each slot names a block of the tile, 0 to 15; row 1 a source 0 to 8, 4 meaning the tile itself; row 2 a block of the source: 0 to 15 for source 4, else 0 to 3. Only the first contact_count slots count. `contact_count`: some tile uses all 64 slots in every draw. `move_index`: the floes named by one tile over all directions and slots are distinct. `move_count`: every tile fills all 128 slots towards at least one neighbour. `remap_cells`: Row-major index over the 1024 rows and the tile's 128 columns. The floes of tile row i lie in grid rows i * 64 - 64 // 2 to i * 64 + 64 + 64 // 2 - 1 (within the grid), and every tile has floes in the first and the last row of that band.
All inputs are finite; a program needn't handle non-finite values.
Results may differ from a plain program's by a relative error of at most 0.0003.
Values sent between devices are 32-bit elements; how exact they have to be, the bound alone decides.
No kernel may reach another device: no remote copies, remote signals or barrier semaphores. Data moves between devices by JAX's collectives and lax.ppermute only.
A program may use at most 64 MiB of HBM per device.

v0:
```python
import math

import jax
import jax.numpy as jnp
from jax import lax
from jax.experimental import pallas as pl
from jax.experimental.pallas import tpu as pltpu
from jax.sharding import PartitionSpec as P

OSTEPS = 4
GHOST = 4


SOFTEN = 0.1
STIFFNESS = 0.1
DAMPING = 0.05
VERT_MIX = 0.15
CORIOLIS = 0.1
SURFACE_GAIN = 0.25
WATER_DRAG = 0.1
AIR_GAIN = 0.2
ICE_STEP = 0.5
PLACES = (0, 1, 2, 3, 5, 6, 7, 8)


def with_halo(array, sides, width):
    for axis, dim in sides:
        size, length = (lax.axis_size(axis), array.shape[dim])
        up = [(i, (i + 1) % size) for i in range(size - 1)]
        down = [(j, i) for i, j in up]
        last = lax.slice_in_dim(array, length - width, length, axis=dim)
        leading = lax.slice_in_dim(array, 0, width, axis=dim)
        before = lax.ppermute(last, axis, up)
        after = lax.ppermute(leading, axis, down)
        array = jnp.concatenate([before, array, after], axis=dim)
    return array


def ocean_substep(flow, padded, wet, wind):
    levels_here = flow.shape[1]
    lap = (
        padded[:, :, :-2, 1:-1]
        + padded[:, :, 2:, 1:-1]
        + padded[:, :, 1:-1, :-2]
        + padded[:, :, 1:-1, 2:]
        - 4.0 * flow
    )
    depth = jnp.arange(levels_here, dtype=jnp.float32)
    horizontal = (0.15 - 0.05 * depth / levels_here)[None, :, None, None]
    flux = VERT_MIX * (flow[:, 1:] - flow[:, :-1]) * wet[None, 1:]
    empty = jnp.zeros_like(flow[:, :1])
    vert = jnp.concatenate([flux, empty], axis=1) - jnp.concatenate([empty, flux], axis=1)
    turning = jnp.stack([CORIOLIS * flow[1], -CORIOLIS * flow[0]])
    surface = jnp.concatenate([SURFACE_GAIN * wind[:, None], jnp.zeros_like(flow[:, 1:])], axis=1)
    return (flow + horizontal * lap + vert + turning + surface) * wet[None]


def pair_forces(first, second):
    own = first[:, :, None, :]
    other = second[:, :, :, None]
    delta_x = own[:, 0] - other[:, 0]
    delta_y = own[:, 1] - other[:, 1]
    inverse = lax.rsqrt(delta_x * delta_x + delta_y * delta_y + SOFTEN * SOFTEN)
    distance = (delta_x * delta_x + delta_y * delta_y + SOFTEN * SOFTEN) * inverse
    reach = own[:, 4] + other[:, 4]
    intersection = jnp.maximum(reach - distance, 0.0)
    reduced = own[:, 4] * other[:, 4] / reach
    normal_x = delta_x * inverse
    normal_y = delta_y * inverse
    closing = (own[:, 2] - other[:, 2]) * normal_x + (own[:, 3] - other[:, 3]) * normal_y
    magnitude = intersection * reduced * (STIFFNESS - DAMPING * closing)
    return jnp.stack(
        [jnp.sum(magnitude * normal_x, axis=1), jnp.sum(magnitude * normal_y, axis=1)], axis=1
    )


def block_table(own, ghosts):
    blocks = own.shape[1] // 128
    edge_blocks = ghosts.shape[2] // 128
    mine = own.reshape(5, blocks, 128).transpose(1, 0, 2)
    theirs = (
        ghosts.reshape(8, 5, edge_blocks, 128)
        .transpose(0, 2, 1, 3)
        .reshape(8 * edge_blocks, 5, 128)
    )
    return jnp.concatenate([mine, theirs], axis=0)


def contact_batch(table, lists, valid, blocks, edge_blocks):
    source = lists[1]
    neighbour = source - (source > 4).astype(jnp.int32)
    partner = jnp.where(source == 4, lists[2], blocks + neighbour * edge_blocks + lists[2])
    forces = pair_forces(table[lists[0]], table[partner])
    forces = jnp.where(valid[:, None, None], forces, 0.0)
    onehot = (lists[0][:, None] == jnp.arange(blocks, dtype=jnp.int32)[None, :]).astype(jnp.float32)
    return jnp.einsum("pn,pcf->ncf", onehot, forces, precision=lax.Precision.HIGHEST)


def split_parts(x):
    high = x.astype(jnp.bfloat16).astype(jnp.float32)
    rest = x - high
    middle = rest.astype(jnp.bfloat16).astype(jnp.float32)
    low = (rest - middle).astype(jnp.bfloat16).astype(jnp.float32)
    return high, middle, low


def stacked_select(stack_ref, x, onehot):
    rows = x.shape[0]
    pitch = stack_ref.shape[0] // 3
    for part, value in enumerate(split_parts(x)):
        stack_ref[part * pitch : part * pitch + rows, :] = value
    picked = jnp.dot(
        stack_ref[...].astype(jnp.bfloat16), onehot, preferred_element_type=jnp.float32
    )
    return (picked[0:rows] + picked[pitch : pitch + rows]) + picked[2 * pitch : 2 * pitch + rows]


def sample_kernel(window_ref, rows_ref, cols_ref, out_ref, stack_ref):
    window_rows, window_cols = window_ref.shape[1:]
    floes = rows_ref.shape[1]
    onehot = (
        lax.broadcasted_iota(jnp.int32, (window_rows, floes), 0) == rows_ref[...]
    ).astype(jnp.bfloat16)
    pick = lax.broadcasted_iota(jnp.int32, (window_cols, floes), 0) == cols_ref[...]
    for channel in range(window_ref.shape[0]):
        picked = stacked_select(stack_ref, window_ref[channel].T, onehot)
        out_ref[channel : channel + 1, :] = jnp.sum(
            jnp.where(pick, picked, 0.0), axis=0, keepdims=True
        )


def sample_surface(window, rows, cols):
    return pl.pallas_call(
        sample_kernel,
        out_shape=jax.ShapeDtypeStruct((window.shape[0], rows.shape[1]), jnp.float32),
        scratch_shapes=[pltpu.VMEM((3 * window.shape[2], window.shape[1]), jnp.float32)],
    )(window, rows, cols)


def gather_kernel(state_ref, radius_ref, mass_ref, polygon_ref, index_ref, out_ref, record_ref, stack_ref):
    floes = state_ref.shape[1]
    slots = index_ref.shape[1]
    width = out_ref.shape[1]
    record_ref[...] = jnp.zeros_like(record_ref)
    stack_ref[...] = jnp.zeros_like(stack_ref)
    record_ref[0:4, :] = state_ref[...]
    record_ref[4:5, :] = radius_ref[...]
    record_ref[5:6, :] = mass_ref[...]
    record_ref[6:width, :] = polygon_ref[...]
    record = record_ref[...]
    for way in range(index_ref.shape[0]):
        onehot = (
            lax.broadcasted_iota(jnp.int32, (floes, slots), 0) == index_ref[way : way + 1, :]
        ).astype(jnp.bfloat16)
        out_ref[way] = stacked_select(stack_ref, record, onehot)[0:width]


def gather_records(state, radius, mass, polygon, index):
    width = 6 + polygon.shape[0]
    padded = -(-width // 16) * 16
    return pl.pallas_call(
        gather_kernel,
        out_shape=jax.ShapeDtypeStruct((index.shape[0], width, index.shape[1]), jnp.float32),
        scratch_shapes=[
            pltpu.VMEM((padded, state.shape[1]), jnp.float32),
            pltpu.VMEM((3 * padded, state.shape[1]), jnp.float32),
        ],
    )(state, radius, mass, polygon, index)


def exchange(low, high, axis):
    size = lax.axis_size(axis)
    up = [(i, i + 1) for i in range(size - 1)]
    down = [(i + 1, i) for i in range(size - 1)]
    from_previous = lax.ppermute(high, axis, up)
    from_next = lax.ppermute(low, axis, down)
    return from_previous, from_next


def shards(
    ocean_velocity,
    wind_stress,
    level_counts,
    floe_position,
    floe_velocity,
    floe_radius,
    floe_mass,
    floe_polygon,
    remap_cells,
    contact_count,
    contact_list,
    move_index,
    move_count,
):
    columns = ("sec", "gy")
    comps, levels_here, rows_here, cols_here = ocean_velocity.shape
    halo = OSTEPS
    position = floe_position[0, 0]
    velocity = floe_velocity[0, 0]
    radius = floe_radius[0, 0]
    mass = floe_mass[0, 0]
    cells = remap_cells[0, 0]
    floes = position.shape[1]
    blocks = floes // 128
    record = jnp.concatenate([position, velocity, radius[None]], axis=0)
    edge = record[:, : GHOST * 128]
    edge_size = edge.size

    fields = jnp.concatenate(
        [
            ocean_velocity.reshape(comps * levels_here, rows_here, cols_here),
            wind_stress,
            level_counts.astype(jnp.float32)[None],
        ],
        axis=0,
    )
    channels = fields.shape[0]
    row_strip = channels * halo * cols_here
    low = jnp.concatenate([fields[:, :halo].reshape(-1), edge.reshape(-1)])
    high = jnp.concatenate([fields[:, -halo:].reshape(-1), edge.reshape(-1)])
    above, below = exchange(low, high, "gx")
    extended = jnp.concatenate(
        [
            above[:row_strip].reshape(channels, halo, cols_here),
            fields,
            below[:row_strip].reshape(channels, halo, cols_here),
        ],
        axis=1,
    )
    ghost_column = jnp.stack(
        [above[row_strip:].reshape(edge.shape), edge, below[row_strip:].reshape(edge.shape)]
    )
    ext_rows = rows_here + 2 * halo
    col_strip = channels * ext_rows * halo
    low = jnp.concatenate([extended[:, :, :halo].reshape(-1), ghost_column.reshape(-1)])
    high = jnp.concatenate([extended[:, :, -halo:].reshape(-1), ghost_column.reshape(-1)])
    left, right = exchange(low, high, columns)
    extended = jnp.concatenate(
        [
            left[:col_strip].reshape(channels, ext_rows, halo),
            extended,
            right[:col_strip].reshape(channels, ext_rows, halo),
        ],
        axis=2,
    )
    ghost_left = left[col_strip:].reshape(3, *edge.shape)
    ghost_right = right[col_strip:].reshape(3, *edge.shape)
    beside = [ghost_left, ghost_column, ghost_right]
    ghosts = jnp.stack([beside[p % 3][p // 3] for p in PLACES])

    ext_cols = cols_here + 2 * halo
    counts_ext = extended[-1]
    wet = (jnp.arange(levels_here, dtype=jnp.float32)[:, None, None] < counts_ext[None]).astype(
        jnp.float32
    )
    wind_ext = extended[comps * levels_here : comps * levels_here + 2]
    flow = extended[: comps * levels_here].reshape(comps, levels_here, ext_rows, ext_cols) * wet[None]
    for substep in range(OSTEPS):
        padded = jnp.pad(flow, ((0, 0), (0, 0), (1, 1), (1, 1)))
        flow = ocean_substep(flow, padded, wet, wind_ext)
    flow = flow[:, :, halo : halo + rows_here, halo : halo + cols_here]

    table = block_table(record, ghosts)
    surface = jnp.stack([flow[0, 0], flow[1, 0], wind_stress[0], wind_stress[1]])
    margin = rows_here // 2
    from_above, from_below = exchange(surface[:, :margin], surface[:, -margin:], "gx")
    near = jnp.concatenate([from_above, surface, from_below], axis=1)
    first_row = lax.axis_index("gx") * rows_here - margin
    sampled = sample_surface(
        near,
        (cells // cols_here - first_row)[None],
        (cells % cols_here)[None],
    )
    lists = contact_list[0, 0]
    count = contact_count[0, 0]
    slots = lists.shape[1]
    sizes = sorted({min(slots, size) for size in (16, 32, slots)})

    def pass_over(size):
        def run(lists, count):
            valid = jnp.arange(size, dtype=jnp.int32) < count
            return contact_batch(table, lists[:, :size], valid, blocks, GHOST)

        return run

    which = sum((count > size).astype(jnp.int32) for size in sizes[:-1])
    contact = lax.switch(which, [pass_over(size) for size in sizes], lists, count)
    contact = contact.transpose(1, 0, 2).reshape(2, floes)
    area = math.pi * radius * radius
    relative = sampled[0:2] - velocity
    speed = jnp.sqrt(jnp.sum(relative * relative, axis=0, keepdims=True))
    total = contact + area[None] * (WATER_DRAG * speed * relative + AIR_GAIN * sampled[2:4])
    new_velocity = velocity + ICE_STEP * total / mass[None]
    new_position = position + ICE_STEP * new_velocity
    floe_next = jnp.concatenate([new_position, new_velocity], axis=0)
    leaving = move_index[0, 0]
    capacity = leaving.shape[1]
    valid_slots = jnp.arange(capacity, dtype=jnp.int32)[None, :] < move_count[0, 0][:, None]
    outgoing = gather_records(
        floe_next, radius[None], mass[None], floe_polygon[0, 0], jnp.where(valid_slots, leaving, -1)
    )
    from_above, from_below = exchange(outgoing[0:3], outgoing[5:8], "gx")
    heading_left = jnp.stack([from_below[0], outgoing[3], from_above[0]])
    heading_right = jnp.stack([from_below[2], outgoing[4], from_above[2]])
    from_left, from_right = exchange(heading_left, heading_right, columns)
    arrivals = jnp.stack(
        [
            from_right[0],
            from_below[1],
            from_left[0],
            from_right[1],
            from_left[1],
            from_right[2],
            from_above[1],
            from_left[2],
        ]
    )
    return (flow, floe_next[None, None], arrivals[None, None])


def solution(mesh):
    return jax.shard_map(
        shards,
        mesh=mesh,
        in_specs=(
            P(None, None, "gx", ("sec", "gy")),
            P(None, "gx", ("sec", "gy")),
            P("gx", ("sec", "gy")),
            P("gx", ("sec", "gy"), None, None),
            P("gx", ("sec", "gy"), None, None),
            P("gx", ("sec", "gy"), None),
            P("gx", ("sec", "gy"), None),
            P("gx", ("sec", "gy"), None, None),
            P("gx", ("sec", "gy"), None),
            P("gx", ("sec", "gy")),
            P("gx", ("sec", "gy"), None, None),
            P("gx", ("sec", "gy"), None, None),
            P("gx", ("sec", "gy"), None),
        ),
        out_specs=(
            P(None, None, "gx", ("sec", "gy")),
            P("gx", ("sec", "gy"), None, None),
            P("gx", ("sec", "gy"), None, None, None),
        ),
        check_vma=False,
    )
```

profile of v0, /device:TPU:24, one launch (start us, length us, event | category | flops | bytes accessed | tf_op | source)
XLA Modules:
  0.0 97.2 jit_solution(5267624941269948796)
XLA Ops:
  0.7 0.8 pad_maximum_fusion.17
  1.5 0.8 convert_bitcast_fusion
  2.3 0.9 pad_maximum_fusion.15
  3.3 3.8 %collective-permute-start = (f32[12288]{0:T(1024)S(1)}, f32[12288]{0:T(1024)S(1)}, u32[]{:S(2)}, u32[]{:S(2)}) collective-permute-start(f32[12288]{0:T(1024)S(1)} %get-tuple-element.133), channel_id=1, source_target_pairs={{0,8},{8,16},{16,24},{24,32},{32,40},{40,48},{48,56},{56,64},{64,7... | collective-permute-start | bytes 147464 | tf_op jit(solution)/shard_map/ppermute | solution.py:175
  7.1 6.0 %collective-permute-start.1 = (f32[12288]{0:T(1024)S(1)}, f32[12288]{0:T(1024)S(1)}, u32[]{:S(2)}, u32[]{:S(2)}) collective-permute-start(f32[12288]{0:T(1024)S(1)} %get-tuple-element.134), channel_id=1, source_target_pairs={{8,0},{16,8},{24,16},{32,24},{40,32},{48,40},{56,48},{64,56},{72,6... | collective-permute-start | bytes 147464 | tf_op jit(solution)/shard_map/ppermute | solution.py:176
  13.2 0.6 multiply_multiply_fusion
  13.8 0.6 and_select_fusion
  14.4 0.7 bitcast_select_fusion.index_ref
  15.1 0.6 fusion.105.rows_ref
  15.7 0.7 maximum_bitcast_fusion.1
  16.6 0.2 fusion.113
  16.9 0.1 copy-done.9
  17.1 0.4 reshape.551
  17.4 0.4 reshape.554
  17.9 1.9 %collective-permute-start.2 = (f32[13152]{0:T(1024)S(1)}, f32[13152]{0:T(1024)S(1)}, u32[]{:S(2)}, u32[]{:S(2)}) collective-permute-start(f32[13152]{0:T(1024)S(1)} %get-tuple-element.131), channel_id=1, source_target_pairs={{0,1},{1,2},{2,3},{3,4},{4,5},{5,6},{6,7},{7,128},{128,129},{129,1... | collective-permute-start | bytes 157832 | tf_op jit(solution)/shard_map/ppermute | solution.py:175
  19.8 7.3 %collective-permute-start.3 = (f32[13152]{0:T(1024)S(1)}, f32[13152]{0:T(1024)S(1)}, u32[]{:S(2)}, u32[]{:S(2)}) collective-permute-start(f32[13152]{0:T(1024)S(1)} %get-tuple-element.132), channel_id=1, source_target_pairs={{1,0},{2,1},{3,2},{4,3},{5,4},{6,5},{7,6},{128,7},{129,128},{130,1... | collective-permute-start | bytes 157832 | tf_op jit(solution)/shard_map/ppermute | solution.py:176
  27.7 0.6 copy.28
  28.3 0.5 collective-permute-done.3
  28.8 0.7 reshape.555
  29.6 0.7 reshape.553
  30.3 0.1 maximum_bitcast_fusion
  30.4 0.1 fusion.101
  30.6 0.7 pad_maximum_fusion
  31.5 0.1 broadcast_multiply_fusion
  31.6 0.1 slice_multiply_fusion.7
  31.7 0.2 fusion.99
  31.9 1.1 %fusion.92 = f32[2,8,72,136]{3,2,1,0:T(8,128)S(1)} fusion(f32[2,1,72,136]{3,2,1,0:T(8,128)S(1)} %fusion.101, f32[1,8,72,136]{3,2,1,0:T(8,128)S(1)} %get-tuple-element.104, f32[1,8,72,136]{3,2,1,0:T(8,128)S(1)} %get-tuple-element.103, f32[2,7,72,136]{3,2,1,0:T(8,128)S(1)} %fusion.99, f32[2,8,72,136]{3,2,1,0:T(8,128)S(1)} %broadcast_multiply_fusion, ...), kind=kLoop, calls=%fused_computation.173 | loop fusion | flops 2036736 | bytes 2820128 | tf_op jit(solution)/shard_map/mul | solution.py:55
  33.0 0.2 fusion.98
  33.1 0.1 slice_multiply_fusion.5
  33.3 1.1 %fusion.93 = f32[2,8,72,136]{3,2,1,0:T(8,128)S(1)} fusion(f32[2,1,72,136]{3,2,1,0:T(8,128)S(1)} %fusion.101, f32[1,8,72,136]{3,2,1,0:T(8,128)S(1)} %get-tuple-element.102, f32[1,8,72,136]{3,2,1,0:T(8,128)S(1)} %get-tuple-element.101, f32[2,7,72,136]{3,2,1,0:T(8,128)S(1)} %fusion.98, f32[2,8,72,136]{3,2,1,0:T(8,128)S(1)} %fusion.92, ...), kind=kLoop, calls=%fused_computation.174 | loop fusion | flops 2036736 | bytes 2820128 | tf_op jit(solution)/shard_map/mul | solution.py:55
  34.4 0.2 fusion.97
  34.5 0.1 slice_multiply_fusion.3
  34.6 1.1 %fusion.94 = f32[2,8,72,136]{3,2,1,0:T(8,128)S(1)} fusion(f32[2,1,72,136]{3,2,1,0:T(8,128)S(1)} %fusion.101, f32[1,8,72,136]{3,2,1,0:T(8,128)S(1)} %get-tuple-element.100, f32[1,8,72,136]{3,2,1,0:T(8,128)S(1)} %get-tuple-element.99, f32[2,7,72,136]{3,2,1,0:T(8,128)S(1)} %fusion.97, f32[2,8,72,136]{3,2,1,0:T(8,128)S(1)} %fusion.93, ...), kind=kLoop, calls=%fused_computation.175 | loop fusion | flops 2036736 | bytes 2820128 | tf_op jit(solution)/shard_map/mul | solution.py:55
  35.7 0.1 fusion.96
  35.9 1.2 %slice_multiply_fusion.1 = (f32[1,8,72,136]{3,2,1,0:T(8,128)}, f32[1,8,72,136]{3,2,1,0:T(8,128)}) fusion(f32[2,8,72,136]{3,2,1,0:T(8,128)S(1)} %fusion.94), kind=kLoop, calls=%fused_computation.187 | loop fusion | flops 156672 | bytes 1253376 | tf_op jit(solution)/shard_map/mul | solution.py:53
  37.2 0.1 fusion.120
  37.5 0.2 copy-done.21
  37.8 2.2 %fusion.95 = f32[2,8,72,136]{3,2,1,0:T(8,128)S(1)} fusion(f32[2,1,72,136]{3,2,1,0:T(8,128)S(1)} %fusion.101, f32[1,8,72,136]{3,2,1,0:T(8,128)} %get-tuple-element.98, f32[1,8,72,136]{3,2,1,0:T(8,128)} %get-tuple-element.97, f32[2,7,72,136]{3,2,1,0:T(8,128)S(1)} %fusion.96, f32[2,8,72,136]{3,2,1,0:T(8,128)S(1)} %fusion.94, f32[8]{0:T(128)S(1)} %copy-done.21, ...), kind=kLoop, calls=%fused_computation.176 | loop fusion | flops 2036736 | bytes 2820128 | tf_op jit(solution)/shard_map/mul | solution.py:55
  40.0 0.1 slice_bitcast_fusion.4
  40.1 1.9 %collective-permute-start.4 = (f32[4,32,128]{2,1,0:T(8,128)S(1)}, f32[4,32,128]{2,1,0:T(8,128)S(1)}, u32[]{:S(2)}, u32[]{:S(2)}) collective-permute-start(f32[4,32,128]{2,1,0:T(8,128)S(1)} %get-tuple-element.117), channel_id=1, source_target_pairs={{0,8},{8,16},{16,24},{24,32},{32,40},{40,48},{48,56},{56,64},{64,7... | collective-permute-start | bytes 196616 | tf_op jit(solution)/shard_map/ppermute | solution.py:175
  42.1 6.0 %collective-permute-start.5 = (f32[4,32,128]{2,1,0:T(8,128)S(1)}, f32[4,32,128]{2,1,0:T(8,128)S(1)}, u32[]{:S(2)}, u32[]{:S(2)}) collective-permute-start(f32[4,32,128]{2,1,0:T(8,128)S(1)} %get-tuple-element.118), channel_id=1, source_target_pairs={{8,0},{16,8},{24,16},{32,24},{40,32},{48,40},{56,48},{64,56},{72,6... | collective-permute-start | bytes 196616 | tf_op jit(solution)/shard_map/ppermute | solution.py:176
  48.2 4.1 %conditional.1 = (f32[16,2,128]{2,0,1:T(8,128)S(1)}) conditional(s32[]{:T(128)} %clamp.3, (s32[3,64]{1,0:T(4,128)S(1)}, s32[]{:T(128)}, f32[48,5,128]{2,1,0:T(8,128)S(1)}) %tuple.82, (s32[3,64]{1,0:T(4,128)S(1)}, s32[]{:T(128)}, f32[48,5,128]{2,1,0:T(8,128)S(1)}) %tuple.83, (s32[3,64]{1,0:T(4,128)S(1)}, s32[]{:T(128)}, ...), branch_computations={%region_0.3_spmd, %region_3.6_spmd, %region_6.9_spmd} | conditional | flops 31477696 | bytes 1797260 | solution.py:287
  48.2 0.7 iota_compare_fusion.1
  48.9 0.6 gather_fusion.1
  49.5 0.6 gather_fusion
  50.1 1.8 %multiply_reduce_fusion.1 = (f32[16,128]{1,0:T(8,128)S(1)}, f32[16,128]{1,0:T(8,128)S(1)}) fusion(f32[16,128]{1,0:T(8,128)S(1)} %bitcast.224, f32[16,128]{1,0:T(8,128)S(1)} %bitcast.219, f32[16,128]{1,0:T(8,128)S(1)} %bitcast.225, f32[16,128]{1,0:T(8,128)S(1)} %bitcast.220, f32[16,128]{1,0:T(8,128)S(1)} %bitcast.222, f32[16,128]{1,0:T(8,128)S(1)} %bitcast.217, ...), kind=kLoop, calls=%fused_computation.19 | loop fusion | flops 7073792 | bytes 98304 | tf_op jit(solution)/shard_map/cond/branch_0_fun/reduce_sum | solution.py:73
  51.9 0.2 fusion.5
  52.3 0.7 pad_maximum_fusion.2.window_ref
  53.0 3.5 %shard_map.148 = f32[4,2048]{1,0:T(4,128)} custom-call(f32[4,128,128]{2,1,0:T(8,128)} %pad_maximum_fusion.2.window_ref, s32[1,2048]{1,0:T(1,128)} %fusion.105.rows_ref, s32[1,2048]{1,0:T(1,128)} %get-tuple-element.51.cols_ref), custom_call_target="tpu_custom_call" | custom-call | tf_op jit(solution)/shard_map/pallas_call | solution.py:133
  56.5 0.8 multiply_reduce_fusion.6
  57.4 0.9 multiply_add_fusion
  58.3 0.6 pad_maximum_fusion.16
  58.9 3.2 %shard_map.149 = f32[8,38,128]{2,1,0:T(8,128)} custom-call(f32[4,2048]{1,0:T(4,128)} %get-tuple-element.129.state_ref, f32[1,2048]{1,0:T(1,128)} %bitcast.187, f32[1,2048]{1,0:T(1,128)} %bitcast.200, f32[32,2048]{1,0:T(8,128)} %bitcast.179, s32[8,128]{1,0:T(8,128)} %bitcast_select_fusion.index_ref), custom_call_target="tpu_custom_call" | custom-call | tf_op jit(solution)/shard_map/pallas_call | solution.py:161
  62.1 0.9 fusion.115
  63.0 4.1 %collective-permute-start.6 = (f32[3,38,128]{2,1,0:T(8,128)S(1)}, f32[3,38,128]{2,1,0:T(8,128)S(1)}, u32[]{:S(2)}, u32[]{:S(2)}) collective-permute-start(f32[3,38,128]{2,1,0:T(8,128)S(1)} %get-tuple-element.111), channel_id=1, source_target_pairs={{8,0},{16,8},{24,16},{32,24},{40,32},{48,40},{56,48},{64,56},{72,6... | collective-permute-start | bytes 175112 | tf_op jit(solution)/shard_map/ppermute | solution.py:176
  67.0 1.9 %collective-permute-start.7 = (f32[3,38,128]{2,1,0:T(8,128)S(1)}, f32[3,38,128]{2,1,0:T(8,128)S(1)}, u32[]{:S(2)}, u32[]{:S(2)}) collective-permute-start(f32[3,38,128]{2,1,0:T(8,128)S(1)} %get-tuple-element.112), channel_id=1, source_target_pairs={{0,8},{8,16},{16,24},{24,32},{32,40},{40,48},{48,56},{56,64},{64,7... | collective-permute-start | bytes 175112 | tf_op jit(solution)/shard_map/ppermute | solution.py:175
  69.0 0.8 fusion.114
  69.7 5.6 %collective-permute-done.7 = f32[3,38,128]{2,1,0:T(8,128)S(1)} collective-permute-done((f32[3,38,128]{2,1,0:T(8,128)S(1)}, f32[3,38,128]{2,1,0:T(8,128)S(1)}, u32[]{:S(2)}, u32[]{:S(2)}) %collective-permute-start.7) | collective-permute-done | bytes 58400 | tf_op jit(solution)/shard_map/ppermute | solution.py:175
  75.4 10.0 %collective-permute-start.8 = (f32[3,38,128]{2,1,0:T(8,128)S(1)}, f32[3,38,128]{2,1,0:T(8,128)S(1)}, u32[]{:S(2)}, u32[]{:S(2)}) collective-permute-start(f32[3,38,128]{2,1,0:T(8,128)S(1)} %pad_maximum_fusion.8), channel_id=1, source_target_pairs={{1,0},{2,1},{3,2},{4,3},{5,4},{6,5},{7,6},{128,7},{129,128},{130,1... | collective-permute-start | bytes 175112 | tf_op jit(solution)/shard_map/ppermute | solution.py:176
  85.4 1.8 %collective-permute-done.8 = f32[3,38,128]{2,1,0:T(8,128)S(1)} collective-permute-done((f32[3,38,128]{2,1,0:T(8,128)S(1)}, f32[3,38,128]{2,1,0:T(8,128)S(1)}, u32[]{:S(2)}, u32[]{:S(2)}) %collective-permute-start.8) | collective-permute-done | bytes 58400 | tf_op jit(solution)/shard_map/ppermute | solution.py:176
  87.2 1.9 %collective-permute-start.9 = (f32[3,38,128]{2,1,0:T(8,128)S(1)}, f32[3,38,128]{2,1,0:T(8,128)S(1)}, u32[]{:S(2)}, u32[]{:S(2)}) collective-permute-start(f32[3,38,128]{2,1,0:T(8,128)S(1)} %pad_maximum_fusion.9), channel_id=1, source_target_pairs={{0,1},{1,2},{2,3},{3,4},{4,5},{5,6},{6,7},{7,128},{128,129},{129,1... | collective-permute-start | bytes 175112 | tf_op jit(solution)/shard_map/ppermute | solution.py:175
  89.2 2.3 %slice.599 = f32[2,8,64,128]{3,2,1,0:T(8,128)} slice(f32[2,8,72,136]{3,2,1,0:T(8,128)} %copy-done.2), slice={[0:2], [0:8], [4:68], [4:132]} | slice | bytes 1048576 | tf_op jit(solution)/shard_map/slice | solution.py:261
  91.4 5.0 %collective-permute-done.9 = f32[3,38,128]{2,1,0:T(8,128)S(1)} collective-permute-done((f32[3,38,128]{2,1,0:T(8,128)S(1)}, f32[3,38,128]{2,1,0:T(8,128)S(1)}, u32[]{:S(2)}, u32[]{:S(2)}) %collective-permute-start.9) | collective-permute-done | bytes 58400 | tf_op jit(solution)/shard_map/ppermute | solution.py:175
  96.5 0.7 copy.18
  (115 shorter events, 1.0 us)
Async XLA Ops:
  0.6 12.5 %copy-start.11 = (f32[1,1,2048]{2,1,0:T(1,128)S(1)}, f32[1,1,2048]{2,1,0:T(1,128)}, u32[]{:S(2)}) copy-start(f32[1,1,2048]{2,1,0:T(1,128)} %param.21) | copy-start | bytes 24580
  0.6 15.0 %copy-start.5 = (f32[1,1,2,2048]{3,2,1,0:T(2,128)S(1)}, f32[1,1,2,2048]{3,2,1,0:T(2,128)}, u32[]{:S(2)}) copy-start(f32[1,1,2,2048]{3,2,1,0:T(2,128)} %param.19) | copy-start | bytes 49156
  0.7 15.0 %copy-start.3 = (f32[1,1,2,2048]{3,2,1,0:T(2,128)S(1)}, f32[1,1,2,2048]{3,2,1,0:T(2,128)}, u32[]{:S(2)}) copy-start(f32[1,1,2,2048]{3,2,1,0:T(2,128)} %param.20) | copy-start | bytes 49156
  0.7 15.9 %copy-start.1 = (f32[2,64,128]{2,1,0:T(8,128)S(1)}, f32[2,64,128]{2,1,0:T(8,128)}, u32[]{:S(2)}) copy-start(f32[2,64,128]{2,1,0:T(8,128)} %param.17) | copy-start | bytes 196612
  0.7 15.9 %copy-start = (f32[2,8,64,128]{3,2,1,0:T(8,128)S(1)}, f32[2,8,64,128]{3,2,1,0:T(8,128)}, u32[]{:S(2)}) copy-start(f32[2,8,64,128]{3,2,1,0:T(8,128)} %param.16) | copy-start | bytes 1572868
  0.7 13.1 %copy-start.16 = (s32[1,1,2048]{2,1,0:T(1,128)S(1)}, s32[1,1,2048]{2,1,0:T(1,128)}, u32[]{:S(2)}) copy-start(s32[1,1,2048]{2,1,0:T(1,128)} %param.24) | copy-start | bytes 24580
  0.7 13.7 %copy-start.24 = (s32[1,1,8]{2,1,0:T(1,128)S(1)}, s32[1,1,8]{2,1,0:T(1,128)}, u32[]{:S(2)}) copy-start(s32[1,1,8]{2,1,0:T(1,128)} %param.28) | copy-start | bytes 100
  0.7 13.7 %copy-start.22 = (s32[1,1,8,128]{3,2,1,0:T(8,128)S(1)}, s32[1,1,8,128]{3,2,1,0:T(8,128)}, u32[]{:S(2)}) copy-start(s32[1,1,8,128]{3,2,1,0:T(8,128)} %param.27) | copy-start | bytes 12292
  3.3 13.1 %collective-permute-start = (f32[12288]{0:T(1024)S(1)}, f32[12288]{0:T(1024)S(1)}, u32[]{:S(2)}, u32[]{:S(2)}) collective-permute-start(f32[12288]{0:T(1024)S(1)} %get-tuple-element.133), channel_id=1, source_target_pairs={{0,8},{8,16},{16,24},{24,32},{32,40},{40,48},{48,56},{56,64},{64,7... | collective-permute-start | bytes 147464 | tf_op jit(solution)/shard_map/ppermute | solution.py:175
  7.1 9.3 %collective-permute-start.1 = (f32[12288]{0:T(1024)S(1)}, f32[12288]{0:T(1024)S(1)}, u32[]{:S(2)}, u32[]{:S(2)}) collective-permute-start(f32[12288]{0:T(1024)S(1)} %get-tuple-element.134), channel_id=1, source_target_pairs={{8,0},{16,8},{24,16},{32,24},{40,32},{48,40},{56,48},{64,56},{72,6... | collective-permute-start | bytes 147464 | tf_op jit(solution)/shard_map/ppermute | solution.py:176
  16.4 0.6 copy-start.9
  16.5 0.6 copy-start.7
  17.1 10.7 %copy-start.23 = (s32[1,1,3,64]{3,1,2,0:T(1,128)S(1)}, s32[1,1,3,64]{3,1,2,0:T(1,128)}, u32[]{:S(2)}) copy-start(s32[1,1,3,64]{3,1,2,0:T(1,128)} %param.26) | copy-start | bytes 2308
  17.9 11.7 %collective-permute-start.2 = (f32[13152]{0:T(1024)S(1)}, f32[13152]{0:T(1024)S(1)}, u32[]{:S(2)}, u32[]{:S(2)}) collective-permute-start(f32[13152]{0:T(1024)S(1)} %get-tuple-element.131), channel_id=1, source_target_pairs={{0,1},{1,2},{2,3},{3,4},{4,5},{5,6},{6,7},{7,128},{128,129},{129,1... | collective-permute-start | bytes 157832 | tf_op jit(solution)/shard_map/ppermute | solution.py:175
  19.8 9.0 %collective-permute-start.3 = (f32[13152]{0:T(1024)S(1)}, f32[13152]{0:T(1024)S(1)}, u32[]{:S(2)}, u32[]{:S(2)}) collective-permute-start(f32[13152]{0:T(1024)S(1)} %get-tuple-element.132), channel_id=1, source_target_pairs={{1,0},{2,1},{3,2},{4,3},{5,4},{6,5},{7,6},{128,7},{129,128},{130,1... | collective-permute-start | bytes 157832 | tf_op jit(solution)/shard_map/ppermute | solution.py:176
  27.1 7.6 %copy-start.20 = (f32[8]{0:T(128)}, f32[8]{0:T(128)S(1)}, u32[]{:S(2)}) copy-start(f32[8]{0:T(128)S(1)} %multiply_subtract_fusion) | copy-start | bytes 100
  28.8 1.6 %copy-start.12 = (f32[13152]{0:T(1024)}, f32[13152]{0:T(1024)S(1)}, u32[]{:S(2)}) copy-start(f32[13152]{0:T(1024)S(1)} %collective-permute-done.3) | copy-start | bytes 157828
  29.6 0.7 copy-start.14
  35.9 1.2 %copy-start.15 = (f32[13152]{0:T(1024)S(1)}, f32[13152]{0:T(1024)}, u32[]{:S(2)}) copy-start(f32[13152]{0:T(1024)} %copy-done.14) | copy-start | bytes 157828
  35.9 1.3 %copy-start.13 = (f32[13152]{0:T(1024)S(1)}, f32[13152]{0:T(1024)}, u32[]{:S(2)}) copy-start(f32[13152]{0:T(1024)} %copy-done.12) | copy-start | bytes 157828
  35.9 1.4 %copy-start.10 = (f32[1,5,512]{2,1,0:T(8,128)S(1)}, f32[1,5,512]{2,1,0:T(8,128)}, u32[]{:S(2)}) copy-start(f32[1,5,512]{2,1,0:T(8,128)} %copy-done.9) | copy-start | bytes 30724
  35.9 1.5 %copy-start.8 = (f32[1,5,512]{2,1,0:T(8,128)S(1)}, f32[1,5,512]{2,1,0:T(8,128)}, u32[]{:S(2)}) copy-start(f32[1,5,512]{2,1,0:T(8,128)} %copy-done.7) | copy-start | bytes 30724
  37.1 0.7 copy-start.21
  37.7 10.4 %copy-start.4 = (f32[16,5,128]{2,1,0:T(8,128)S(1)}, f32[16,5,128]{2,1,0:T(8,128)}, u32[]{:S(2)}) copy-start(f32[16,5,128]{2,1,0:T(8,128)} %maximum_bitcast_fusion.1) | copy-start | bytes 122884
  37.7 10.4 %copy-start.19 = (s32[1,1,3,64]{3,2,1,0:T(4,128)S(1)}, s32[1,1,3,64]{3,2,1,0:T(4,128)}, u32[]{:S(2)}) copy-start(s32[1,1,3,64]{3,2,1,0:T(4,128)} %copy.28) | copy-start | bytes 2308
  40.0 8.2 %copy-start.2 = (f32[2,8,72,136]{3,2,1,0:T(8,128)}, f32[2,8,72,136]{3,2,1,0:T(8,128)S(1)}, u32[]{:S(2)}) copy-start(f32[2,8,72,136]{3,2,1,0:T(8,128)S(1)} %fusion.95) | copy-start | bytes 1880068
  40.1 12.1 %collective-permute-start.4 = (f32[4,32,128]{2,1,0:T(8,128)S(1)}, f32[4,32,128]{2,1,0:T(8,128)S(1)}, u32[]{:S(2)}, u32[]{:S(2)}) collective-permute-start(f32[4,32,128]{2,1,0:T(8,128)S(1)} %get-tuple-element.117), channel_id=1, source_target_pairs={{0,8},{8,16},{16,24},{24,32},{32,40},{40,48},{48,56},{56,64},{64,7... | collective-permute-start | bytes 196616 | tf_op jit(solution)/shard_map/ppermute | solution.py:175
  42.1 10.2 %collective-permute-start.5 = (f32[4,32,128]{2,1,0:T(8,128)S(1)}, f32[4,32,128]{2,1,0:T(8,128)S(1)}, u32[]{:S(2)}, u32[]{:S(2)}) collective-permute-start(f32[4,32,128]{2,1,0:T(8,128)S(1)} %get-tuple-element.118), channel_id=1, source_target_pairs={{8,0},{16,8},{24,16},{32,24},{40,32},{48,40},{56,48},{64,56},{72,6... | collective-permute-start | bytes 196616 | tf_op jit(solution)/shard_map/ppermute | solution.py:176
  48.2 9.2 %copy-start.6 = (f32[1,1,2,2048]{3,2,1,0:T(2,128)S(1)}, f32[1,1,2,2048]{3,2,1,0:T(2,128)}, u32[]{:S(2)}) copy-start(f32[1,1,2,2048]{3,2,1,0:T(2,128)} %param.19) | copy-start | bytes 49156
  48.2 9.2 %copy-start.17 = (f32[2048]{0:T(1024)S(1)}, f32[2048]{0:T(1024)}, u32[]{:S(2)}) copy-start(f32[2048]{0:T(1024)} %multiply_multiply_fusion) | copy-start | bytes 24580
  48.2 9.2 %copy-start.18 = (f32[1,1,2048]{2,1,0:T(1,128)S(1)}, f32[1,1,2048]{2,1,0:T(1,128)}, u32[]{:S(2)}) copy-start(f32[1,1,2048]{2,1,0:T(1,128)} %param.22) | copy-start | bytes 24580
  63.0 6.8 %collective-permute-start.6 = (f32[3,38,128]{2,1,0:T(8,128)S(1)}, f32[3,38,128]{2,1,0:T(8,128)S(1)}, u32[]{:S(2)}, u32[]{:S(2)}) collective-permute-start(f32[3,38,128]{2,1,0:T(8,128)S(1)} %get-tuple-element.111), channel_id=1, source_target_pairs={{8,0},{16,8},{24,16},{32,24},{40,32},{48,40},{56,48},{64,56},{72,6... | collective-permute-start | bytes 175112 | tf_op jit(solution)/shard_map/ppermute | solution.py:176
  67.0 8.3 %collective-permute-start.7 = (f32[3,38,128]{2,1,0:T(8,128)S(1)}, f32[3,38,128]{2,1,0:T(8,128)S(1)}, u32[]{:S(2)}, u32[]{:S(2)}) collective-permute-start(f32[3,38,128]{2,1,0:T(8,128)S(1)} %get-tuple-element.112), channel_id=1, source_target_pairs={{0,8},{8,16},{16,24},{24,32},{32,40},{40,48},{48,56},{56,64},{64,7... | collective-permute-start | bytes 175112 | tf_op jit(solution)/shard_map/ppermute | solution.py:175
  75.4 11.8 %collective-permute-start.8 = (f32[3,38,128]{2,1,0:T(8,128)S(1)}, f32[3,38,128]{2,1,0:T(8,128)S(1)}, u32[]{:S(2)}, u32[]{:S(2)}) collective-permute-start(f32[3,38,128]{2,1,0:T(8,128)S(1)} %pad_maximum_fusion.8), channel_id=1, source_target_pairs={{1,0},{2,1},{3,2},{4,3},{5,4},{6,5},{7,6},{128,7},{129,128},{130,1... | collective-permute-start | bytes 175112 | tf_op jit(solution)/shard_map/ppermute | solution.py:176
  87.2 9.2 %collective-permute-start.9 = (f32[3,38,128]{2,1,0:T(8,128)S(1)}, f32[3,38,128]{2,1,0:T(8,128)S(1)}, u32[]{:S(2)}, u32[]{:S(2)}) collective-permute-start(f32[3,38,128]{2,1,0:T(8,128)S(1)} %pad_maximum_fusion.9), channel_id=1, source_target_pairs={{0,1},{1,2},{2,3},{3,4},{4,5},{5,6},{6,7},{7,128},{128,129},{129,1... | collective-permute-start | bytes 175112 | tf_op jit(solution)/shard_map/ppermute | solution.py:175
where the time goes:
time: 95.7 us; the launch traced here: 97.2 us
  starting transfers between devices  44.9 us (47%)
  other arithmetic  20.1 us (21%)
  waiting for transfers between devices  13 us (14%)
  local copies, waits for them, and re-layouts  9.88 us (10%)
  Pallas kernels  6.71 us (7%)
  between operations  2.16 us (2%)
    ppermute x5, starting transfers between devices, exchange(): from_next = lax.ppermute(low, axis, down)  33.4 us
    ppermute x5, starting transfers between devices, exchange(): from_previous = lax.ppermute(high, axis, up)  11.5 us
    ppermute x5, waiting for transfers between devices, exchange(): from_previous = lax.ppermute(high, axis, up)  10.7 us
    mul x4, other arithmetic, ocean_substep(): return (flow + horizontal * lap + vert + turning + surface) * wet[None]  5.52 us
    pallas_call x1, Pallas kernels, sample_surface(): pl.pallas_call(sample_kernel, out_shape=jax.ShapeDtypeStruct((window.shap...  3.52 us
    pallas_call x1, Pallas kernels, gather_records(): pl.pallas_call(gather_kernel, out_shape=jax.ShapeDtypeStruct((index.shape...  3.19 us
    ppermute x5, waiting for transfers between devices, exchange(): from_next = lax.ppermute(low, axis, down)  2.36 us
    slice x1, local copies, waits for them, and re-layouts, shards(): flow = flow[:, :, halo:halo + rows_here, halo:halo + cols_here]  2.27 us
  transfers between devices with their start and end apart: 10, of which 4 were waited for; matrix products, arithmetic and copies ran while one was open for 12% of the time, Pallas kernels for 0%

commit v1 on v0

--- a/solution.py
+++ b/solution.py
@@ -255,10 +255,18 @@
     )
     wind_ext = extended[comps * levels_here : comps * levels_here + 2]
     flow = extended[: comps * levels_here].reshape(comps, levels_here, ext_rows, ext_cols) * wet[None]
-    for substep in range(OSTEPS):
+    for substep in range(OSTEPS - 1):
         padded = jnp.pad(flow, ((0, 0), (0, 0), (1, 1), (1, 1)))
         flow = ocean_substep(flow, padded, wet, wind_ext)
-    flow = flow[:, :, halo : halo + rows_here, halo : halo + cols_here]
+    wet_tile = (jnp.arange(levels_here, dtype=jnp.int32)[:, None, None] < level_counts[None]).astype(
+        jnp.float32
+    )
+    flow = ocean_substep(
+        flow[:, :, halo : halo + rows_here, halo : halo + cols_here],
+        flow[:, :, halo - 1 : halo + rows_here + 1, halo - 1 : halo + cols_here + 1],
+        wet_tile,
+        wind_stress,
+    )
 
     table = block_table(record, ghosts)
     surface = jnp.stack([flow[0, 0], flow[1, 0], wind_stress[0], wind_stress[1]])

time: 95.7 us -> 91.1 us (0.952); the launches traced: 97.2 us -> 89.3 us
  starting transfers between devices: 44.9 us -> 32.9 us
  waiting for transfers between devices: 13 us -> 23.2 us
  local copies, waits for them, and re-layouts: 9.88 us -> 6.45 us
  other arithmetic: 20.1 us -> 17.6 us
    ppermute x5, starting transfers between devices: 33.4 us -> 17.9 us  [exchange(): from_next = lax.ppermute(low, axis, down)]
    ppermute x5, waiting for transfers between devices: 10.7 us -> 17.2 us  [exchange(): from_previous = lax.ppermute(high, axis, up)]
    ppermute x5, waiting for transfers between devices: 2.36 us -> 6.02 us  [exchange(): from_next = lax.ppermute(low, axis, down)]
    ppermute x5, starting transfers between devices: 11.5 us -> 15 us  [exchange(): from_previous = lax.ppermute(high, axis, up)]
    slice x1 -> x0, local copies, waits for them, and re-layouts: 2.27 us -> none  [shards(): flow = flow[:, :, halo:halo + rows_here, halo:halo + cols_here]]
    mul x4, other arithmetic: 5.52 us -> 4.05 us  [ocean_substep(): return (flow + horizontal * lap + vert + turning + surface) * wet[None]]
    unnamed x65 -> x39, local copies, waits for them, and re-layouts: 1.9 us -> 0.8 us
    mul x4, other arithmetic: 1.49 us -> 0.52 us  [ocean_substep(): turning = jnp.stack([CORIOLIS * flow[1], -CORIOLIS * flow[0]])]
  transfers between devices with their start and end apart: 10 -> 10, of which waited for: 4 -> 6; matrix products, arithmetic and copies ran while one was open for 12% -> 9% of each run, Pallas kernels for 0% -> 0%
where the time goes in v1:
time: 91.1 us; the launch traced here: 89.3 us
  starting transfers between devices  32.9 us (36%)
  waiting for transfers between devices  23.2 us (25%)
  other arithmetic  17.6 us (19%)
  Pallas kernels  6.7 us (7%)
  local copies, waits for them, and re-layouts  6.45 us (7%)
  between operations  2.02 us (2%)
    ppermute x5, starting transfers between devices, exchange(): from_next = lax.ppermute(low, axis, down)  17.9 us
    ppermute x5, waiting for transfers between devices, exchange(): from_previous = lax.ppermute(high, axis, up)  17.2 us
    ppermute x5, starting transfers between devices, exchange(): from_previous = lax.ppermute(high, axis, up)  15 us
    ppermute x5, waiting for transfers between devices, exchange(): from_next = lax.ppermute(low, axis, down)  6.02 us
    mul x4, other arithmetic, ocean_substep(): return (flow + horizontal * lap + vert + turning + surface) * wet[None]  4.05 us
    pallas_call x1, Pallas kernels, sample_surface(): pl.pallas_call(sample_kernel, out_shape=jax.ShapeDtypeStruct((window.shap...  3.52 us
    pallas_call x1, Pallas kernels, gather_records(): pl.pallas_call(gather_kernel, out_shape=jax.ShapeDtypeStruct((index.shape...  3.18 us
  transfers between devices with their start and end apart: 10, of which 6 were waited for; matrix products, arithmetic and copies ran while one was open for 9% of the time, Pallas kernels for 0%

profile of v1, /device:TPU:24, one launch (start us, length us, event | category | flops | bytes accessed | tf_op | source)
XLA Modules:
  0.0 89.3 jit_solution(7087159166925129039)
XLA Ops:
  0.7 0.8 pad_maximum_fusion.17
  1.5 0.8 convert_bitcast_fusion
  2.3 1.0 %pad_maximum_fusion.15 = (f32[19,4,128]{2,1,0:T(4,128)S(1)}, f32[19,4,128]{2,1,0:T(4,128)S(1)}) fusion(f32[1,64,128]{2,1,0:T(8,128)S(1)} %convert_bitcast_fusion, f32[2,64,128]{2,1,0:T(8,128)} %param.17, f32[16,64,128]{2,1,0:T(8,128)} %bitcast.169), kind=kLoop, calls=%fused_computation.215 | loop fusion | flops 38912 | bytes 700416 | tf_op jit(solution)/shard_map/slice | solution.py:220
  3.3 7.9 %collective-permute-start.1 = (f32[12288]{0:T(1024)S(1)}, f32[12288]{0:T(1024)S(1)}, u32[]{:S(2)}, u32[]{:S(2)}) collective-permute-start(f32[12288]{0:T(1024)S(1)} %get-tuple-element.134), channel_id=1, source_target_pairs={{8,0},{16,8},{24,16},{32,24},{40,32},{48,40},{56,48},{64,56},{72,6... | collective-permute-start | bytes 147464 | tf_op jit(solution)/shard_map/ppermute | solution.py:176
  11.3 1.9 %collective-permute-start = (f32[12288]{0:T(1024)S(1)}, f32[12288]{0:T(1024)S(1)}, u32[]{:S(2)}, u32[]{:S(2)}) collective-permute-start(f32[12288]{0:T(1024)S(1)} %get-tuple-element.133), channel_id=1, source_target_pairs={{0,8},{8,16},{16,24},{24,32},{32,40},{40,48},{48,56},{56,64},{64,7... | collective-permute-start | bytes 147464 | tf_op jit(solution)/shard_map/ppermute | solution.py:175
  13.2 0.8 multiply_bitcast_fusion
  14.1 0.6 and_select_fusion
  14.7 0.6 fusion.104.rows_ref
  15.4 0.7 bitcast_select_fusion.index_ref
  16.1 3.2 %collective-permute-done = f32[12288]{0:T(1024)S(1)} collective-permute-done((f32[12288]{0:T(1024)S(1)}, f32[12288]{0:T(1024)S(1)}, u32[]{:S(2)}, u32[]{:S(2)}) %collective-permute-start) | collective-permute-done | bytes 49184 | tf_op jit(solution)/shard_map/ppermute | solution.py:175
  19.5 0.1 pad_maximum_fusion.1
  19.6 0.2 fusion.112
  19.8 0.4 reshape.558
  20.2 0.4 reshape.561
  20.5 0.1 pad_maximum_fusion.11
  20.6 3.0 %collective-permute-start.3 = (f32[13152]{0:T(1024)S(1)}, f32[13152]{0:T(1024)S(1)}, u32[]{:S(2)}, u32[]{:S(2)}) collective-permute-start(f32[13152]{0:T(1024)S(1)} %get-tuple-element.132), channel_id=1, source_target_pairs={{1,0},{2,1},{3,2},{4,3},{5,4},{6,5},{7,6},{128,7},{129,128},{130,1... | collective-permute-start | bytes 157832 | tf_op jit(solution)/shard_map/ppermute | solution.py:176
  23.7 1.9 %collective-permute-start.2 = (f32[13152]{0:T(1024)S(1)}, f32[13152]{0:T(1024)S(1)}, u32[]{:S(2)}, u32[]{:S(2)}) collective-permute-start(f32[13152]{0:T(1024)S(1)} %get-tuple-element.131), channel_id=1, source_target_pairs={{0,1},{1,2},{2,3},{3,4},{4,5},{5,6},{6,7},{7,128},{128,129},{129,1... | collective-permute-start | bytes 157832 | tf_op jit(solution)/shard_map/ppermute | solution.py:175
  26.3 0.7 reshape.562
  27.0 5.7 %collective-permute-done.2 = f32[13152]{0:T(1024)S(1)} collective-permute-done((f32[13152]{0:T(1024)S(1)}, f32[13152]{0:T(1024)S(1)}, u32[]{:S(2)}, u32[]{:S(2)}) %collective-permute-start.2) | collective-permute-done | bytes 52640 | tf_op jit(solution)/shard_map/ppermute | solution.py:175
  32.7 0.7 reshape.560
  33.5 0.1 fusion.100
  33.6 0.7 pad_maximum_fusion
  34.3 0.1 maximum_bitcast_fusion
  34.4 0.1 slice.591
  34.6 0.1 broadcast_multiply_fusion
  34.7 0.1 slice_multiply_fusion.5
  34.9 0.2 fusion.89
  35.0 1.1 %fusion.84 = f32[2,8,72,136]{3,2,1,0:T(8,128)S(1)} fusion(f32[2,1,72,136]{3,2,1,0:T(8,128)S(1)} %fusion.100, f32[1,8,72,136]{3,2,1,0:T(8,128)S(1)} %get-tuple-element.102, f32[1,8,72,136]{3,2,1,0:T(8,128)S(1)} %get-tuple-element.101, f32[2,7,72,136]{3,2,1,0:T(8,128)S(1)} %fusion.89, f32[2,8,72,136]{3,2,1,0:T(8,128)S(1)} %broadcast_multiply_fusion, ...), kind=kLoop, calls=%fused_computation.160 | loop fusion | flops 2036736 | bytes 2820128 | tf_op jit(solution)/shard_map/mul | solution.py:55
  36.1 0.1 slice_multiply_fusion.3
  36.2 0.2 fusion.88
  36.4 1.1 %fusion.85 = f32[2,8,72,136]{3,2,1,0:T(8,128)S(1)} fusion(f32[2,1,72,136]{3,2,1,0:T(8,128)S(1)} %fusion.100, f32[1,8,72,136]{3,2,1,0:T(8,128)S(1)} %get-tuple-element.100, f32[1,8,72,136]{3,2,1,0:T(8,128)S(1)} %get-tuple-element.99, f32[2,7,72,136]{3,2,1,0:T(8,128)S(1)} %fusion.88, f32[2,8,72,136]{3,2,1,0:T(8,128)S(1)} %fusion.84, ...), kind=kLoop, calls=%fused_computation.161 | loop fusion | flops 2036736 | bytes 2820128 | tf_op jit(solution)/shard_map/mul | solution.py:55
  37.5 0.1 slice_multiply_fusion.1
  37.6 0.2 fusion.87
  37.8 1.1 %fusion.86 = f32[2,8,72,136]{3,2,1,0:T(8,128)S(1)} fusion(f32[2,1,72,136]{3,2,1,0:T(8,128)S(1)} %fusion.100, f32[1,8,72,136]{3,2,1,0:T(8,128)S(1)} %get-tuple-element.98, f32[1,8,72,136]{3,2,1,0:T(8,128)S(1)} %get-tuple-element.97, f32[2,7,72,136]{3,2,1,0:T(8,128)S(1)} %fusion.87, f32[2,8,72,136]{3,2,1,0:T(8,128)S(1)} %fusion.85, ...), kind=kLoop, calls=%fused_computation.162 | loop fusion | flops 2036736 | bytes 2820128 | tf_op jit(solution)/shard_map/mul | solution.py:55
  38.9 0.2 slice_multiply_fusion.8
  39.1 0.3 fusion.98
  39.4 0.8 fusion.97
  40.2 3.1 %collective-permute-start.5 = (f32[4,32,128]{2,1,0:T(8,128)S(1)}, f32[4,32,128]{2,1,0:T(8,128)S(1)}, u32[]{:S(2)}, u32[]{:S(2)}) collective-permute-start(f32[4,32,128]{2,1,0:T(8,128)S(1)} %get-tuple-element.118), channel_id=1, source_target_pairs={{8,0},{16,8},{24,16},{32,24},{40,32},{48,40},{56,48},{64,56},{72,6... | collective-permute-start | bytes 196616 | tf_op jit(solution)/shard_map/ppermute | solution.py:176
  43.3 2.8 %collective-permute-start.4 = (f32[4,32,128]{2,1,0:T(8,128)S(1)}, f32[4,32,128]{2,1,0:T(8,128)S(1)}, u32[]{:S(2)}, u32[]{:S(2)}) collective-permute-start(f32[4,32,128]{2,1,0:T(8,128)S(1)} %get-tuple-element.117), channel_id=1, source_target_pairs={{0,8},{8,16},{16,24},{24,32},{32,40},{40,48},{48,56},{56,64},{64,7... | collective-permute-start | bytes 196616 | tf_op jit(solution)/shard_map/ppermute | solution.py:175
  46.1 0.1 fusion.120
  46.2 0.1 fusion.119
  46.5 4.1 %conditional.1 = (f32[16,2,128]{2,0,1:T(8,128)S(1)}) conditional(s32[]{:T(128)} %clamp.3, (s32[3,64]{1,0:T(4,128)S(1)}, s32[]{:T(128)}, f32[48,5,128]{2,1,0:T(8,128)S(1)}) %tuple.82, (s32[3,64]{1,0:T(4,128)S(1)}, s32[]{:T(128)}, f32[48,5,128]{2,1,0:T(8,128)S(1)}) %tuple.83, (s32[3,64]{1,0:T(4,128)S(1)}, s32[]{:T(128)}, ...), branch_computations={%region_0.3_spmd, %region_3.6_spmd, %region_6.9_spmd} | conditional | flops 31477696 | bytes 1797260 | solution.py:295
  46.6 0.6 gather_fusion.1
  47.2 0.6 gather_fusion
  47.8 1.8 %multiply_reduce_fusion.1 = (f32[16,128]{1,0:T(8,128)S(1)}, f32[16,128]{1,0:T(8,128)S(1)}) fusion(f32[16,128]{1,0:T(8,128)S(1)} %bitcast.221, f32[16,128]{1,0:T(8,128)S(1)} %bitcast.226, f32[16,128]{1,0:T(8,128)S(1)} %bitcast.222, f32[16,128]{1,0:T(8,128)S(1)} %bitcast.227, f32[16,128]{1,0:T(8,128)S(1)} %bitcast.219, f32[16,128]{1,0:T(8,128)S(1)} %bitcast.224, ...), kind=kLoop, calls=%fused_computation.19 | loop fusion | flops 7073792 | bytes 98304 | tf_op jit(solution)/shard_map/cond/branch_0_fun/reduce_sum | solution.py:73
  49.6 0.7 iota_compare_fusion.1
  50.2 0.2 fusion.5
  50.6 1.0 %collective-permute-done.4 = f32[4,32,128]{2,1,0:T(8,128)S(1)} collective-permute-done((f32[4,32,128]{2,1,0:T(8,128)S(1)}, f32[4,32,128]{2,1,0:T(8,128)S(1)}, u32[]{:S(2)}, u32[]{:S(2)}) %collective-permute-start.4) | collective-permute-done | bytes 65568 | tf_op jit(solution)/shard_map/ppermute | solution.py:175
  51.6 0.7 pad_maximum_fusion.2.window_ref
  52.3 3.5 %shard_map.148 = f32[4,2048]{1,0:T(4,128)} custom-call(f32[4,128,128]{2,1,0:T(8,128)} %pad_maximum_fusion.2.window_ref, s32[1,2048]{1,0:T(1,128)} %fusion.104.rows_ref, s32[1,2048]{1,0:T(1,128)} %get-tuple-element.51.cols_ref), custom_call_target="tpu_custom_call" | custom-call | tf_op jit(solution)/shard_map/pallas_call | solution.py:133
  55.8 0.8 multiply_reduce_fusion.6
  56.6 0.9 multiply_add_fusion
  57.5 0.6 pad_maximum_fusion.16
  58.2 3.2 %shard_map.149 = f32[8,38,128]{2,1,0:T(8,128)} custom-call(f32[4,2048]{1,0:T(4,128)} %get-tuple-element.129.state_ref, f32[1,2048]{1,0:T(1,128)} %bitcast.189, f32[1,2048]{1,0:T(1,128)} %bitcast.202, f32[32,2048]{1,0:T(8,128)} %bitcast.181, s32[8,128]{1,0:T(8,128)} %bitcast_select_fusion.index_ref), custom_call_target="tpu_custom_call" | custom-call | tf_op jit(solution)/shard_map/pallas_call | solution.py:161
  61.4 0.9 fusion.114
  62.2 6.5 %collective-permute-start.7 = (f32[3,38,128]{2,1,0:T(8,128)S(1)}, f32[3,38,128]{2,1,0:T(8,128)S(1)}, u32[]{:S(2)}, u32[]{:S(2)}) collective-permute-start(f32[3,38,128]{2,1,0:T(8,128)S(1)} %get-tuple-element.112), channel_id=1, source_target_pairs={{0,8},{8,16},{16,24},{24,32},{32,40},{40,48},{48,56},{56,64},{64,7... | collective-permute-start | bytes 175112 | tf_op jit(solution)/shard_map/ppermute | solution.py:175
  68.7 0.8 fusion.113
  69.5 1.9 %collective-permute-start.6 = (f32[3,38,128]{2,1,0:T(8,128)S(1)}, f32[3,38,128]{2,1,0:T(8,128)S(1)}, u32[]{:S(2)}, u32[]{:S(2)}) collective-permute-start(f32[3,38,128]{2,1,0:T(8,128)S(1)} %get-tuple-element.111), channel_id=1, source_target_pairs={{8,0},{16,8},{24,16},{32,24},{40,32},{48,40},{56,48},{64,56},{72,6... | collective-permute-start | bytes 175112 | tf_op jit(solution)/shard_map/ppermute | solution.py:176
  71.4 4.2 %collective-permute-done.6 = f32[3,38,128]{2,1,0:T(8,128)S(1)} collective-permute-done((f32[3,38,128]{2,1,0:T(8,128)S(1)}, f32[3,38,128]{2,1,0:T(8,128)S(1)}, u32[]{:S(2)}, u32[]{:S(2)}) %collective-permute-start.6) | collective-permute-done | bytes 58400 | tf_op jit(solution)/shard_map/ppermute | solution.py:176
  75.6 1.9 %collective-permute-start.8 = (f32[3,38,128]{2,1,0:T(8,128)S(1)}, f32[3,38,128]{2,1,0:T(8,128)S(1)}, u32[]{:S(2)}, u32[]{:S(2)}) collective-permute-start(f32[3,38,128]{2,1,0:T(8,128)S(1)} %pad_maximum_fusion.8), channel_id=1, source_target_pairs={{1,0},{2,1},{3,2},{4,3},{5,4},{6,5},{7,6},{128,7},{129,128},{130,1... | collective-permute-start | bytes 175112 | tf_op jit(solution)/shard_map/ppermute | solution.py:176
  77.5 1.8 %collective-permute-done.8 = f32[3,38,128]{2,1,0:T(8,128)S(1)} collective-permute-done((f32[3,38,128]{2,1,0:T(8,128)S(1)}, f32[3,38,128]{2,1,0:T(8,128)S(1)}, u32[]{:S(2)}, u32[]{:S(2)}) %collective-permute-start.8) | collective-permute-done | bytes 58400 | tf_op jit(solution)/shard_map/ppermute | solution.py:176
  79.4 1.9 %collective-permute-start.9 = (f32[3,38,128]{2,1,0:T(8,128)S(1)}, f32[3,38,128]{2,1,0:T(8,128)S(1)}, u32[]{:S(2)}, u32[]{:S(2)}) collective-permute-start(f32[3,38,128]{2,1,0:T(8,128)S(1)} %pad_maximum_fusion.9), channel_id=1, source_target_pairs={{0,1},{1,2},{2,3},{3,4},{4,5},{5,6},{6,7},{7,128},{128,129},{129,1... | collective-permute-start | bytes 175112 | tf_op jit(solution)/shard_map/ppermute | solution.py:175
  81.3 7.3 %collective-permute-done.9 = f32[3,38,128]{2,1,0:T(8,128)S(1)} collective-permute-done((f32[3,38,128]{2,1,0:T(8,128)S(1)}, f32[3,38,128]{2,1,0:T(8,128)S(1)}, u32[]{:S(2)}, u32[]{:S(2)}) %collective-permute-start.9) | collective-permute-done | bytes 58400 | tf_op jit(solution)/shard_map/ppermute | solution.py:175
  88.7 0.7 copy.18
  (91 shorter events, 0.7 us)
Async XLA Ops:
  0.6 14.1 %copy-start.6 = (f32[1,1,2048]{2,1,0:T(1,128)S(1)}, f32[1,1,2048]{2,1,0:T(1,128)}, u32[]{:S(2)}) copy-start(f32[1,1,2048]{2,1,0:T(1,128)} %param.21) | copy-start | bytes 24580
  0.6 15.4 %copy-start.3 = (f32[1,1,2,2048]{3,2,1,0:T(2,128)S(1)}, f32[1,1,2,2048]{3,2,1,0:T(2,128)}, u32[]{:S(2)}) copy-start(f32[1,1,2,2048]{3,2,1,0:T(2,128)} %param.20) | copy-start | bytes 49156
  0.7 15.4 %copy-start.4 = (f32[1,1,2,2048]{3,2,1,0:T(2,128)S(1)}, f32[1,1,2,2048]{3,2,1,0:T(2,128)}, u32[]{:S(2)}) copy-start(f32[1,1,2,2048]{3,2,1,0:T(2,128)} %param.19) | copy-start | bytes 49156
  0.7 13.4 %copy-start.5 = (s32[64,128]{1,0:T(8,128)S(1)}, s32[64,128]{1,0:T(8,128)}, u32[]{:S(2)}) copy-start(s32[64,128]{1,0:T(8,128)} %param.18) | copy-start | bytes 98308
  0.7 13.4 %copy-start.7 = (s32[1,1,2048]{2,1,0:T(1,128)S(1)}, s32[1,1,2048]{2,1,0:T(1,128)}, u32[]{:S(2)}) copy-start(s32[1,1,2048]{2,1,0:T(1,128)} %param.24) | copy-start | bytes 24580
  0.7 14.7 %copy-start.9 = (s32[1,1,8,128]{3,2,1,0:T(8,128)S(1)}, s32[1,1,8,128]{3,2,1,0:T(8,128)}, u32[]{:S(2)}) copy-start(s32[1,1,8,128]{3,2,1,0:T(8,128)} %param.27) | copy-start | bytes 12292
  0.7 14.7 %copy-start.11 = (s32[1,1,8]{2,1,0:T(1,128)S(1)}, s32[1,1,8]{2,1,0:T(1,128)}, u32[]{:S(2)}) copy-start(s32[1,1,8]{2,1,0:T(1,128)} %param.28) | copy-start | bytes 100
  2.3 17.2 %copy-start = (f32[2,8,64,128]{3,2,1,0:T(8,128)S(1)}, f32[2,8,64,128]{3,2,1,0:T(8,128)}, u32[]{:S(2)}) copy-start(f32[2,8,64,128]{3,2,1,0:T(8,128)} %param.16) | copy-start | bytes 1572868
  2.3 17.2 %copy-start.1 = (f32[2,64,128]{2,1,0:T(8,128)S(1)}, f32[2,64,128]{2,1,0:T(8,128)}, u32[]{:S(2)}) copy-start(f32[2,64,128]{2,1,0:T(8,128)} %param.17) | copy-start | bytes 196612
  3.3 12.8 %collective-permute-start.1 = (f32[12288]{0:T(1024)S(1)}, f32[12288]{0:T(1024)S(1)}, u32[]{:S(2)}, u32[]{:S(2)}) collective-permute-start(f32[12288]{0:T(1024)S(1)} %get-tuple-element.134), channel_id=1, source_target_pairs={{8,0},{16,8},{24,16},{32,24},{40,32},{48,40},{56,48},{64,56},{72,6... | collective-permute-start | bytes 147464 | tf_op jit(solution)/shard_map/ppermute | solution.py:176
  11.3 8.1 %collective-permute-start = (f32[12288]{0:T(1024)S(1)}, f32[12288]{0:T(1024)S(1)}, u32[]{:S(2)}, u32[]{:S(2)}) collective-permute-start(f32[12288]{0:T(1024)S(1)} %get-tuple-element.133), channel_id=1, source_target_pairs={{0,8},{8,16},{16,24},{24,32},{32,40},{40,48},{48,56},{56,64},{64,7... | collective-permute-start | bytes 147464 | tf_op jit(solution)/shard_map/ppermute | solution.py:175
  19.8 6.5 %copy-start.10 = (s32[1,1,3,64]{3,1,2,0:T(1,128)S(1)}, s32[1,1,3,64]{3,1,2,0:T(1,128)}, u32[]{:S(2)}) copy-start(s32[1,1,3,64]{3,1,2,0:T(1,128)} %param.26) | copy-start | bytes 2308
  20.6 5.7 %collective-permute-start.3 = (f32[13152]{0:T(1024)S(1)}, f32[13152]{0:T(1024)S(1)}, u32[]{:S(2)}, u32[]{:S(2)}) collective-permute-start(f32[13152]{0:T(1024)S(1)} %get-tuple-element.132), channel_id=1, source_target_pairs={{1,0},{2,1},{3,2},{4,3},{5,4},{6,5},{7,6},{128,7},{129,128},{130,1... | collective-permute-start | bytes 157832 | tf_op jit(solution)/shard_map/ppermute | solution.py:176
  23.7 9.1 %collective-permute-start.2 = (f32[13152]{0:T(1024)S(1)}, f32[13152]{0:T(1024)S(1)}, u32[]{:S(2)}, u32[]{:S(2)}) collective-permute-start(f32[13152]{0:T(1024)S(1)} %get-tuple-element.131), channel_id=1, source_target_pairs={{0,1},{1,2},{2,3},{3,4},{4,5},{5,6},{6,7},{7,128},{128,129},{129,1... | collective-permute-start | bytes 157832 | tf_op jit(solution)/shard_map/ppermute | solution.py:175
  40.2 6.4 %copy-start.2 = (f32[2,8,64,128]{3,2,1,0:T(8,128)}, f32[2,8,64,128]{3,2,1,0:T(8,128)S(1)}, u32[]{:S(2)}) copy-start(f32[2,8,64,128]{3,2,1,0:T(8,128)S(1)} %fusion.97) | copy-start | bytes 1572868
  40.2 10.4 %collective-permute-start.5 = (f32[4,32,128]{2,1,0:T(8,128)S(1)}, f32[4,32,128]{2,1,0:T(8,128)S(1)}, u32[]{:S(2)}, u32[]{:S(2)}) collective-permute-start(f32[4,32,128]{2,1,0:T(8,128)S(1)} %get-tuple-element.118), channel_id=1, source_target_pairs={{8,0},{16,8},{24,16},{32,24},{40,32},{48,40},{56,48},{64,56},{72,6... | collective-permute-start | bytes 196616 | tf_op jit(solution)/shard_map/ppermute | solution.py:176
  43.3 8.3 %collective-permute-start.4 = (f32[4,32,128]{2,1,0:T(8,128)S(1)}, f32[4,32,128]{2,1,0:T(8,128)S(1)}, u32[]{:S(2)}, u32[]{:S(2)}) collective-permute-start(f32[4,32,128]{2,1,0:T(8,128)S(1)} %get-tuple-element.117), channel_id=1, source_target_pairs={{0,8},{8,16},{16,24},{24,32},{32,40},{40,48},{48,56},{56,64},{64,7... | collective-permute-start | bytes 196616 | tf_op jit(solution)/shard_map/ppermute | solution.py:175
  46.5 10.1 %copy-start.8 = (f32[1,1,2048]{2,1,0:T(1,128)S(1)}, f32[1,1,2048]{2,1,0:T(1,128)}, u32[]{:S(2)}) copy-start(f32[1,1,2048]{2,1,0:T(1,128)} %param.22) | copy-start | bytes 24580
  62.2 9.2 %collective-permute-start.7 = (f32[3,38,128]{2,1,0:T(8,128)S(1)}, f32[3,38,128]{2,1,0:T(8,128)S(1)}, u32[]{:S(2)}, u32[]{:S(2)}) collective-permute-start(f32[3,38,128]{2,1,0:T(8,128)S(1)} %get-tuple-element.112), channel_id=1, source_target_pairs={{0,8},{8,16},{16,24},{24,32},{32,40},{40,48},{48,56},{56,64},{64,7... | collective-permute-start | bytes 175112 | tf_op jit(solution)/shard_map/ppermute | solution.py:175
  69.5 6.1 %collective-permute-start.6 = (f32[3,38,128]{2,1,0:T(8,128)S(1)}, f32[3,38,128]{2,1,0:T(8,128)S(1)}, u32[]{:S(2)}, u32[]{:S(2)}) collective-permute-start(f32[3,38,128]{2,1,0:T(8,128)S(1)} %get-tuple-element.111), channel_id=1, source_target_pairs={{8,0},{16,8},{24,16},{32,24},{40,32},{48,40},{56,48},{64,56},{72,6... | collective-permute-start | bytes 175112 | tf_op jit(solution)/shard_map/ppermute | solution.py:176
  75.6 3.8 %collective-permute-start.8 = (f32[3,38,128]{2,1,0:T(8,128)S(1)}, f32[3,38,128]{2,1,0:T(8,128)S(1)}, u32[]{:S(2)}, u32[]{:S(2)}) collective-permute-start(f32[3,38,128]{2,1,0:T(8,128)S(1)} %pad_maximum_fusion.8), channel_id=1, source_target_pairs={{1,0},{2,1},{3,2},{4,3},{5,4},{6,5},{7,6},{128,7},{129,128},{130,1... | collective-permute-start | bytes 175112 | tf_op jit(solution)/shard_map/ppermute | solution.py:176
  79.4 9.2 %collective-permute-start.9 = (f32[3,38,128]{2,1,0:T(8,128)S(1)}, f32[3,38,128]{2,1,0:T(8,128)S(1)}, u32[]{:S(2)}, u32[]{:S(2)}) collective-permute-start(f32[3,38,128]{2,1,0:T(8,128)S(1)} %pad_maximum_fusion.9), channel_id=1, source_target_pairs={{0,1},{1,2},{2,3},{3,4},{4,5},{5,6},{6,7},{7,128},{128,129},{129,1... | collective-permute-start | bytes 175112 | tf_op jit(solution)/shard_map/ppermute | solution.py:175

commit v2 on v1

--- a/solution.py
+++ b/solution.py
@@ -166,6 +166,34 @@
             pltpu.VMEM((3 * padded, state.shape[1]), jnp.float32),
         ],
     )(state, radius, mass, polygon, index)
+
+
+def state_kernel(state_ref, index_ref, static_ref, out_ref, record_ref, stack_ref):
+    floes = state_ref.shape[1]
+    slots = index_ref.shape[1]
+    rows = state_ref.shape[0]
+    record_ref[...] = jnp.zeros_like(record_ref)
+    stack_ref[...] = jnp.zeros_like(stack_ref)
+    record_ref[0:rows, :] = state_ref[...]
+    record = record_ref[...]
+    out_ref[...] = static_ref[...]
+    for way in range(index_ref.shape[0]):
+        onehot = (
+            lax.broadcasted_iota(jnp.int32, (floes, slots), 0) == index_ref[way : way + 1, :]
+        ).astype(jnp.bfloat16)
+        out_ref[way, 0:rows, :] = stacked_select(stack_ref, record, onehot)[0:rows]
+
+
+def gather_state(state, index, static):
+    padded = -(-state.shape[0] // 8) * 8
+    return pl.pallas_call(
+        state_kernel,
+        out_shape=jax.ShapeDtypeStruct(static.shape, jnp.float32),
+        scratch_shapes=[
+            pltpu.VMEM((padded, state.shape[1]), jnp.float32),
+            pltpu.VMEM((3 * padded, state.shape[1]), jnp.float32),
+        ],
+    )(state, index, static)
 
 
 def exchange(low, high, axis):
@@ -216,9 +244,23 @@
     )
     channels = fields.shape[0]
     row_strip = channels * halo * cols_here
-    low = jnp.concatenate([fields[:, :halo].reshape(-1), edge.reshape(-1)])
-    high = jnp.concatenate([fields[:, -halo:].reshape(-1), edge.reshape(-1)])
+    margin = rows_here // 2
+    low = jnp.concatenate(
+        [fields[:, :halo].reshape(-1), edge.reshape(-1), wind_stress[:, :margin].reshape(-1)]
+    )
+    high = jnp.concatenate(
+        [fields[:, -halo:].reshape(-1), edge.reshape(-1), wind_stress[:, -margin:].reshape(-1)]
+    )
     above, below = exchange(low, high, "gx")
+    wind_strip = (2, margin, cols_here)
+    wind_window = jnp.concatenate(
+        [
+            above[row_strip + edge_size :].reshape(wind_strip),
+            wind_stress,
+            below[row_strip + edge_size :].reshape(wind_strip),
+        ],
+        axis=1,
+    )
     extended = jnp.concatenate(
         [
             above[:row_strip].reshape(channels, halo, cols_here),
@@ -228,7 +270,11 @@
         axis=1,
     )
     ghost_column = jnp.stack(
-        [above[row_strip:].reshape(edge.shape), edge, below[row_strip:].reshape(edge.shape)]
+        [
+            above[row_strip : row_strip + edge_size].reshape(edge.shape),
+            edge,
+            below[row_strip : row_strip + edge_size].reshape(edge.shape),
+        ]
     )
     ext_rows = rows_here + 2 * halo
     col_strip = channels * ext_rows * halo
@@ -255,6 +301,18 @@
     )
     wind_ext = extended[comps * levels_here : comps * levels_here + 2]
     flow = extended[: comps * levels_here].reshape(comps, levels_here, ext_rows, ext_cols) * wet[None]
+    first_row = lax.axis_index("gx") * rows_here - margin
+    floe_rows = (cells // cols_here - first_row)[None]
+    floe_cols = (cells % cols_here)[None]
+    sampled_wind = sample_surface(wind_window, floe_rows, floe_cols)
+    leaving = move_index[0, 0]
+    capacity = leaving.shape[1]
+    valid_slots = jnp.arange(capacity, dtype=jnp.int32)[None, :] < move_count[0, 0][:, None]
+    chosen = jnp.where(valid_slots, leaving, -1)
+    fixed_records = gather_records(
+        jnp.zeros((4, floes), jnp.float32), radius[None], mass[None], floe_polygon[0, 0], chosen
+    )
+    flow, sampled_wind, fixed_records = lax.optimization_barrier((flow, sampled_wind, fixed_records))
     for substep in range(OSTEPS - 1):
         padded = jnp.pad(flow, ((0, 0), (0, 0), (1, 1), (1, 1)))
         flow = ocean_substep(flow, padded, wet, wind_ext)
@@ -269,16 +327,10 @@
     )
 
     table = block_table(record, ghosts)
-    surface = jnp.stack([flow[0, 0], flow[1, 0], wind_stress[0], wind_stress[1]])
-    margin = rows_here // 2
+    surface = jnp.stack([flow[0, 0], flow[1, 0]])
     from_above, from_below = exchange(surface[:, :margin], surface[:, -margin:], "gx")
     near = jnp.concatenate([from_above, surface, from_below], axis=1)
-    first_row = lax.axis_index("gx") * rows_here - margin
-    sampled = sample_surface(
-        near,
-        (cells // cols_here - first_row)[None],
-        (cells % cols_here)[None],
-    )
+    sampled_flow = sample_surface(near, floe_rows, floe_cols)
     lists = contact_list[0, 0]
     count = contact_count[0, 0]
     slots = lists.shape[1]
@@ -295,18 +347,13 @@
     contact = lax.switch(which, [pass_over(size) for size in sizes], lists, count)
     contact = contact.transpose(1, 0, 2).reshape(2, floes)
     area = math.pi * radius * radius
-    relative = sampled[0:2] - velocity
+    relative = sampled_flow - velocity
     speed = jnp.sqrt(jnp.sum(relative * relative, axis=0, keepdims=True))
-    total = contact + area[None] * (WATER_DRAG * speed * relative + AIR_GAIN * sampled[2:4])
+    total = contact + area[None] * (WATER_DRAG * speed * relative + AIR_GAIN * sampled_wind)
     new_velocity = velocity + ICE_STEP * total / mass[None]
     new_position = position + ICE_STEP * new_velocity
     floe_next = jnp.concatenate([new_position, new_velocity], axis=0)
-    leaving = move_index[0, 0]
-    capacity = leaving.shape[1]
-    valid_slots = jnp.arange(capacity, dtype=jnp.int32)[None, :] < move_count[0, 0][:, None]
-    outgoing = gather_records(
-        floe_next, radius[None], mass[None], floe_polygon[0, 0], jnp.where(valid_slots, leaving, -1)
-    )
+    outgoing = gather_state(floe_next, chosen, fixed_records)
     from_above, from_below = exchange(outgoing[0:3], outgoing[5:8], "gx")
     heading_left = jnp.stack([from_below[0], outgoing[3], from_above[0]])
     heading_right = jnp.stack([from_below[2], outgoing[4], from_above[2]])

time: 91.1 us -> 92.9 us (1.020); the launches traced: 89.3 us -> 94.5 us
  waiting for transfers between devices: 23.2 us -> 14 us
  other arithmetic: 17.6 us -> 22.5 us
  Pallas kernels: 6.7 us -> 10.9 us
  starting transfers between devices: 32.9 us -> 36.4 us
  local copies, waits for them, and re-layouts: 6.45 us -> 8.17 us
    ppermute x5, starting transfers between devices: 17.9 us -> 26.8 us  [exchange(): from_next = lax.ppermute(low, axis, down)]
    ppermute x5, waiting for transfers between devices: 17.2 us -> 10.3 us  [exchange(): from_previous = lax.ppermute(high, axis, up)]
    ppermute x5, starting transfers between devices: 15 us -> 9.6 us  [exchange(): from_previous = lax.ppermute(high, axis, up)]
    reduce_sum x1, other arithmetic: 1.77 us -> 7.06 us  [pair_forces(): jnp.sum(magnitude * normal_x, axis=1)]
    pallas_call x0 -> x1, Pallas kernels: none -> 2.39 us  [gather_state(): pl.pallas_call(state_kernel, out_shape=jax.ShapeDtypeStruct(static.shape,...]
    ppermute x5, waiting for transfers between devices: 6.02 us -> 3.68 us  [exchange(): from_next = lax.ppermute(low, axis, down)]
    pallas_call x1 -> x2, Pallas kernels: 3.52 us -> 5.33 us  [sample_surface(): pl.pallas_call(sample_kernel, out_shape=jax.ShapeDtypeStruct((window.shap...]
  transfers between devices with their start and end apart: 10 -> 10, of which waited for: 6 -> 4; matrix products, arithmetic and copies ran while one was open for 9% -> 15% of each run, Pallas kernels for 0% -> 6%
where the time goes in v2:
time: 92.9 us; the launch traced here: 94.5 us
  starting transfers between devices  36.4 us (39%)
  other arithmetic  22.5 us (24%)
  waiting for transfers between devices  14 us (15%)
  Pallas kernels  10.9 us (12%)
  local copies, waits for them, and re-layouts  8.17 us (9%)
  between operations  2.09 us (2%)
    ppermute x5, starting transfers between devices, exchange(): from_next = lax.ppermute(low, axis, down)  26.8 us
    ppermute x5, waiting for transfers between devices, exchange(): from_previous = lax.ppermute(high, axis, up)  10.3 us
    ppermute x5, starting transfers between devices, exchange(): from_previous = lax.ppermute(high, axis, up)  9.6 us
    reduce_sum x1, other arithmetic, pair_forces(): jnp.sum(magnitude * normal_x, axis=1)  7.06 us
    pallas_call x2, Pallas kernels, sample_surface(): pl.pallas_call(sample_kernel, out_shape=jax.ShapeDtypeStruct((window.shap...  5.33 us
    mul x4, other arithmetic, ocean_substep(): return (flow + horizontal * lap + vert + turning + surface) * wet[None]  4.05 us
    ppermute x5, waiting for transfers between devices, exchange(): from_next = lax.ppermute(low, axis, down)  3.68 us
    pallas_call x1, Pallas kernels, gather_records(): pl.pallas_call(gather_kernel, out_shape=jax.ShapeDtypeStruct((index.shape...  3.18 us
  transfers between devices with their start and end apart: 10, of which 4 were waited for; matrix products, arithmetic and copies ran while one was open for 15% of the time, Pallas kernels for 6%

profile of v2, /device:TPU:24, one launch (start us, length us, event | category | flops | bytes accessed | tf_op | source)
XLA Modules:
  0.0 94.5 jit_solution(11269483662942169025)
XLA Ops:
  0.7 0.8 pad_maximum_fusion.18
  1.5 0.8 fusion.116
  2.3 0.8 convert_bitcast_fusion
  3.1 0.9 pad_maximum_fusion.15
  4.1 8.1 %collective-permute-start.1 = (f32[20480]{0:T(1024)S(1)}, f32[20480]{0:T(1024)S(1)}, u32[]{:S(2)}, u32[]{:S(2)}) collective-permute-start(f32[20480]{0:T(1024)S(1)} %get-tuple-element.142), channel_id=1, source_target_pairs={{8,0},{16,8},{24,16},{32,24},{40,32},{48,40},{56,48},{64,56},{72,6... | collective-permute-start | bytes 245768 | tf_op jit(solution)/shard_map/ppermute | solution.py:204
  12.2 1.9 %collective-permute-start = (f32[20480]{0:T(1024)S(1)}, f32[20480]{0:T(1024)S(1)}, u32[]{:S(2)}, u32[]{:S(2)}) collective-permute-start(f32[20480]{0:T(1024)S(1)} %get-tuple-element.141), channel_id=1, source_target_pairs={{0,8},{8,16},{16,24},{24,32},{32,40},{40,48},{48,56},{56,64},{64,7... | collective-permute-start | bytes 245768 | tf_op jit(solution)/shard_map/ppermute | solution.py:203
  14.2 0.6 and_select_fusion
  15.5 0.6 fusion.104.rows_ref
  16.2 0.7 bitcast_select_fusion.index_ref
  16.9 0.6 broadcast_in_dim.69.state_ref
  17.5 3.2 %shard_map.149.static_ref = f32[8,38,128]{2,1,0:T(8,128)} custom-call(f32[4,2048]{1,0:T(4,128)} %broadcast_in_dim.69.state_ref, f32[1,2048]{1,0:T(1,128)} %bitcast.201, f32[1,2048]{1,0:T(1,128)} %bitcast.214, f32[32,2048]{1,0:T(8,128)} %bitcast.189, s32[8,128]{1,0:T(8,128)} %bitcast_select_fusion.index_ref), custom_call_target="tpu_custom_call" | custom-call | tf_op jit(solution)/shard_map/pallas_call | solution.py:161
  20.9 0.2 fusion.112
  21.2 0.4 reshape.584
  21.5 0.4 reshape.587
  22.0 4.2 %collective-permute-start.3 = (f32[13152]{0:T(1024)S(1)}, f32[13152]{0:T(1024)S(1)}, u32[]{:S(2)}, u32[]{:S(2)}) collective-permute-start(f32[13152]{0:T(1024)S(1)} %get-tuple-element.140), channel_id=1, source_target_pairs={{1,0},{2,1},{3,2},{4,3},{5,4},{6,5},{7,6},{128,7},{129,128},{130,1... | collective-permute-start | bytes 157832 | tf_op jit(solution)/shard_map/ppermute | solution.py:204
  26.2 1.9 %collective-permute-start.2 = (f32[13152]{0:T(1024)S(1)}, f32[13152]{0:T(1024)S(1)}, u32[]{:S(2)}, u32[]{:S(2)}) collective-permute-start(f32[13152]{0:T(1024)S(1)} %get-tuple-element.139), channel_id=1, source_target_pairs={{0,1},{1,2},{2,3},{3,4},{4,5},{5,6},{6,7},{7,128},{128,129},{129,1... | collective-permute-start | bytes 157832 | tf_op jit(solution)/shard_map/ppermute | solution.py:203
  28.1 0.7 pad_maximum_fusion.3.window_ref
  28.8 2.7 %shard_map.148 = f32[2,2048]{1,0:T(2,128)} custom-call(f32[2,128,128]{2,1,0:T(8,128)} %pad_maximum_fusion.3.window_ref, s32[1,2048]{1,0:T(1,128)} %fusion.104.rows_ref, s32[1,2048]{1,0:T(1,128)} %get-tuple-element.57.cols_ref), custom_call_target="tpu_custom_call" | custom-call | tf_op jit(solution)/shard_map/pallas_call | solution.py:133
  31.5 0.7 reshape.588
  32.2 3.0 %collective-permute-done.2 = f32[13152]{0:T(1024)S(1)} collective-permute-done((f32[13152]{0:T(1024)S(1)}, f32[13152]{0:T(1024)S(1)}, u32[]{:S(2)}, u32[]{:S(2)}) %collective-permute-start.2) | collective-permute-done | bytes 52640 | tf_op jit(solution)/shard_map/ppermute | solution.py:203
  35.2 0.7 reshape.586
  36.0 0.1 fusion.99
  36.1 0.7 pad_maximum_fusion
  36.8 0.1 maximum_bitcast_fusion
  37.1 0.1 broadcast_multiply_fusion
  37.2 0.1 slice_multiply_fusion.5
  37.4 0.2 subtract_multiply_fusion.12
  37.5 1.1 %fusion.84 = f32[2,8,72,136]{3,2,1,0:T(8,128)S(1)} fusion(f32[2,1,72,136]{3,2,1,0:T(8,128)S(1)} %fusion.99, f32[1,8,72,136]{3,2,1,0:T(8,128)S(1)} %get-tuple-element.108, f32[1,8,72,136]{3,2,1,0:T(8,128)S(1)} %get-tuple-element.107, f32[2,7,72,136]{3,2,1,0:T(8,128)S(1)} %subtract_multiply_fusion.12, f32[2,8,72,136]{3,2,1,0:T(8,128)S(1)} %broadcast_multiply_fusion, ...), kind=kLoop, calls=%fused_computation.160 | loop fusion | flops 2036736 | bytes 2820128 | tf_op jit(solution)/shard_map/mul | solution.py:55
  38.6 0.1 slice_multiply_fusion.3
  38.7 0.2 fusion.88
  38.9 1.1 %fusion.85 = f32[2,8,72,136]{3,2,1,0:T(8,128)S(1)} fusion(f32[2,1,72,136]{3,2,1,0:T(8,128)S(1)} %fusion.99, f32[1,8,72,136]{3,2,1,0:T(8,128)S(1)} %get-tuple-element.106, f32[1,8,72,136]{3,2,1,0:T(8,128)S(1)} %get-tuple-element.105, f32[2,7,72,136]{3,2,1,0:T(8,128)S(1)} %fusion.88, f32[2,8,72,136]{3,2,1,0:T(8,128)S(1)} %fusion.84, ...), kind=kLoop, calls=%fused_computation.161 | loop fusion | flops 2036736 | bytes 2820128 | tf_op jit(solution)/shard_map/mul | solution.py:55
  40.0 0.1 slice_multiply_fusion.1
  40.1 0.2 fusion.87
  40.3 1.1 %fusion.86 = f32[2,8,72,136]{3,2,1,0:T(8,128)S(1)} fusion(f32[2,1,72,136]{3,2,1,0:T(8,128)S(1)} %fusion.99, f32[1,8,72,136]{3,2,1,0:T(8,128)S(1)} %get-tuple-element.104, f32[1,8,72,136]{3,2,1,0:T(8,128)S(1)} %get-tuple-element.103, f32[2,7,72,136]{3,2,1,0:T(8,128)S(1)} %fusion.87, f32[2,8,72,136]{3,2,1,0:T(8,128)S(1)} %fusion.85, ...), kind=kLoop, calls=%fused_computation.162 | loop fusion | flops 2036736 | bytes 2820128 | tf_op jit(solution)/shard_map/mul | solution.py:55
  41.4 0.2 slice_multiply_fusion.8
  41.6 0.3 fusion.97
  41.9 0.8 fusion.96
  42.7 5.1 %collective-permute-start.5 = (f32[2,32,128]{2,1,0:T(8,128)S(1)}, f32[2,32,128]{2,1,0:T(8,128)S(1)}, u32[]{:S(2)}, u32[]{:S(2)}) collective-permute-start(f32[2,32,128]{2,1,0:T(8,128)S(1)} %get-tuple-element.124), channel_id=1, source_target_pairs={{8,0},{16,8},{24,16},{32,24},{40,32},{48,40},{56,48},{64,56},{72,6... | collective-permute-start | bytes 98312 | tf_op jit(solution)/shard_map/ppermute | solution.py:204
  47.8 1.9 %collective-permute-start.4 = (f32[2,32,128]{2,1,0:T(8,128)S(1)}, f32[2,32,128]{2,1,0:T(8,128)S(1)}, u32[]{:S(2)}, u32[]{:S(2)}) collective-permute-start(f32[2,32,128]{2,1,0:T(8,128)S(1)} %get-tuple-element.123), channel_id=1, source_target_pairs={{0,8},{8,16},{16,24},{24,32},{32,40},{40,48},{48,56},{56,64},{64,7... | collective-permute-start | bytes 98312 | tf_op jit(solution)/shard_map/ppermute | solution.py:203
  49.8 0.1 fusion.120
  50.2 9.7 %conditional.1 = (f32[16,2,128]{2,0,1:T(8,128)S(1)}) conditional(s32[]{:T(128)} %clamp.3, (s32[3,64]{1,0:T(4,128)S(1)}, s32[]{:T(128)}, f32[48,5,128]{2,1,0:T(8,128)S(1)}) %tuple.85, (s32[3,64]{1,0:T(4,128)S(1)}, s32[]{:T(128)}, f32[48,5,128]{2,1,0:T(8,128)S(1)}) %tuple.86, (s32[3,64]{1,0:T(4,128)S(1)}, s32[]{:T(128)}, ...), branch_computations={%region_0.3_spmd, %region_3.6_spmd, %region_6.9_spmd} | conditional | flops 31477696 | bytes 1797260 | solution.py:347
  50.5 0.6 gather_fusion.5
  51.1 0.1 fusion.111
  51.2 0.6 gather_fusion.4
  51.9 0.1 fusion.110
  52.0 7.1 %multiply_reduce_fusion.5 = (f32[64,128]{1,0:T(8,128)S(1)}, f32[64,128]{1,0:T(8,128)S(1)}) fusion(f32[64,128]{1,0:T(8,128)S(1)} %bitcast.207, f32[64,128]{1,0:T(8,128)S(1)} %bitcast.212, f32[64,128]{1,0:T(8,128)S(1)} %bitcast.208, f32[64,128]{1,0:T(8,128)S(1)} %bitcast.213, f32[64,128]{1,0:T(8,128)S(1)} %bitcast.205, f32[64,128]{1,0:T(8,128)S(1)} %bitcast.210, ...), kind=kLoop, calls=%fused_computation.95 | loop fusion | flops 28295168 | bytes 393216 | tf_op jit(solution)/shard_map/cond/branch_2_fun/reduce_sum | solution.py:73
  59.1 0.7 iota_compare_fusion.5
  59.7 0.2 fusion.45
  60.0 0.7 pad_maximum_fusion.4.window_ref
  60.6 2.7 %shard_map.150 = f32[2,2048]{1,0:T(2,128)} custom-call(f32[2,128,128]{2,1,0:T(8,128)} %pad_maximum_fusion.4.window_ref, s32[1,2048]{1,0:T(1,128)} %fusion.104.rows_ref, s32[1,2048]{1,0:T(1,128)} %get-tuple-element.57.cols_ref), custom_call_target="tpu_custom_call" | custom-call | tf_op jit(solution)/shard_map/pallas_call | solution.py:133
  63.3 0.7 multiply_reduce_fusion.6
  64.1 0.8 multiply_add_fusion
  64.9 0.6 pad_maximum_fusion.17
  65.5 2.4 %shard_map.151 = f32[8,38,128]{2,1,0:T(8,128)} custom-call(f32[4,2048]{1,0:T(4,128)} %get-tuple-element.137.state_ref, s32[8,128]{1,0:T(8,128)} %bitcast_select_fusion.index_ref, f32[8,38,128]{2,1,0:T(8,128)} %shard_map.149.static_ref), custom_call_target="tpu_custom_call" | custom-call | tf_op jit(solution)/shard_map/pallas_call | solution.py:189
  67.9 0.9 fusion.114
  68.8 1.9 %collective-permute-start.7 = (f32[3,38,128]{2,1,0:T(8,128)S(1)}, f32[3,38,128]{2,1,0:T(8,128)S(1)}, u32[]{:S(2)}, u32[]{:S(2)}) collective-permute-start(f32[3,38,128]{2,1,0:T(8,128)S(1)} %get-tuple-element.118), channel_id=1, source_target_pairs={{0,8},{8,16},{16,24},{24,32},{32,40},{40,48},{48,56},{56,64},{64,7... | collective-permute-start | bytes 175112 | tf_op jit(solution)/shard_map/ppermute | solution.py:203
  70.7 0.8 fusion.113
  71.4 6.0 %collective-permute-start.6 = (f32[3,38,128]{2,1,0:T(8,128)S(1)}, f32[3,38,128]{2,1,0:T(8,128)S(1)}, u32[]{:S(2)}, u32[]{:S(2)}) collective-permute-start(f32[3,38,128]{2,1,0:T(8,128)S(1)} %get-tuple-element.117), channel_id=1, source_target_pairs={{8,0},{16,8},{24,16},{32,24},{40,32},{48,40},{56,48},{64,56},{72,6... | collective-permute-start | bytes 175112 | tf_op jit(solution)/shard_map/ppermute | solution.py:204
  77.5 1.8 %collective-permute-done.6 = f32[3,38,128]{2,1,0:T(8,128)S(1)} collective-permute-done((f32[3,38,128]{2,1,0:T(8,128)S(1)}, f32[3,38,128]{2,1,0:T(8,128)S(1)}, u32[]{:S(2)}, u32[]{:S(2)}) %collective-permute-start.6) | collective-permute-done | bytes 58400 | tf_op jit(solution)/shard_map/ppermute | solution.py:204
  79.3 3.4 %collective-permute-start.8 = (f32[3,38,128]{2,1,0:T(8,128)S(1)}, f32[3,38,128]{2,1,0:T(8,128)S(1)}, u32[]{:S(2)}, u32[]{:S(2)}) collective-permute-start(f32[3,38,128]{2,1,0:T(8,128)S(1)} %pad_maximum_fusion.8), channel_id=1, source_target_pairs={{1,0},{2,1},{3,2},{4,3},{5,4},{6,5},{7,6},{128,7},{129,128},{130,1... | collective-permute-start | bytes 175112 | tf_op jit(solution)/shard_map/ppermute | solution.py:204
  82.7 1.8 %collective-permute-done.8 = f32[3,38,128]{2,1,0:T(8,128)S(1)} collective-permute-done((f32[3,38,128]{2,1,0:T(8,128)S(1)}, f32[3,38,128]{2,1,0:T(8,128)S(1)}, u32[]{:S(2)}, u32[]{:S(2)}) %collective-permute-start.8) | collective-permute-done | bytes 58400 | tf_op jit(solution)/shard_map/ppermute | solution.py:204
  84.6 1.9 %collective-permute-start.9 = (f32[3,38,128]{2,1,0:T(8,128)S(1)}, f32[3,38,128]{2,1,0:T(8,128)S(1)}, u32[]{:S(2)}, u32[]{:S(2)}) collective-permute-start(f32[3,38,128]{2,1,0:T(8,128)S(1)} %pad_maximum_fusion.9), channel_id=1, source_target_pairs={{0,1},{1,2},{2,3},{3,4},{4,5},{5,6},{6,7},{7,128},{128,129},{129,1... | collective-permute-start | bytes 175112 | tf_op jit(solution)/shard_map/ppermute | solution.py:203
  86.5 7.3 %collective-permute-done.9 = f32[3,38,128]{2,1,0:T(8,128)S(1)} collective-permute-done((f32[3,38,128]{2,1,0:T(8,128)S(1)}, f32[3,38,128]{2,1,0:T(8,128)S(1)}, u32[]{:S(2)}, u32[]{:S(2)}) %collective-permute-start.9) | collective-permute-done | bytes 58400 | tf_op jit(solution)/shard_map/ppermute | solution.py:203
  93.8 0.7 copy.18
  (99 shorter events, 1.0 us)
Async XLA Ops:
  0.6 14.2 %copy-start.6 = (f32[1,1,2048]{2,1,0:T(1,128)S(1)}, f32[1,1,2048]{2,1,0:T(1,128)}, u32[]{:S(2)}) copy-start(f32[1,1,2048]{2,1,0:T(1,128)} %param.21) | copy-start | bytes 24580
  0.6 16.2 %copy-start.3 = (f32[1,1,2,2048]{3,2,1,0:T(2,128)S(1)}, f32[1,1,2,2048]{3,2,1,0:T(2,128)}, u32[]{:S(2)}) copy-start(f32[1,1,2,2048]{3,2,1,0:T(2,128)} %param.20) | copy-start | bytes 49156
  0.7 16.2 %copy-start.4 = (f32[1,1,2,2048]{3,2,1,0:T(2,128)S(1)}, f32[1,1,2,2048]{3,2,1,0:T(2,128)}, u32[]{:S(2)}) copy-start(f32[1,1,2,2048]{3,2,1,0:T(2,128)} %param.19) | copy-start | bytes 49156
  0.7 13.4 %copy-start.1 = (f32[2,64,128]{2,1,0:T(8,128)S(1)}, f32[2,64,128]{2,1,0:T(8,128)}, u32[]{:S(2)}) copy-start(f32[2,64,128]{2,1,0:T(8,128)} %param.17) | copy-start | bytes 196612
  0.7 13.5 %copy-start.5 = (s32[64,128]{1,0:T(8,128)S(1)}, s32[64,128]{1,0:T(8,128)}, u32[]{:S(2)}) copy-start(s32[64,128]{1,0:T(8,128)} %param.18) | copy-start | bytes 98308
  0.7 13.5 %copy-start.8 = (s32[1,1,2048]{2,1,0:T(1,128)S(1)}, s32[1,1,2048]{2,1,0:T(1,128)}, u32[]{:S(2)}) copy-start(s32[1,1,2048]{2,1,0:T(1,128)} %param.24) | copy-start | bytes 24580
  0.7 14.8 %copy-start.11 = (s32[1,1,3,64]{3,1,2,0:T(1,128)S(1)}, s32[1,1,3,64]{3,1,2,0:T(1,128)}, u32[]{:S(2)}) copy-start(s32[1,1,3,64]{3,1,2,0:T(1,128)} %param.26) | copy-start | bytes 2308
  0.7 15.5 %copy-start.10 = (s32[1,1,8,128]{3,2,1,0:T(8,128)S(1)}, s32[1,1,8,128]{3,2,1,0:T(8,128)}, u32[]{:S(2)}) copy-start(s32[1,1,8,128]{3,2,1,0:T(8,128)} %param.27) | copy-start | bytes 12292
  0.7 15.4 %copy-start.12 = (s32[1,1,8]{2,1,0:T(1,128)S(1)}, s32[1,1,8]{2,1,0:T(1,128)}, u32[]{:S(2)}) copy-start(s32[1,1,8]{2,1,0:T(1,128)} %param.28) | copy-start | bytes 100
  4.0 16.8 %copy-start = (f32[2,8,64,128]{3,2,1,0:T(8,128)S(1)}, f32[2,8,64,128]{3,2,1,0:T(8,128)}, u32[]{:S(2)}) copy-start(f32[2,8,64,128]{3,2,1,0:T(8,128)} %param.16) | copy-start | bytes 1572868
  4.1 16.6 %collective-permute-start.1 = (f32[20480]{0:T(1024)S(1)}, f32[20480]{0:T(1024)S(1)}, u32[]{:S(2)}, u32[]{:S(2)}) collective-permute-start(f32[20480]{0:T(1024)S(1)} %get-tuple-element.142), channel_id=1, source_target_pairs={{8,0},{16,8},{24,16},{32,24},{40,32},{48,40},{56,48},{64,56},{72,6... | collective-permute-start | bytes 245768 | tf_op jit(solution)/shard_map/ppermute | solution.py:204
  12.2 8.5 %collective-permute-start = (f32[20480]{0:T(1024)S(1)}, f32[20480]{0:T(1024)S(1)}, u32[]{:S(2)}, u32[]{:S(2)}) collective-permute-start(f32[20480]{0:T(1024)S(1)} %get-tuple-element.141), channel_id=1, source_target_pairs={{0,8},{8,16},{16,24},{24,32},{32,40},{40,48},{48,56},{56,64},{64,7... | collective-permute-start | bytes 245768 | tf_op jit(solution)/shard_map/ppermute | solution.py:203
  22.0 9.5 %collective-permute-start.3 = (f32[13152]{0:T(1024)S(1)}, f32[13152]{0:T(1024)S(1)}, u32[]{:S(2)}, u32[]{:S(2)}) collective-permute-start(f32[13152]{0:T(1024)S(1)} %get-tuple-element.140), channel_id=1, source_target_pairs={{1,0},{2,1},{3,2},{4,3},{5,4},{6,5},{7,6},{128,7},{129,128},{130,1... | collective-permute-start | bytes 157832 | tf_op jit(solution)/shard_map/ppermute | solution.py:204
  26.2 9.1 %collective-permute-start.2 = (f32[13152]{0:T(1024)S(1)}, f32[13152]{0:T(1024)S(1)}, u32[]{:S(2)}, u32[]{:S(2)}) collective-permute-start(f32[13152]{0:T(1024)S(1)} %get-tuple-element.139), channel_id=1, source_target_pairs={{0,1},{1,2},{2,3},{3,4},{4,5},{5,6},{6,7},{7,128},{128,129},{129,1... | collective-permute-start | bytes 157832 | tf_op jit(solution)/shard_map/ppermute | solution.py:203
  42.7 7.6 %copy-start.2 = (f32[2,8,64,128]{3,2,1,0:T(8,128)}, f32[2,8,64,128]{3,2,1,0:T(8,128)S(1)}, u32[]{:S(2)}) copy-start(f32[2,8,64,128]{3,2,1,0:T(8,128)S(1)} %fusion.96) | copy-start | bytes 1572868
  42.7 17.3 %collective-permute-start.5 = (f32[2,32,128]{2,1,0:T(8,128)S(1)}, f32[2,32,128]{2,1,0:T(8,128)S(1)}, u32[]{:S(2)}, u32[]{:S(2)}) collective-permute-start(f32[2,32,128]{2,1,0:T(8,128)S(1)} %get-tuple-element.124), channel_id=1, source_target_pairs={{8,0},{16,8},{24,16},{32,24},{40,32},{48,40},{56,48},{64,56},{72,6... | collective-permute-start | bytes 98312 | tf_op jit(solution)/shard_map/ppermute | solution.py:204
  47.8 12.1 %collective-permute-start.4 = (f32[2,32,128]{2,1,0:T(8,128)S(1)}, f32[2,32,128]{2,1,0:T(8,128)S(1)}, u32[]{:S(2)}, u32[]{:S(2)}) collective-permute-start(f32[2,32,128]{2,1,0:T(8,128)S(1)} %get-tuple-element.123), channel_id=1, source_target_pairs={{0,8},{8,16},{16,24},{24,32},{32,40},{40,48},{48,56},{56,64},{64,7... | collective-permute-start | bytes 98312 | tf_op jit(solution)/shard_map/ppermute | solution.py:203
  50.2 13.9 %copy-start.7 = (f32[2,2048]{1,0:T(2,128)S(1)}, f32[2,2048]{1,0:T(2,128)}, u32[]{:S(2)}) copy-start(f32[2,2048]{1,0:T(2,128)} %shard_map.148) | copy-start | bytes 49156
  50.2 13.9 %copy-start.9 = (f32[1,1,2048]{2,1,0:T(1,128)S(1)}, f32[1,1,2048]{2,1,0:T(1,128)}, u32[]{:S(2)}) copy-start(f32[1,1,2048]{2,1,0:T(1,128)} %param.22) | copy-start | bytes 24580
  68.8 8.7 %collective-permute-start.7 = (f32[3,38,128]{2,1,0:T(8,128)S(1)}, f32[3,38,128]{2,1,0:T(8,128)S(1)}, u32[]{:S(2)}, u32[]{:S(2)}) collective-permute-start(f32[3,38,128]{2,1,0:T(8,128)S(1)} %get-tuple-element.118), channel_id=1, source_target_pairs={{0,8},{8,16},{16,24},{24,32},{32,40},{40,48},{48,56},{56,64},{64,7... | collective-permute-start | bytes 175112 | tf_op jit(solution)/shard_map/ppermute | solution.py:203
  71.4 7.9 %collective-permute-start.6 = (f32[3,38,128]{2,1,0:T(8,128)S(1)}, f32[3,38,128]{2,1,0:T(8,128)S(1)}, u32[]{:S(2)}, u32[]{:S(2)}) collective-permute-start(f32[3,38,128]{2,1,0:T(8,128)S(1)} %get-tuple-element.117), channel_id=1, source_target_pairs={{8,0},{16,8},{24,16},{32,24},{40,32},{48,40},{56,48},{64,56},{72,6... | collective-permute-start | bytes 175112 | tf_op jit(solution)/shard_map/ppermute | solution.py:204
  79.3 5.3 %collective-permute-start.8 = (f32[3,38,128]{2,1,0:T(8,128)S(1)}, f32[3,38,128]{2,1,0:T(8,128)S(1)}, u32[]{:S(2)}, u32[]{:S(2)}) collective-permute-start(f32[3,38,128]{2,1,0:T(8,128)S(1)} %pad_maximum_fusion.8), channel_id=1, source_target_pairs={{1,0},{2,1},{3,2},{4,3},{5,4},{6,5},{7,6},{128,7},{129,128},{130,1... | collective-permute-start | bytes 175112 | tf_op jit(solution)/shard_map/ppermute | solution.py:204
  84.6 9.2 %collective-permute-start.9 = (f32[3,38,128]{2,1,0:T(8,128)S(1)}, f32[3,38,128]{2,1,0:T(8,128)S(1)}, u32[]{:S(2)}, u32[]{:S(2)}) collective-permute-start(f32[3,38,128]{2,1,0:T(8,128)S(1)} %pad_maximum_fusion.9), channel_id=1, source_target_pairs={{0,1},{1,2},{2,3},{3,4},{4,5},{5,6},{6,7},{7,128},{128,129},{129,1... | collective-permute-start | bytes 175112 | tf_op jit(solution)/shard_map/ppermute | solution.py:203

commit v3 on v2

--- a/solution.py
+++ b/solution.py
@@ -194,6 +194,70 @@
             pltpu.VMEM((3 * padded, state.shape[1]), jnp.float32),
         ],
     )(state, index, static)
+
+
+def tail_kernel(
+    window_ref, rows_ref, cols_ref, position_ref, velocity_ref, radius_ref, mass_ref, contact_ref,
+    wind_ref, index_ref, fixed_ref, next_ref, out_ref, sample_ref, record_ref, stack_ref,
+):
+    window_rows, window_cols = window_ref.shape[1:]
+    floes = rows_ref.shape[1]
+    slots = index_ref.shape[1]
+    onehot = (
+        lax.broadcasted_iota(jnp.int32, (window_rows, floes), 0) == rows_ref[...]
+    ).astype(jnp.bfloat16)
+    pick = lax.broadcasted_iota(jnp.int32, (window_cols, floes), 0) == cols_ref[...]
+    sampled = [
+        jnp.sum(
+            jnp.where(pick, stacked_select(sample_ref, window_ref[channel].T, onehot), 0.0),
+            axis=0,
+            keepdims=True,
+        )
+        for channel in range(2)
+    ]
+    velocity = velocity_ref[...]
+    position = position_ref[...]
+    contact = contact_ref[...]
+    wind = wind_ref[...]
+    radius = radius_ref[...]
+    mass = mass_ref[...]
+    relative = [sampled[axis] - velocity[axis : axis + 1] for axis in range(2)]
+    speed = jnp.sqrt(relative[0] * relative[0] + relative[1] * relative[1])
+    area = math.pi * radius * radius
+    for axis in range(2):
+        total = contact[axis : axis + 1] + area * (
+            WATER_DRAG * speed * relative[axis] + AIR_GAIN * wind[axis : axis + 1]
+        )
+        new_velocity = velocity[axis : axis + 1] + ICE_STEP * total / mass
+        next_ref[2 + axis : 3 + axis, :] = new_velocity
+        next_ref[axis : axis + 1, :] = position[axis : axis + 1] + ICE_STEP * new_velocity
+    rows = next_ref.shape[0]
+    record_ref[...] = jnp.zeros_like(record_ref)
+    stack_ref[...] = jnp.zeros_like(stack_ref)
+    record_ref[0:rows, :] = next_ref[...]
+    record = record_ref[...]
+    out_ref[...] = fixed_ref[...]
+    for way in range(index_ref.shape[0]):
+        chosen = (
+            lax.broadcasted_iota(jnp.int32, (floes, slots), 0) == index_ref[way : way + 1, :]
+        ).astype(jnp.bfloat16)
+        out_ref[way, 0:rows, :] = stacked_select(stack_ref, record, chosen)[0:rows]
+
+
+def sample_update_gather(window, rows, cols, position, velocity, radius, mass, contact, wind, index, fixed):
+    floes = rows.shape[1]
+    return pl.pallas_call(
+        tail_kernel,
+        out_shape=(
+            jax.ShapeDtypeStruct((4, floes), jnp.float32),
+            jax.ShapeDtypeStruct(fixed.shape, jnp.float32),
+        ),
+        scratch_shapes=[
+            pltpu.VMEM((3 * window.shape[2], window.shape[1]), jnp.float32),
+            pltpu.VMEM((8, floes), jnp.float32),
+            pltpu.VMEM((24, floes), jnp.float32),
+        ],
+    )(window, rows, cols, position, velocity, radius, mass, contact, wind, index, fixed)
 
 
 def exchange(low, high, axis):
@@ -330,7 +394,6 @@
     surface = jnp.stack([flow[0, 0], flow[1, 0]])
     from_above, from_below = exchange(surface[:, :margin], surface[:, -margin:], "gx")
     near = jnp.concatenate([from_above, surface, from_below], axis=1)
-    sampled_flow = sample_surface(near, floe_rows, floe_cols)
     lists = contact_list[0, 0]
     count = contact_count[0, 0]
     slots = lists.shape[1]
@@ -346,14 +409,10 @@
     which = sum((count > size).astype(jnp.int32) for size in sizes[:-1])
     contact = lax.switch(which, [pass_over(size) for size in sizes], lists, count)
     contact = contact.transpose(1, 0, 2).reshape(2, floes)
-    area = math.pi * radius * radius
-    relative = sampled_flow - velocity
-    speed = jnp.sqrt(jnp.sum(relative * relative, axis=0, keepdims=True))
-    total = contact + area[None] * (WATER_DRAG * speed * relative + AIR_GAIN * sampled_wind)
-    new_velocity = velocity + ICE_STEP * total / mass[None]
-    new_position = position + ICE_STEP * new_velocity
-    floe_next = jnp.concatenate([new_position, new_velocity], axis=0)
-    outgoing = gather_state(floe_next, chosen, fixed_records)
+    floe_next, outgoing = sample_update_gather(
+        near, floe_rows, floe_cols, position, velocity, radius[None], mass[None], contact,
+        sampled_wind, chosen, fixed_records,
+    )
     from_above, from_below = exchange(outgoing[0:3], outgoing[5:8], "gx")
     heading_left = jnp.stack([from_below[0], outgoing[3], from_above[0]])
     heading_right = jnp.stack([from_below[2], outgoing[4], from_above[2]])

time: 92.9 us -> 92.5 us (level); the launches traced: 94.5 us -> 91.7 us
  other arithmetic: 22.5 us -> 14.8 us
  starting transfers between devices: 36.4 us -> 41.2 us
  Pallas kernels: 10.9 us -> 9.87 us
    reduce_sum x1, other arithmetic: 7.06 us -> 1.77 us  [pair_forces(): jnp.sum(magnitude * normal_x, axis=1)]
    ppermute x5, starting transfers between devices: 26.8 us -> 31.6 us  [exchange(): from_next = lax.ppermute(low, axis, down)]
    pallas_call x2 -> x1, Pallas kernels: 5.33 us -> 2.66 us  [sample_surface(): pl.pallas_call(sample_kernel, out_shape=jax.ShapeDtypeStruct((window.shap...]
    pallas_call x1, Pallas kernels: 2.39 us -> 4.03 us  [sample_update_gather(): pl.pallas_call(tail_kernel, out_shape=(jax.ShapeDtypeStruct((4, floes), j...]
  transfers between devices with their start and end apart: 10 -> 10, of which waited for: 4 -> 5; matrix products, arithmetic and copies ran while one was open for 15% -> 10% of each run, Pallas kernels for 6% -> 6%
where the time goes in v3:
time: 92.5 us; the launch traced here: 91.7 us
  starting transfers between devices  41.2 us (45%)
  waiting for transfers between devices  14.9 us (16%)
  other arithmetic  14.8 us (16%)
  Pallas kernels  9.87 us (11%)
  local copies, waits for them, and re-layouts  8.46 us (9%)
  between operations  2.05 us (2%)
    ppermute x5, starting transfers between devices, exchange(): from_next = lax.ppermute(low, axis, down)  31.6 us
    ppermute x5, waiting for transfers between devices, exchange(): from_previous = lax.ppermute(high, axis, up)  11.2 us
    ppermute x5, starting transfers between devices, exchange(): from_previous = lax.ppermute(high, axis, up)  9.6 us
    pallas_call x1, Pallas kernels, sample_update_gather(): pl.pallas_call(tail_kernel, out_shape=(jax.ShapeDtypeStruct((4, floes), j...  4.03 us
    mul x4, other arithmetic, ocean_substep(): return (flow + horizontal * lap + vert + turning + surface) * wet[None]  3.99 us
    ppermute x5, waiting for transfers between devices, exchange(): from_next = lax.ppermute(low, axis, down)  3.67 us
    pallas_call x1, Pallas kernels, gather_records(): pl.pallas_call(gather_kernel, out_shape=jax.ShapeDtypeStruct((index.shape...  3.18 us
    pallas_call x1, Pallas kernels, sample_surface(): pl.pallas_call(sample_kernel, out_shape=jax.ShapeDtypeStruct((window.shap...  2.66 us
  transfers between devices with their start and end apart: 10, of which 5 were waited for; matrix products, arithmetic and copies ran while one was open for 10% of the time, Pallas kernels for 6%

profile of v3, /device:TPU:24, one launch (start us, length us, event | category | flops | bytes accessed | tf_op | source)
XLA Modules:
  0.0 91.7 jit_solution(17769528778739927410)
XLA Ops:
  0.7 0.8 pad_maximum_fusion.17
  1.5 0.8 fusion.114
  2.3 0.8 convert_bitcast_fusion
  3.1 0.9 %pad_maximum_fusion.15 = (f32[19,4,128]{2,1,0:T(4,128)S(1)}, f32[19,4,128]{2,1,0:T(4,128)S(1)}) fusion(f32[1,64,128]{2,1,0:T(8,128)S(1)} %convert_bitcast_fusion, f32[2,64,128]{2,1,0:T(8,128)} %param.17, f32[16,64,128]{2,1,0:T(8,128)} %bitcast.162), kind=kLoop, calls=%fused_computation.218 | loop fusion | flops 38912 | bytes 700416 | tf_op jit(solution)/shard_map/slice | solution.py:316
  4.1 8.1 %collective-permute-start.1 = (f32[20480]{0:T(1024)S(1)}, f32[20480]{0:T(1024)S(1)}, u32[]{:S(2)}, u32[]{:S(2)}) collective-permute-start(f32[20480]{0:T(1024)S(1)} %get-tuple-element.142), channel_id=1, source_target_pairs={{8,0},{16,8},{24,16},{32,24},{40,32},{48,40},{56,48},{64,56},{72,6... | collective-permute-start | bytes 245768 | tf_op jit(solution)/shard_map/ppermute | solution.py:268
  12.2 1.9 %collective-permute-start = (f32[20480]{0:T(1024)S(1)}, f32[20480]{0:T(1024)S(1)}, u32[]{:S(2)}, u32[]{:S(2)}) collective-permute-start(f32[20480]{0:T(1024)S(1)} %get-tuple-element.141), channel_id=1, source_target_pairs={{0,8},{8,16},{16,24},{24,32},{32,40},{40,48},{48,56},{56,64},{64,7... | collective-permute-start | bytes 245768 | tf_op jit(solution)/shard_map/ppermute | solution.py:267
  14.2 0.6 and_select_fusion
  15.5 0.6 fusion.103.rows_ref
  16.1 0.7 bitcast_select_fusion.index_ref
  16.8 0.6 broadcast_in_dim.69.state_ref
  17.5 3.2 %shard_map.149.fixed_ref = f32[8,38,128]{2,1,0:T(8,128)} custom-call(f32[4,2048]{1,0:T(4,128)} %broadcast_in_dim.69.state_ref, f32[1,2048]{1,0:T(1,128)} %bitcast.188, f32[1,2048]{1,0:T(1,128)} %bitcast.202, f32[32,2048]{1,0:T(8,128)} %bitcast.172, s32[8,128]{1,0:T(8,128)} %bitcast_select_fusion.index_ref), custom_call_target="tpu_custom_call" | custom-call | tf_op jit(solution)/shard_map/pallas_call | solution.py:161
  20.8 0.1 pad_maximum_fusion.1
  20.9 0.2 fusion.110
  21.2 0.4 reshape.568
  21.5 0.4 reshape.571
  21.9 0.1 pad_maximum_fusion.11
  22.0 4.2 %collective-permute-start.3 = (f32[13152]{0:T(1024)S(1)}, f32[13152]{0:T(1024)S(1)}, u32[]{:S(2)}, u32[]{:S(2)}) collective-permute-start(f32[13152]{0:T(1024)S(1)} %get-tuple-element.140), channel_id=1, source_target_pairs={{1,0},{2,1},{3,2},{4,3},{5,4},{6,5},{7,6},{128,7},{129,128},{130,1... | collective-permute-start | bytes 157832 | tf_op jit(solution)/shard_map/ppermute | solution.py:268
  26.2 1.9 %collective-permute-start.2 = (f32[13152]{0:T(1024)S(1)}, f32[13152]{0:T(1024)S(1)}, u32[]{:S(2)}, u32[]{:S(2)}) collective-permute-start(f32[13152]{0:T(1024)S(1)} %get-tuple-element.139), channel_id=1, source_target_pairs={{0,1},{1,2},{2,3},{3,4},{4,5},{5,6},{6,7},{7,128},{128,129},{129,1... | collective-permute-start | bytes 157832 | tf_op jit(solution)/shard_map/ppermute | solution.py:267
  28.1 0.7 pad_maximum_fusion.3.window_ref
  28.8 2.7 %shard_map.148.wind_ref = f32[2,2048]{1,0:T(2,128)} custom-call(f32[2,128,128]{2,1,0:T(8,128)} %pad_maximum_fusion.3.window_ref, s32[1,2048]{1,0:T(1,128)} %fusion.103.rows_ref, s32[1,2048]{1,0:T(1,128)} %get-tuple-element.59.cols_ref), custom_call_target="tpu_custom_call" | custom-call | tf_op jit(solution)/shard_map/pallas_call | solution.py:133
  31.4 0.7 reshape.572
  32.2 3.1 %collective-permute-done.2 = f32[13152]{0:T(1024)S(1)} collective-permute-done((f32[13152]{0:T(1024)S(1)}, f32[13152]{0:T(1024)S(1)}, u32[]{:S(2)}, u32[]{:S(2)}) %collective-permute-start.2) | collective-permute-done | bytes 52640 | tf_op jit(solution)/shard_map/ppermute | solution.py:267
  35.2 0.7 reshape.570
  35.9 0.1 fusion.99
  36.1 0.7 pad_maximum_fusion
  36.8 0.1 maximum_bitcast_fusion
  36.9 0.1 slice.618
  37.1 0.1 broadcast_multiply_fusion
  37.2 0.1 slice_multiply_fusion.5
  37.3 0.1 subtract_multiply_fusion.12
  37.5 1.1 %fusion.84 = f32[2,8,72,136]{3,2,1,0:T(8,128)S(1)} fusion(f32[2,1,72,136]{3,2,1,0:T(8,128)S(1)} %fusion.99, f32[1,8,72,136]{3,2,1,0:T(8,128)S(1)} %get-tuple-element.110, f32[1,8,72,136]{3,2,1,0:T(8,128)S(1)} %get-tuple-element.109, f32[2,7,72,136]{3,2,1,0:T(8,128)S(1)} %subtract_multiply_fusion.12, f32[2,8,72,136]{3,2,1,0:T(8,128)S(1)} %broadcast_multiply_fusion, ...), kind=kLoop, calls=%fused_computation.160 | loop fusion | flops 2036736 | bytes 2820128 | tf_op jit(solution)/shard_map/mul | solution.py:55
  38.5 0.1 slice_multiply_fusion.3
  38.7 0.1 fusion.88
  38.8 1.1 %fusion.85 = f32[2,8,72,136]{3,2,1,0:T(8,128)S(1)} fusion(f32[2,1,72,136]{3,2,1,0:T(8,128)S(1)} %fusion.99, f32[1,8,72,136]{3,2,1,0:T(8,128)S(1)} %get-tuple-element.108, f32[1,8,72,136]{3,2,1,0:T(8,128)S(1)} %get-tuple-element.107, f32[2,7,72,136]{3,2,1,0:T(8,128)S(1)} %fusion.88, f32[2,8,72,136]{3,2,1,0:T(8,128)S(1)} %fusion.84, ...), kind=kLoop, calls=%fused_computation.161 | loop fusion | flops 2036736 | bytes 2820128 | tf_op jit(solution)/shard_map/mul | solution.py:55
  39.9 0.1 slice_multiply_fusion.1
  40.0 0.1 fusion.87
  40.1 1.1 %fusion.86 = f32[2,8,72,136]{3,2,1,0:T(8,128)S(1)} fusion(f32[2,1,72,136]{3,2,1,0:T(8,128)S(1)} %fusion.99, f32[1,8,72,136]{3,2,1,0:T(8,128)S(1)} %get-tuple-element.106, f32[1,8,72,136]{3,2,1,0:T(8,128)S(1)} %get-tuple-element.105, f32[2,7,72,136]{3,2,1,0:T(8,128)S(1)} %fusion.87, f32[2,8,72,136]{3,2,1,0:T(8,128)S(1)} %fusion.85, ...), kind=kLoop, calls=%fused_computation.162 | loop fusion | flops 2036736 | bytes 2820128 | tf_op jit(solution)/shard_map/mul | solution.py:55
  41.2 0.2 slice_multiply_fusion.8
  41.4 0.3 fusion.97
  41.7 0.8 fusion.96
  42.5 5.1 %collective-permute-start.5 = (f32[2,32,128]{2,1,0:T(8,128)S(1)}, f32[2,32,128]{2,1,0:T(8,128)S(1)}, u32[]{:S(2)}, u32[]{:S(2)}) collective-permute-start(f32[2,32,128]{2,1,0:T(8,128)S(1)} %get-tuple-element.126), channel_id=1, source_target_pairs={{8,0},{16,8},{24,16},{32,24},{40,32},{48,40},{56,48},{64,56},{72,6... | collective-permute-start | bytes 98312 | tf_op jit(solution)/shard_map/ppermute | solution.py:268
  47.7 1.9 %collective-permute-start.4 = (f32[2,32,128]{2,1,0:T(8,128)S(1)}, f32[2,32,128]{2,1,0:T(8,128)S(1)}, u32[]{:S(2)}, u32[]{:S(2)}) collective-permute-start(f32[2,32,128]{2,1,0:T(8,128)S(1)} %get-tuple-element.125), channel_id=1, source_target_pairs={{0,8},{8,16},{16,24},{24,32},{32,40},{40,48},{48,56},{56,64},{64,7... | collective-permute-start | bytes 98312 | tf_op jit(solution)/shard_map/ppermute | solution.py:267
  49.6 0.1 fusion.118
  49.7 0.1 fusion.117
  50.0 4.1 %conditional.1 = (f32[16,2,128]{2,0,1:T(8,128)S(1)}) conditional(s32[]{:T(128)} %clamp.3, (s32[3,64]{1,0:T(4,128)S(1)}, s32[]{:T(128)}, f32[48,5,128]{2,1,0:T(8,128)S(1)}) %tuple.83, (s32[3,64]{1,0:T(4,128)S(1)}, s32[]{:T(128)}, f32[48,5,128]{2,1,0:T(8,128)S(1)}) %tuple.84, (s32[3,64]{1,0:T(4,128)S(1)}, s32[]{:T(128)}, ...), branch_computations={%region_0.3_spmd, %region_3.6_spmd, %region_6.9_spmd} | conditional | flops 31477696 | bytes 1797260 | solution.py:410
  50.3 0.6 gather_fusion.1
  50.9 0.6 gather_fusion
  51.5 1.8 %multiply_reduce_fusion.1 = (f32[16,128]{1,0:T(8,128)S(1)}, f32[16,128]{1,0:T(8,128)S(1)}) fusion(f32[16,128]{1,0:T(8,128)S(1)} %bitcast.221, f32[16,128]{1,0:T(8,128)S(1)} %bitcast.226, f32[16,128]{1,0:T(8,128)S(1)} %bitcast.222, f32[16,128]{1,0:T(8,128)S(1)} %bitcast.227, f32[16,128]{1,0:T(8,128)S(1)} %bitcast.219, f32[16,128]{1,0:T(8,128)S(1)} %bitcast.224, ...), kind=kLoop, calls=%fused_computation.19 | loop fusion | flops 7073792 | bytes 98304 | tf_op jit(solution)/shard_map/cond/branch_0_fun/reduce_sum | solution.py:73
  53.3 0.7 iota_compare_fusion.1
  53.9 0.2 fusion.5
  54.1 0.6 copy.27
  54.7 0.8 collective-permute-done.4
  55.6 0.7 pad_maximum_fusion.4.window_ref
  56.3 4.0 %shard_map.150 = (f32[4,2048]{1,0:T(4,128)}, f32[8,38,128]{2,1,0:T(8,128)}) custom-call(f32[2,128,128]{2,1,0:T(8,128)} %pad_maximum_fusion.4.window_ref, s32[1,2048]{1,0:T(1,128)} %fusion.103.rows_ref, s32[1,2048]{1,0:T(1,128)} %get-tuple-element.59.cols_ref, f32[2,2048]{1,0:T(2,128)} %bitcast.180, f32[2,2048]{1,0:T(2,128)} %bitcast.177, ...), custom_call_target="tpu_custom_call" | custom-call | tf_op jit(solution)/shard_map/pallas_call | solution.py:249
  60.3 0.9 fusion.112
  61.2 1.9 %collective-permute-start.7 = (f32[3,38,128]{2,1,0:T(8,128)S(1)}, f32[3,38,128]{2,1,0:T(8,128)S(1)}, u32[]{:S(2)}, u32[]{:S(2)}) collective-permute-start(f32[3,38,128]{2,1,0:T(8,128)S(1)} %get-tuple-element.120), channel_id=1, source_target_pairs={{0,8},{8,16},{16,24},{24,32},{32,40},{40,48},{48,56},{56,64},{64,7... | collective-permute-start | bytes 175112 | tf_op jit(solution)/shard_map/ppermute | solution.py:267
  63.1 0.8 fusion.111
  63.8 10.8 %collective-permute-start.6 = (f32[3,38,128]{2,1,0:T(8,128)S(1)}, f32[3,38,128]{2,1,0:T(8,128)S(1)}, u32[]{:S(2)}, u32[]{:S(2)}) collective-permute-start(f32[3,38,128]{2,1,0:T(8,128)S(1)} %get-tuple-element.119), channel_id=1, source_target_pairs={{8,0},{16,8},{24,16},{32,24},{40,32},{48,40},{56,48},{64,56},{72,6... | collective-permute-start | bytes 175112 | tf_op jit(solution)/shard_map/ppermute | solution.py:268
  74.7 1.8 %collective-permute-done.6 = f32[3,38,128]{2,1,0:T(8,128)S(1)} collective-permute-done((f32[3,38,128]{2,1,0:T(8,128)S(1)}, f32[3,38,128]{2,1,0:T(8,128)S(1)}, u32[]{:S(2)}, u32[]{:S(2)}) %collective-permute-start.6) | collective-permute-done | bytes 58400 | tf_op jit(solution)/shard_map/ppermute | solution.py:268
  76.5 3.4 %collective-permute-start.8 = (f32[3,38,128]{2,1,0:T(8,128)S(1)}, f32[3,38,128]{2,1,0:T(8,128)S(1)}, u32[]{:S(2)}, u32[]{:S(2)}) collective-permute-start(f32[3,38,128]{2,1,0:T(8,128)S(1)} %pad_maximum_fusion.8), channel_id=1, source_target_pairs={{1,0},{2,1},{3,2},{4,3},{5,4},{6,5},{7,6},{128,7},{129,128},{130,1... | collective-permute-start | bytes 175112 | tf_op jit(solution)/shard_map/ppermute | solution.py:268
  79.9 1.8 %collective-permute-done.8 = f32[3,38,128]{2,1,0:T(8,128)S(1)} collective-permute-done((f32[3,38,128]{2,1,0:T(8,128)S(1)}, f32[3,38,128]{2,1,0:T(8,128)S(1)}, u32[]{:S(2)}, u32[]{:S(2)}) %collective-permute-start.8) | collective-permute-done | bytes 58400 | tf_op jit(solution)/shard_map/ppermute | solution.py:268
  81.8 1.9 %collective-permute-start.9 = (f32[3,38,128]{2,1,0:T(8,128)S(1)}, f32[3,38,128]{2,1,0:T(8,128)S(1)}, u32[]{:S(2)}, u32[]{:S(2)}) collective-permute-start(f32[3,38,128]{2,1,0:T(8,128)S(1)} %pad_maximum_fusion.9), channel_id=1, source_target_pairs={{0,1},{1,2},{2,3},{3,4},{4,5},{5,6},{6,7},{7,128},{128,129},{129,1... | collective-permute-start | bytes 175112 | tf_op jit(solution)/shard_map/ppermute | solution.py:267
  83.7 7.3 %collective-permute-done.9 = f32[3,38,128]{2,1,0:T(8,128)S(1)} collective-permute-done((f32[3,38,128]{2,1,0:T(8,128)S(1)}, f32[3,38,128]{2,1,0:T(8,128)S(1)}, u32[]{:S(2)}, u32[]{:S(2)}) %collective-permute-start.9) | collective-permute-done | bytes 58400 | tf_op jit(solution)/shard_map/ppermute | solution.py:267
  91.0 0.7 copy.18
  (90 shorter events, 0.7 us)
Async XLA Ops:
  0.6 16.2 %copy-start.6 = (f32[1,1,2048]{2,1,0:T(1,128)S(1)}, f32[1,1,2048]{2,1,0:T(1,128)}, u32[]{:S(2)}) copy-start(f32[1,1,2048]{2,1,0:T(1,128)} %param.21) | copy-start | bytes 24580
  0.6 16.2 %copy-start.3 = (f32[1,1,2,2048]{3,2,1,0:T(2,128)S(1)}, f32[1,1,2,2048]{3,2,1,0:T(2,128)}, u32[]{:S(2)}) copy-start(f32[1,1,2,2048]{3,2,1,0:T(2,128)} %param.20) | copy-start | bytes 49156
  0.7 16.2 %copy-start.4 = (f32[1,1,2,2048]{3,2,1,0:T(2,128)S(1)}, f32[1,1,2,2048]{3,2,1,0:T(2,128)}, u32[]{:S(2)}) copy-start(f32[1,1,2,2048]{3,2,1,0:T(2,128)} %param.19) | copy-start | bytes 49156
  0.7 13.4 %copy-start.1 = (f32[2,64,128]{2,1,0:T(8,128)S(1)}, f32[2,64,128]{2,1,0:T(8,128)}, u32[]{:S(2)}) copy-start(f32[2,64,128]{2,1,0:T(8,128)} %param.17) | copy-start | bytes 196612
  0.7 13.5 %copy-start.5 = (s32[64,128]{1,0:T(8,128)S(1)}, s32[64,128]{1,0:T(8,128)}, u32[]{:S(2)}) copy-start(s32[64,128]{1,0:T(8,128)} %param.18) | copy-start | bytes 98308
  0.7 13.5 %copy-start.7 = (s32[1,1,2048]{2,1,0:T(1,128)S(1)}, s32[1,1,2048]{2,1,0:T(1,128)}, u32[]{:S(2)}) copy-start(s32[1,1,2048]{2,1,0:T(1,128)} %param.24) | copy-start | bytes 24580
  0.7 14.8 %copy-start.9 = (s32[1,1,3,64]{3,1,2,0:T(1,128)S(1)}, s32[1,1,3,64]{3,1,2,0:T(1,128)}, u32[]{:S(2)}) copy-start(s32[1,1,3,64]{3,1,2,0:T(1,128)} %param.26) | copy-start | bytes 2308
  0.7 15.4 %copy-start.8 = (s32[1,1,8,128]{3,2,1,0:T(8,128)S(1)}, s32[1,1,8,128]{3,2,1,0:T(8,128)}, u32[]{:S(2)}) copy-start(s32[1,1,8,128]{3,2,1,0:T(8,128)} %param.27) | copy-start | bytes 12292
  0.7 15.4 %copy-start.10 = (s32[1,1,8]{2,1,0:T(1,128)S(1)}, s32[1,1,8]{2,1,0:T(1,128)}, u32[]{:S(2)}) copy-start(s32[1,1,8]{2,1,0:T(1,128)} %param.28) | copy-start | bytes 100
  4.0 16.8 %copy-start = (f32[2,8,64,128]{3,2,1,0:T(8,128)S(1)}, f32[2,8,64,128]{3,2,1,0:T(8,128)}, u32[]{:S(2)}) copy-start(f32[2,8,64,128]{3,2,1,0:T(8,128)} %param.16) | copy-start | bytes 1572868
  4.1 16.6 %collective-permute-start.1 = (f32[20480]{0:T(1024)S(1)}, f32[20480]{0:T(1024)S(1)}, u32[]{:S(2)}, u32[]{:S(2)}) collective-permute-start(f32[20480]{0:T(1024)S(1)} %get-tuple-element.142), channel_id=1, source_target_pairs={{8,0},{16,8},{24,16},{32,24},{40,32},{48,40},{56,48},{64,56},{72,6... | collective-permute-start | bytes 245768 | tf_op jit(solution)/shard_map/ppermute | solution.py:268
  12.2 8.5 %collective-permute-start = (f32[20480]{0:T(1024)S(1)}, f32[20480]{0:T(1024)S(1)}, u32[]{:S(2)}, u32[]{:S(2)}) collective-permute-start(f32[20480]{0:T(1024)S(1)} %get-tuple-element.141), channel_id=1, source_target_pairs={{0,8},{8,16},{16,24},{24,32},{32,40},{40,48},{48,56},{56,64},{64,7... | collective-permute-start | bytes 245768 | tf_op jit(solution)/shard_map/ppermute | solution.py:267
  22.0 9.5 %collective-permute-start.3 = (f32[13152]{0:T(1024)S(1)}, f32[13152]{0:T(1024)S(1)}, u32[]{:S(2)}, u32[]{:S(2)}) collective-permute-start(f32[13152]{0:T(1024)S(1)} %get-tuple-element.140), channel_id=1, source_target_pairs={{1,0},{2,1},{3,2},{4,3},{5,4},{6,5},{7,6},{128,7},{129,128},{130,1... | collective-permute-start | bytes 157832 | tf_op jit(solution)/shard_map/ppermute | solution.py:268
  26.2 9.1 %collective-permute-start.2 = (f32[13152]{0:T(1024)S(1)}, f32[13152]{0:T(1024)S(1)}, u32[]{:S(2)}, u32[]{:S(2)}) collective-permute-start(f32[13152]{0:T(1024)S(1)} %get-tuple-element.139), channel_id=1, source_target_pairs={{0,1},{1,2},{2,3},{3,4},{4,5},{5,6},{6,7},{7,128},{128,129},{129,1... | collective-permute-start | bytes 157832 | tf_op jit(solution)/shard_map/ppermute | solution.py:267
  42.5 7.5 %copy-start.2 = (f32[2,8,64,128]{3,2,1,0:T(8,128)}, f32[2,8,64,128]{3,2,1,0:T(8,128)S(1)}, u32[]{:S(2)}) copy-start(f32[2,8,64,128]{3,2,1,0:T(8,128)S(1)} %fusion.96) | copy-start | bytes 1572868
  42.5 12.2 %collective-permute-start.5 = (f32[2,32,128]{2,1,0:T(8,128)S(1)}, f32[2,32,128]{2,1,0:T(8,128)S(1)}, u32[]{:S(2)}, u32[]{:S(2)}) collective-permute-start(f32[2,32,128]{2,1,0:T(8,128)S(1)} %get-tuple-element.126), channel_id=1, source_target_pairs={{8,0},{16,8},{24,16},{32,24},{40,32},{48,40},{56,48},{64,56},{72,6... | collective-permute-start | bytes 98312 | tf_op jit(solution)/shard_map/ppermute | solution.py:268
  47.7 7.9 %collective-permute-start.4 = (f32[2,32,128]{2,1,0:T(8,128)S(1)}, f32[2,32,128]{2,1,0:T(8,128)S(1)}, u32[]{:S(2)}, u32[]{:S(2)}) collective-permute-start(f32[2,32,128]{2,1,0:T(8,128)S(1)} %get-tuple-element.125), channel_id=1, source_target_pairs={{0,8},{8,16},{16,24},{24,32},{32,40},{40,48},{48,56},{56,64},{64,7... | collective-permute-start | bytes 98312 | tf_op jit(solution)/shard_map/ppermute | solution.py:267
  61.2 13.5 %collective-permute-start.7 = (f32[3,38,128]{2,1,0:T(8,128)S(1)}, f32[3,38,128]{2,1,0:T(8,128)S(1)}, u32[]{:S(2)}, u32[]{:S(2)}) collective-permute-start(f32[3,38,128]{2,1,0:T(8,128)S(1)} %get-tuple-element.120), channel_id=1, source_target_pairs={{0,8},{8,16},{16,24},{24,32},{32,40},{40,48},{48,56},{56,64},{64,7... | collective-permute-start | bytes 175112 | tf_op jit(solution)/shard_map/ppermute | solution.py:267
  63.8 12.7 %collective-permute-start.6 = (f32[3,38,128]{2,1,0:T(8,128)S(1)}, f32[3,38,128]{2,1,0:T(8,128)S(1)}, u32[]{:S(2)}, u32[]{:S(2)}) collective-permute-start(f32[3,38,128]{2,1,0:T(8,128)S(1)} %get-tuple-element.119), channel_id=1, source_target_pairs={{8,0},{16,8},{24,16},{32,24},{40,32},{48,40},{56,48},{64,56},{72,6... | collective-permute-start | bytes 175112 | tf_op jit(solution)/shard_map/ppermute | solution.py:268
  76.5 5.3 %collective-permute-start.8 = (f32[3,38,128]{2,1,0:T(8,128)S(1)}, f32[3,38,128]{2,1,0:T(8,128)S(1)}, u32[]{:S(2)}, u32[]{:S(2)}) collective-permute-start(f32[3,38,128]{2,1,0:T(8,128)S(1)} %pad_maximum_fusion.8), channel_id=1, source_target_pairs={{1,0},{2,1},{3,2},{4,3},{5,4},{6,5},{7,6},{128,7},{129,128},{130,1... | collective-permute-start | bytes 175112 | tf_op jit(solution)/shard_map/ppermute | solution.py:268
  81.8 9.2 %collective-permute-start.9 = (f32[3,38,128]{2,1,0:T(8,128)S(1)}, f32[3,38,128]{2,1,0:T(8,128)S(1)}, u32[]{:S(2)}, u32[]{:S(2)}) collective-permute-start(f32[3,38,128]{2,1,0:T(8,128)S(1)} %pad_maximum_fusion.9), channel_id=1, source_target_pairs={{0,1},{1,2},{2,3},{3,4},{4,5},{5,6},{6,7},{7,128},{128,129},{129,1... | collective-permute-start | bytes 175112 | tf_op jit(solution)/shard_map/ppermute | solution.py:267

commit v4 on v3

--- a/solution.py
+++ b/solution.py
@@ -198,7 +198,7 @@
 
 def tail_kernel(
     window_ref, rows_ref, cols_ref, position_ref, velocity_ref, radius_ref, mass_ref, contact_ref,
-    wind_ref, index_ref, fixed_ref, next_ref, out_ref, sample_ref, record_ref, stack_ref,
+    wind_ref, polygon_ref, index_ref, next_ref, out_ref, sample_ref, record_ref, stack_ref,
 ):
     window_rows, window_cols = window_ref.shape[1:]
     floes = rows_ref.shape[1]
@@ -231,33 +231,37 @@
         new_velocity = velocity[axis : axis + 1] + ICE_STEP * total / mass
         next_ref[2 + axis : 3 + axis, :] = new_velocity
         next_ref[axis : axis + 1, :] = position[axis : axis + 1] + ICE_STEP * new_velocity
-    rows = next_ref.shape[0]
+    width = out_ref.shape[1]
     record_ref[...] = jnp.zeros_like(record_ref)
     stack_ref[...] = jnp.zeros_like(stack_ref)
-    record_ref[0:rows, :] = next_ref[...]
+    record_ref[0:4, :] = next_ref[...]
+    record_ref[4:5, :] = radius
+    record_ref[5:6, :] = mass
+    record_ref[6:width, :] = polygon_ref[...]
     record = record_ref[...]
-    out_ref[...] = fixed_ref[...]
     for way in range(index_ref.shape[0]):
         chosen = (
             lax.broadcasted_iota(jnp.int32, (floes, slots), 0) == index_ref[way : way + 1, :]
         ).astype(jnp.bfloat16)
-        out_ref[way, 0:rows, :] = stacked_select(stack_ref, record, chosen)[0:rows]
-
-
-def sample_update_gather(window, rows, cols, position, velocity, radius, mass, contact, wind, index, fixed):
+        out_ref[way] = stacked_select(stack_ref, record, chosen)[0:width]
+
+
+def sample_update_gather(window, rows, cols, position, velocity, radius, mass, contact, wind, polygon, index):
     floes = rows.shape[1]
+    width = 6 + polygon.shape[0]
+    padded = -(-width // 16) * 16
     return pl.pallas_call(
         tail_kernel,
         out_shape=(
             jax.ShapeDtypeStruct((4, floes), jnp.float32),
-            jax.ShapeDtypeStruct(fixed.shape, jnp.float32),
+            jax.ShapeDtypeStruct((index.shape[0], width, index.shape[1]), jnp.float32),
         ),
         scratch_shapes=[
             pltpu.VMEM((3 * window.shape[2], window.shape[1]), jnp.float32),
-            pltpu.VMEM((8, floes), jnp.float32),
-            pltpu.VMEM((24, floes), jnp.float32),
-        ],
-    )(window, rows, cols, position, velocity, radius, mass, contact, wind, index, fixed)
+            pltpu.VMEM((padded, floes), jnp.float32),
+            pltpu.VMEM((3 * padded, floes), jnp.float32),
+        ],
+    )(window, rows, cols, position, velocity, radius, mass, contact, wind, polygon, index)
 
 
 def exchange(low, high, axis):
@@ -373,10 +377,7 @@
     capacity = leaving.shape[1]
     valid_slots = jnp.arange(capacity, dtype=jnp.int32)[None, :] < move_count[0, 0][:, None]
     chosen = jnp.where(valid_slots, leaving, -1)
-    fixed_records = gather_records(
-        jnp.zeros((4, floes), jnp.float32), radius[None], mass[None], floe_polygon[0, 0], chosen
-    )
-    flow, sampled_wind, fixed_records = lax.optimization_barrier((flow, sampled_wind, fixed_records))
+    flow, sampled_wind = lax.optimization_barrier((flow, sampled_wind))
     for substep in range(OSTEPS - 1):
         padded = jnp.pad(flow, ((0, 0), (0, 0), (1, 1), (1, 1)))
         flow = ocean_substep(flow, padded, wet, wind_ext)
@@ -411,7 +412,7 @@
     contact = contact.transpose(1, 0, 2).reshape(2, floes)
     floe_next, outgoing = sample_update_gather(
         near, floe_rows, floe_cols, position, velocity, radius[None], mass[None], contact,
-        sampled_wind, chosen, fixed_records,
+        sampled_wind, floe_polygon[0, 0], chosen,
     )
     from_above, from_below = exchange(outgoing[0:3], outgoing[5:8], "gx")
     heading_left = jnp.stack([from_below[0], outgoing[3], from_above[0]])

time: 92.5 us -> 88.1 us (0.952)
  starting transfers between devices: 41.2 us -> 36.4 us
  Pallas kernels: 9.87 us -> 6.96 us
  waiting for transfers between devices: 14.9 us -> 17.8 us
  other arithmetic: 14.8 us -> 16.6 us
    ppermute x5, starting transfers between devices: 31.6 us -> 25.4 us  [exchange(): from_next = lax.ppermute(low, axis, down)]
    pallas_call x1 -> x0, Pallas kernels: 3.18 us -> none  [gather_records(): pl.pallas_call(gather_kernel, out_shape=jax.ShapeDtypeStruct((index.shape...]
    ppermute x5, waiting for transfers between devices: 11.2 us -> 14.1 us  [exchange(): from_previous = lax.ppermute(high, axis, up)]
    reduce_sum x1, other arithmetic: 1.77 us -> 3.51 us  [pair_forces(): jnp.sum(magnitude * normal_x, axis=1)]
    ppermute x5, starting transfers between devices: 9.6 us -> 10.9 us  [exchange(): from_previous = lax.ppermute(high, axis, up)]
  transfers between devices with their start and end apart: 10 -> 10, of which waited for: 5 -> 5; matrix products, arithmetic and copies ran while one was open for 10% -> 12% of each run, Pallas kernels for 6% -> 3%
where the time goes in v4:
time: 88.1 us; the launch traced here: 88 us
  starting transfers between devices  36.4 us (41%)
  waiting for transfers between devices  17.8 us (20%)
  other arithmetic  16.6 us (19%)
  local copies, waits for them, and re-layouts  7.94 us (9%)
  Pallas kernels  6.96 us (8%)
  between operations  2.02 us (2%)
    ppermute x5, starting transfers between devices, exchange(): from_next = lax.ppermute(low, axis, down)  25.4 us
    ppermute x5, waiting for transfers between devices, exchange(): from_previous = lax.ppermute(high, axis, up)  14.1 us
    ppermute x5, starting transfers between devices, exchange(): from_previous = lax.ppermute(high, axis, up)  10.9 us
    pallas_call x1, Pallas kernels, sample_update_gather(): pl.pallas_call(tail_kernel, out_shape=(jax.ShapeDtypeStruct((4, floes), j...  4.29 us
    mul x4, other arithmetic, ocean_substep(): return (flow + horizontal * lap + vert + turning + surface) * wet[None]  3.99 us
    ppermute x5, waiting for transfers between devices, exchange(): from_next = lax.ppermute(low, axis, down)  3.67 us
    reduce_sum x1, other arithmetic, pair_forces(): jnp.sum(magnitude * normal_x, axis=1)  3.51 us
    pallas_call x1, Pallas kernels, sample_surface(): pl.pallas_call(sample_kernel, out_shape=jax.ShapeDtypeStruct((window.shap...  2.66 us
  transfers between devices with their start and end apart: 10, of which 5 were waited for; matrix products, arithmetic and copies ran while one was open for 12% of the time, Pallas kernels for 3%

profile of v4, /device:TPU:24, one launch (start us, length us, event | category | flops | bytes accessed | tf_op | source)
XLA Modules:
  0.0 88.0 jit_solution(4810221227445382617)
XLA Ops:
  0.7 0.8 pad_maximum_fusion.17
  1.5 0.8 fusion.114
  2.3 0.8 convert_bitcast_fusion
  3.1 1.0 %pad_maximum_fusion.15 = (f32[19,4,128]{2,1,0:T(4,128)S(1)}, f32[19,4,128]{2,1,0:T(4,128)S(1)}) fusion(f32[1,64,128]{2,1,0:T(8,128)S(1)} %convert_bitcast_fusion, f32[2,64,128]{2,1,0:T(8,128)} %param.17, f32[16,64,128]{2,1,0:T(8,128)} %bitcast.162), kind=kLoop, calls=%fused_computation.218 | loop fusion | flops 38912 | bytes 700416 | tf_op jit(solution)/shard_map/slice | solution.py:320
  4.1 7.9 %collective-permute-start.1 = (f32[20480]{0:T(1024)S(1)}, f32[20480]{0:T(1024)S(1)}, u32[]{:S(2)}, u32[]{:S(2)}) collective-permute-start(f32[20480]{0:T(1024)S(1)} %get-tuple-element.140), channel_id=1, source_target_pairs={{8,0},{16,8},{24,16},{32,24},{40,32},{48,40},{56,48},{64,56},{72,6... | collective-permute-start | bytes 245768 | tf_op jit(solution)/shard_map/ppermute | solution.py:272
  12.1 1.9 %collective-permute-start = (f32[20480]{0:T(1024)S(1)}, f32[20480]{0:T(1024)S(1)}, u32[]{:S(2)}, u32[]{:S(2)}) collective-permute-start(f32[20480]{0:T(1024)S(1)} %get-tuple-element.139), channel_id=1, source_target_pairs={{0,8},{8,16},{16,24},{24,32},{32,40},{40,48},{48,56},{56,64},{64,7... | collective-permute-start | bytes 245768 | tf_op jit(solution)/shard_map/ppermute | solution.py:271
  14.1 0.6 and_select_fusion
  15.4 0.6 fusion.103.rows_ref
  16.1 0.7 bitcast_select_fusion.index_ref
  16.8 3.7 %collective-permute-done = f32[20480]{0:T(1024)S(1)} collective-permute-done((f32[20480]{0:T(1024)S(1)}, f32[20480]{0:T(1024)S(1)}, u32[]{:S(2)}, u32[]{:S(2)}) %collective-permute-start) | collective-permute-done | bytes 81952 | tf_op jit(solution)/shard_map/ppermute | solution.py:271
  20.7 0.1 pad_maximum_fusion.1
  20.7 0.2 fusion.110
  21.0 0.4 reshape.568
  21.3 0.4 reshape.571
  21.7 0.1 pad_maximum_fusion.11
  21.8 3.0 %collective-permute-start.3 = (f32[13152]{0:T(1024)S(1)}, f32[13152]{0:T(1024)S(1)}, u32[]{:S(2)}, u32[]{:S(2)}) collective-permute-start(f32[13152]{0:T(1024)S(1)} %get-tuple-element.138), channel_id=1, source_target_pairs={{1,0},{2,1},{3,2},{4,3},{5,4},{6,5},{7,6},{128,7},{129,128},{130,1... | collective-permute-start | bytes 157832 | tf_op jit(solution)/shard_map/ppermute | solution.py:272
  24.8 1.9 %collective-permute-start.2 = (f32[13152]{0:T(1024)S(1)}, f32[13152]{0:T(1024)S(1)}, u32[]{:S(2)}, u32[]{:S(2)}) collective-permute-start(f32[13152]{0:T(1024)S(1)} %get-tuple-element.137), channel_id=1, source_target_pairs={{0,1},{1,2},{2,3},{3,4},{4,5},{5,6},{6,7},{7,128},{128,129},{129,1... | collective-permute-start | bytes 157832 | tf_op jit(solution)/shard_map/ppermute | solution.py:271
  26.8 0.7 pad_maximum_fusion.3.window_ref
  27.5 2.7 %shard_map.148.wind_ref = f32[2,2048]{1,0:T(2,128)} custom-call(f32[2,128,128]{2,1,0:T(8,128)} %pad_maximum_fusion.3.window_ref, s32[1,2048]{1,0:T(1,128)} %fusion.103.rows_ref, s32[1,2048]{1,0:T(1,128)} %get-tuple-element.57.cols_ref), custom_call_target="tpu_custom_call" | custom-call | tf_op jit(solution)/shard_map/pallas_call | solution.py:133
  30.1 0.7 reshape.572
  30.8 3.1 %collective-permute-done.2 = f32[13152]{0:T(1024)S(1)} collective-permute-done((f32[13152]{0:T(1024)S(1)}, f32[13152]{0:T(1024)S(1)}, u32[]{:S(2)}, u32[]{:S(2)}) %collective-permute-start.2) | collective-permute-done | bytes 52640 | tf_op jit(solution)/shard_map/ppermute | solution.py:271
  33.9 0.7 reshape.570
  34.6 0.1 fusion.99
  34.8 0.7 pad_maximum_fusion
  35.5 0.1 maximum_bitcast_fusion
  35.6 0.1 slice.618
  35.8 0.1 broadcast_multiply_fusion
  35.9 0.1 slice_multiply_fusion.5
  36.0 0.1 subtract_multiply_fusion.12
  36.2 1.1 %fusion.84 = f32[2,8,72,136]{3,2,1,0:T(8,128)S(1)} fusion(f32[2,1,72,136]{3,2,1,0:T(8,128)S(1)} %fusion.99, f32[1,8,72,136]{3,2,1,0:T(8,128)S(1)} %get-tuple-element.108, f32[1,8,72,136]{3,2,1,0:T(8,128)S(1)} %get-tuple-element.107, f32[2,7,72,136]{3,2,1,0:T(8,128)S(1)} %subtract_multiply_fusion.12, f32[2,8,72,136]{3,2,1,0:T(8,128)S(1)} %broadcast_multiply_fusion, ...), kind=kLoop, calls=%fused_computation.160 | loop fusion | flops 2036736 | bytes 2820128 | tf_op jit(solution)/shard_map/mul | solution.py:55
  37.2 0.1 slice_multiply_fusion.3
  37.3 0.1 fusion.88
  37.5 1.1 %fusion.85 = f32[2,8,72,136]{3,2,1,0:T(8,128)S(1)} fusion(f32[2,1,72,136]{3,2,1,0:T(8,128)S(1)} %fusion.99, f32[1,8,72,136]{3,2,1,0:T(8,128)S(1)} %get-tuple-element.106, f32[1,8,72,136]{3,2,1,0:T(8,128)S(1)} %get-tuple-element.105, f32[2,7,72,136]{3,2,1,0:T(8,128)S(1)} %fusion.88, f32[2,8,72,136]{3,2,1,0:T(8,128)S(1)} %fusion.84, ...), kind=kLoop, calls=%fused_computation.161 | loop fusion | flops 2036736 | bytes 2820128 | tf_op jit(solution)/shard_map/mul | solution.py:55
  38.5 0.1 slice_multiply_fusion.1
  38.7 0.1 fusion.87
  38.8 1.1 %fusion.86 = f32[2,8,72,136]{3,2,1,0:T(8,128)S(1)} fusion(f32[2,1,72,136]{3,2,1,0:T(8,128)S(1)} %fusion.99, f32[1,8,72,136]{3,2,1,0:T(8,128)S(1)} %get-tuple-element.104, f32[1,8,72,136]{3,2,1,0:T(8,128)S(1)} %get-tuple-element.103, f32[2,7,72,136]{3,2,1,0:T(8,128)S(1)} %fusion.87, f32[2,8,72,136]{3,2,1,0:T(8,128)S(1)} %fusion.85, ...), kind=kLoop, calls=%fused_computation.162 | loop fusion | flops 2036736 | bytes 2820128 | tf_op jit(solution)/shard_map/mul | solution.py:55
  39.9 0.2 slice_multiply_fusion.8
  40.1 0.3 fusion.97
  40.4 0.8 fusion.96
  41.2 2.6 %collective-permute-start.5 = (f32[2,32,128]{2,1,0:T(8,128)S(1)}, f32[2,32,128]{2,1,0:T(8,128)S(1)}, u32[]{:S(2)}, u32[]{:S(2)}) collective-permute-start(f32[2,32,128]{2,1,0:T(8,128)S(1)} %get-tuple-element.124), channel_id=1, source_target_pairs={{8,0},{16,8},{24,16},{32,24},{40,32},{48,40},{56,48},{64,56},{72,6... | collective-permute-start | bytes 98312 | tf_op jit(solution)/shard_map/ppermute | solution.py:272
  43.8 3.3 %collective-permute-start.4 = (f32[2,32,128]{2,1,0:T(8,128)S(1)}, f32[2,32,128]{2,1,0:T(8,128)S(1)}, u32[]{:S(2)}, u32[]{:S(2)}) collective-permute-start(f32[2,32,128]{2,1,0:T(8,128)S(1)} %get-tuple-element.123), channel_id=1, source_target_pairs={{0,8},{8,16},{16,24},{24,32},{32,40},{40,48},{48,56},{56,64},{64,7... | collective-permute-start | bytes 98312 | tf_op jit(solution)/shard_map/ppermute | solution.py:271
  47.1 0.1 fusion.118
  47.2 0.1 fusion.117
  47.5 5.9 %conditional.1 = (f32[16,2,128]{2,0,1:T(8,128)S(1)}) conditional(s32[]{:T(128)} %clamp.3, (s32[3,64]{1,0:T(4,128)S(1)}, s32[]{:T(128)}, f32[48,5,128]{2,1,0:T(8,128)S(1)}) %tuple.83, (s32[3,64]{1,0:T(4,128)S(1)}, s32[]{:T(128)}, f32[48,5,128]{2,1,0:T(8,128)S(1)}) %tuple.84, (s32[3,64]{1,0:T(4,128)S(1)}, s32[]{:T(128)}, ...), branch_computations={%region_0.3_spmd, %region_3.6_spmd, %region_6.9_spmd} | conditional | flops 31477696 | bytes 1797260 | solution.py:411
  47.5 0.6 gather_fusion.3
  48.1 0.1 fusion.107
  48.2 0.6 gather_fusion.2
  48.8 0.1 fusion.106
  48.9 3.5 %multiply_reduce_fusion.3 = (f32[32,128]{1,0:T(8,128)S(1)}, f32[32,128]{1,0:T(8,128)S(1)}) fusion(f32[32,128]{1,0:T(8,128)S(1)} %bitcast.207, f32[32,128]{1,0:T(8,128)S(1)} %bitcast.212, f32[32,128]{1,0:T(8,128)S(1)} %bitcast.208, f32[32,128]{1,0:T(8,128)S(1)} %bitcast.213, f32[32,128]{1,0:T(8,128)S(1)} %bitcast.205, f32[32,128]{1,0:T(8,128)S(1)} %bitcast.210, ...), kind=kLoop, calls=%fused_computation.57 | loop fusion | flops 14147584 | bytes 196608 | tf_op jit(solution)/shard_map/cond/branch_1_fun/reduce_sum | solution.py:73
  52.4 0.7 iota_compare_fusion.3
  53.1 0.2 fusion.25
  53.3 0.6 copy.27
  54.0 0.7 pad_maximum_fusion.4.window_ref
  54.6 4.3 %shard_map.149 = (f32[4,2048]{1,0:T(4,128)}, f32[8,38,128]{2,1,0:T(8,128)}) custom-call(f32[2,128,128]{2,1,0:T(8,128)} %pad_maximum_fusion.4.window_ref, s32[1,2048]{1,0:T(1,128)} %fusion.103.rows_ref, s32[1,2048]{1,0:T(1,128)} %get-tuple-element.57.cols_ref, f32[2,2048]{1,0:T(2,128)} %bitcast.180, f32[2,2048]{1,0:T(2,128)} %bitcast.177, ...), custom_call_target="tpu_custom_call" | custom-call | tf_op jit(solution)/shard_map/pallas_call | solution.py:253
  58.9 0.9 fusion.112
  59.8 1.9 %collective-permute-start.7 = (f32[3,38,128]{2,1,0:T(8,128)S(1)}, f32[3,38,128]{2,1,0:T(8,128)S(1)}, u32[]{:S(2)}, u32[]{:S(2)}) collective-permute-start(f32[3,38,128]{2,1,0:T(8,128)S(1)} %get-tuple-element.118), channel_id=1, source_target_pairs={{0,8},{8,16},{16,24},{24,32},{32,40},{40,48},{48,56},{56,64},{64,7... | collective-permute-start | bytes 175112 | tf_op jit(solution)/shard_map/ppermute | solution.py:271
  61.7 0.8 fusion.111
  62.5 6.0 %collective-permute-start.6 = (f32[3,38,128]{2,1,0:T(8,128)S(1)}, f32[3,38,128]{2,1,0:T(8,128)S(1)}, u32[]{:S(2)}, u32[]{:S(2)}) collective-permute-start(f32[3,38,128]{2,1,0:T(8,128)S(1)} %get-tuple-element.117), channel_id=1, source_target_pairs={{8,0},{16,8},{24,16},{32,24},{40,32},{48,40},{56,48},{64,56},{72,6... | collective-permute-start | bytes 175112 | tf_op jit(solution)/shard_map/ppermute | solution.py:272
  68.5 1.8 %collective-permute-done.6 = f32[3,38,128]{2,1,0:T(8,128)S(1)} collective-permute-done((f32[3,38,128]{2,1,0:T(8,128)S(1)}, f32[3,38,128]{2,1,0:T(8,128)S(1)}, u32[]{:S(2)}, u32[]{:S(2)}) %collective-permute-start.6) | collective-permute-done | bytes 58400 | tf_op jit(solution)/shard_map/ppermute | solution.py:272
  70.4 5.8 %collective-permute-start.8 = (f32[3,38,128]{2,1,0:T(8,128)S(1)}, f32[3,38,128]{2,1,0:T(8,128)S(1)}, u32[]{:S(2)}, u32[]{:S(2)}) collective-permute-start(f32[3,38,128]{2,1,0:T(8,128)S(1)} %pad_maximum_fusion.8), channel_id=1, source_target_pairs={{1,0},{2,1},{3,2},{4,3},{5,4},{6,5},{7,6},{128,7},{129,128},{130,1... | collective-permute-start | bytes 175112 | tf_op jit(solution)/shard_map/ppermute | solution.py:272
  76.2 1.8 %collective-permute-done.8 = f32[3,38,128]{2,1,0:T(8,128)S(1)} collective-permute-done((f32[3,38,128]{2,1,0:T(8,128)S(1)}, f32[3,38,128]{2,1,0:T(8,128)S(1)}, u32[]{:S(2)}, u32[]{:S(2)}) %collective-permute-start.8) | collective-permute-done | bytes 58400 | tf_op jit(solution)/shard_map/ppermute | solution.py:272
  78.1 1.9 %collective-permute-start.9 = (f32[3,38,128]{2,1,0:T(8,128)S(1)}, f32[3,38,128]{2,1,0:T(8,128)S(1)}, u32[]{:S(2)}, u32[]{:S(2)}) collective-permute-start(f32[3,38,128]{2,1,0:T(8,128)S(1)} %pad_maximum_fusion.9), channel_id=1, source_target_pairs={{0,1},{1,2},{2,3},{3,4},{4,5},{5,6},{6,7},{7,128},{128,129},{129,1... | collective-permute-start | bytes 175112 | tf_op jit(solution)/shard_map/ppermute | solution.py:271
  80.0 7.3 %collective-permute-done.9 = f32[3,38,128]{2,1,0:T(8,128)S(1)} collective-permute-done((f32[3,38,128]{2,1,0:T(8,128)S(1)}, f32[3,38,128]{2,1,0:T(8,128)S(1)}, u32[]{:S(2)}, u32[]{:S(2)}) %collective-permute-start.9) | collective-permute-done | bytes 58400 | tf_op jit(solution)/shard_map/ppermute | solution.py:271
  87.3 0.7 copy.18
  (88 shorter events, 0.6 us)
Async XLA Ops:
  0.6 16.1 %copy-start.6 = (f32[1,1,2048]{2,1,0:T(1,128)S(1)}, f32[1,1,2048]{2,1,0:T(1,128)}, u32[]{:S(2)}) copy-start(f32[1,1,2048]{2,1,0:T(1,128)} %param.21) | copy-start | bytes 24580
  0.6 16.1 %copy-start.3 = (f32[1,1,2,2048]{3,2,1,0:T(2,128)S(1)}, f32[1,1,2,2048]{3,2,1,0:T(2,128)}, u32[]{:S(2)}) copy-start(f32[1,1,2,2048]{3,2,1,0:T(2,128)} %param.20) | copy-start | bytes 49156
  0.7 16.1 %copy-start.4 = (f32[1,1,2,2048]{3,2,1,0:T(2,128)S(1)}, f32[1,1,2,2048]{3,2,1,0:T(2,128)}, u32[]{:S(2)}) copy-start(f32[1,1,2,2048]{3,2,1,0:T(2,128)} %param.19) | copy-start | bytes 49156
  0.7 13.4 %copy-start.1 = (f32[2,64,128]{2,1,0:T(8,128)S(1)}, f32[2,64,128]{2,1,0:T(8,128)}, u32[]{:S(2)}) copy-start(f32[2,64,128]{2,1,0:T(8,128)} %param.17) | copy-start | bytes 196612
  0.7 13.4 %copy-start.5 = (s32[64,128]{1,0:T(8,128)S(1)}, s32[64,128]{1,0:T(8,128)}, u32[]{:S(2)}) copy-start(s32[64,128]{1,0:T(8,128)} %param.18) | copy-start | bytes 98308
  0.7 13.4 %copy-start.7 = (s32[1,1,2048]{2,1,0:T(1,128)S(1)}, s32[1,1,2048]{2,1,0:T(1,128)}, u32[]{:S(2)}) copy-start(s32[1,1,2048]{2,1,0:T(1,128)} %param.24) | copy-start | bytes 24580
  0.7 14.7 %copy-start.9 = (s32[1,1,3,64]{3,1,2,0:T(1,128)S(1)}, s32[1,1,3,64]{3,1,2,0:T(1,128)}, u32[]{:S(2)}) copy-start(s32[1,1,3,64]{3,1,2,0:T(1,128)} %param.26) | copy-start | bytes 2308
  0.7 15.3 %copy-start.8 = (s32[1,1,8,128]{3,2,1,0:T(8,128)S(1)}, s32[1,1,8,128]{3,2,1,0:T(8,128)}, u32[]{:S(2)}) copy-start(s32[1,1,8,128]{3,2,1,0:T(8,128)} %param.27) | copy-start | bytes 12292
  0.7 15.3 %copy-start.10 = (s32[1,1,8]{2,1,0:T(1,128)S(1)}, s32[1,1,8]{2,1,0:T(1,128)}, u32[]{:S(2)}) copy-start(s32[1,1,8]{2,1,0:T(1,128)} %param.28) | copy-start | bytes 100
  3.1 17.6 %copy-start = (f32[2,8,64,128]{3,2,1,0:T(8,128)S(1)}, f32[2,8,64,128]{3,2,1,0:T(8,128)}, u32[]{:S(2)}) copy-start(f32[2,8,64,128]{3,2,1,0:T(8,128)} %param.16) | copy-start | bytes 1572868
  4.1 12.6 %collective-permute-start.1 = (f32[20480]{0:T(1024)S(1)}, f32[20480]{0:T(1024)S(1)}, u32[]{:S(2)}, u32[]{:S(2)}) collective-permute-start(f32[20480]{0:T(1024)S(1)} %get-tuple-element.140), channel_id=1, source_target_pairs={{8,0},{16,8},{24,16},{32,24},{40,32},{48,40},{56,48},{64,56},{72,6... | collective-permute-start | bytes 245768 | tf_op jit(solution)/shard_map/ppermute | solution.py:272
  12.1 8.4 %collective-permute-start = (f32[20480]{0:T(1024)S(1)}, f32[20480]{0:T(1024)S(1)}, u32[]{:S(2)}, u32[]{:S(2)}) collective-permute-start(f32[20480]{0:T(1024)S(1)} %get-tuple-element.139), channel_id=1, source_target_pairs={{0,8},{8,16},{16,24},{24,32},{32,40},{40,48},{48,56},{56,64},{64,7... | collective-permute-start | bytes 245768 | tf_op jit(solution)/shard_map/ppermute | solution.py:271
  21.8 8.3 %collective-permute-start.3 = (f32[13152]{0:T(1024)S(1)}, f32[13152]{0:T(1024)S(1)}, u32[]{:S(2)}, u32[]{:S(2)}) collective-permute-start(f32[13152]{0:T(1024)S(1)} %get-tuple-element.138), channel_id=1, source_target_pairs={{1,0},{2,1},{3,2},{4,3},{5,4},{6,5},{7,6},{128,7},{129,128},{130,1... | collective-permute-start | bytes 157832 | tf_op jit(solution)/shard_map/ppermute | solution.py:272
  24.8 9.1 %collective-permute-start.2 = (f32[13152]{0:T(1024)S(1)}, f32[13152]{0:T(1024)S(1)}, u32[]{:S(2)}, u32[]{:S(2)}) collective-permute-start(f32[13152]{0:T(1024)S(1)} %get-tuple-element.137), channel_id=1, source_target_pairs={{0,1},{1,2},{2,3},{3,4},{4,5},{5,6},{6,7},{7,128},{128,129},{129,1... | collective-permute-start | bytes 157832 | tf_op jit(solution)/shard_map/ppermute | solution.py:271
  41.2 6.3 %copy-start.2 = (f32[2,8,64,128]{3,2,1,0:T(8,128)}, f32[2,8,64,128]{3,2,1,0:T(8,128)S(1)}, u32[]{:S(2)}) copy-start(f32[2,8,64,128]{3,2,1,0:T(8,128)S(1)} %fusion.96) | copy-start | bytes 1572868
  41.2 12.8 %collective-permute-start.5 = (f32[2,32,128]{2,1,0:T(8,128)S(1)}, f32[2,32,128]{2,1,0:T(8,128)S(1)}, u32[]{:S(2)}, u32[]{:S(2)}) collective-permute-start(f32[2,32,128]{2,1,0:T(8,128)S(1)} %get-tuple-element.124), channel_id=1, source_target_pairs={{8,0},{16,8},{24,16},{32,24},{40,32},{48,40},{56,48},{64,56},{72,6... | collective-permute-start | bytes 98312 | tf_op jit(solution)/shard_map/ppermute | solution.py:272
  43.8 10.2 %collective-permute-start.4 = (f32[2,32,128]{2,1,0:T(8,128)S(1)}, f32[2,32,128]{2,1,0:T(8,128)S(1)}, u32[]{:S(2)}, u32[]{:S(2)}) collective-permute-start(f32[2,32,128]{2,1,0:T(8,128)S(1)} %get-tuple-element.123), channel_id=1, source_target_pairs={{0,8},{8,16},{16,24},{24,32},{32,40},{40,48},{48,56},{56,64},{64,7... | collective-permute-start | bytes 98312 | tf_op jit(solution)/shard_map/ppermute | solution.py:271
  59.8 8.7 %collective-permute-start.7 = (f32[3,38,128]{2,1,0:T(8,128)S(1)}, f32[3,38,128]{2,1,0:T(8,128)S(1)}, u32[]{:S(2)}, u32[]{:S(2)}) collective-permute-start(f32[3,38,128]{2,1,0:T(8,128)S(1)} %get-tuple-element.118), channel_id=1, source_target_pairs={{0,8},{8,16},{16,24},{24,32},{32,40},{40,48},{48,56},{56,64},{64,7... | collective-permute-start | bytes 175112 | tf_op jit(solution)/shard_map/ppermute | solution.py:271
  62.5 7.9 %collective-permute-start.6 = (f32[3,38,128]{2,1,0:T(8,128)S(1)}, f32[3,38,128]{2,1,0:T(8,128)S(1)}, u32[]{:S(2)}, u32[]{:S(2)}) collective-permute-start(f32[3,38,128]{2,1,0:T(8,128)S(1)} %get-tuple-element.117), channel_id=1, source_target_pairs={{8,0},{16,8},{24,16},{32,24},{40,32},{48,40},{56,48},{64,56},{72,6... | collective-permute-start | bytes 175112 | tf_op jit(solution)/shard_map/ppermute | solution.py:272
  70.4 7.7 %collective-permute-start.8 = (f32[3,38,128]{2,1,0:T(8,128)S(1)}, f32[3,38,128]{2,1,0:T(8,128)S(1)}, u32[]{:S(2)}, u32[]{:S(2)}) collective-permute-start(f32[3,38,128]{2,1,0:T(8,128)S(1)} %pad_maximum_fusion.8), channel_id=1, source_target_pairs={{1,0},{2,1},{3,2},{4,3},{5,4},{6,5},{7,6},{128,7},{129,128},{130,1... | collective-permute-start | bytes 175112 | tf_op jit(solution)/shard_map/ppermute | solution.py:272
  78.1 9.2 %collective-permute-start.9 = (f32[3,38,128]{2,1,0:T(8,128)S(1)}, f32[3,38,128]{2,1,0:T(8,128)S(1)}, u32[]{:S(2)}, u32[]{:S(2)}) collective-permute-start(f32[3,38,128]{2,1,0:T(8,128)S(1)} %pad_maximum_fusion.9), channel_id=1, source_target_pairs={{0,1},{1,2},{2,3},{3,4},{4,5},{5,6},{6,7},{7,128},{128,129},{129,1... | collective-permute-start | bytes 175112 | tf_op jit(solution)/shard_map/ppermute | solution.py:271

commit v5 on v4

--- a/solution.py
+++ b/solution.py
@@ -313,11 +313,24 @@
     channels = fields.shape[0]
     row_strip = channels * halo * cols_here
     margin = rows_here // 2
+    def strip(rows):
+        return jnp.concatenate(
+            [
+                ocean_velocity[:, :, rows].reshape(-1),
+                wind_stress[:, rows].reshape(-1),
+                level_counts[rows].astype(jnp.float32).reshape(-1),
+            ]
+        )
+
     low = jnp.concatenate(
-        [fields[:, :halo].reshape(-1), edge.reshape(-1), wind_stress[:, :margin].reshape(-1)]
+        [strip(slice(0, halo)), edge.reshape(-1), wind_stress[:, :margin].reshape(-1)]
     )
     high = jnp.concatenate(
-        [fields[:, -halo:].reshape(-1), edge.reshape(-1), wind_stress[:, -margin:].reshape(-1)]
+        [
+            strip(slice(rows_here - halo, rows_here)),
+            edge.reshape(-1),
+            wind_stress[:, -margin:].reshape(-1),
+        ]
     )
     above, below = exchange(low, high, "gx")
     wind_strip = (2, margin, cols_here)

time: 88.1 us -> 90.8 us (1.031); the launches traced: 88 us -> 91.7 us
  waiting for transfers between devices: 17.8 us -> 14.7 us
  starting transfers between devices: 36.4 us -> 39.4 us
  other arithmetic: 16.6 us -> 18.6 us
  local copies, waits for them, and re-layouts: 7.94 us -> 9.63 us
    ppermute x5, starting transfers between devices: 25.4 us -> 29.8 us  [exchange(): from_next = lax.ppermute(low, axis, down)]
    ppermute x5, waiting for transfers between devices: 14.1 us -> 11 us  [exchange(): from_previous = lax.ppermute(high, axis, up)]
    slice x0 -> x2, local copies, waits for them, and re-layouts: none -> 1.7 us  [the longest x1 0.88 us: strip(): ocean_velocity[:, :, rows].reshape(-1)]
    ppermute x5, starting transfers between devices: 10.9 us -> 9.6 us  [exchange(): from_previous = lax.ppermute(high, axis, up)]
    slice x1 -> x0, other arithmetic: 0.98 us -> none  [shards(): fields[:, -halo:].reshape(-1)]
  transfers between devices with their start and end apart: 10 -> 10, of which waited for: 5 -> 5; matrix products, arithmetic and copies ran while one was open for 12% -> 15% of each run, Pallas kernels for 3% -> 3%
where the time goes in v5:
time: 90.8 us; the launch traced here: 91.7 us
  starting transfers between devices  39.4 us (43%)
  other arithmetic  18.6 us (20%)
  waiting for transfers between devices  14.7 us (16%)
  local copies, waits for them, and re-layouts  9.63 us (11%)
  Pallas kernels  6.97 us (8%)
  between operations  2.02 us (2%)
    ppermute x5, starting transfers between devices, exchange(): from_next = lax.ppermute(low, axis, down)  29.8 us
    ppermute x5, waiting for transfers between devices, exchange(): from_previous = lax.ppermute(high, axis, up)  11 us
    ppermute x5, starting transfers between devices, exchange(): from_previous = lax.ppermute(high, axis, up)  9.6 us
    pallas_call x1, Pallas kernels, sample_update_gather(): pl.pallas_call(tail_kernel, out_shape=(jax.ShapeDtypeStruct((4, floes), j...  4.31 us
    mul x4, other arithmetic, ocean_substep(): return (flow + horizontal * lap + vert + turning + surface) * wet[None]  3.99 us
    ppermute x5, waiting for transfers between devices, exchange(): from_next = lax.ppermute(low, axis, down)  3.67 us
    reduce_sum x1, other arithmetic, pair_forces(): jnp.sum(magnitude * normal_x, axis=1)  3.51 us
    pallas_call x1, Pallas kernels, sample_surface(): pl.pallas_call(sample_kernel, out_shape=jax.ShapeDtypeStruct((window.shap...  2.66 us
  transfers between devices with their start and end apart: 10, of which 5 were waited for; matrix products, arithmetic and copies ran while one was open for 15% of the time, Pallas kernels for 3%

profile of v5, /device:TPU:24, one launch (start us, length us, event | category | flops | bytes accessed | tf_op | source)
XLA Modules:
  0.0 91.7 jit_solution(2695903122281436602)
XLA Ops:
  0.7 0.8 fusion.114
  1.5 0.8 fusion.113
  2.3 0.9 fusion.109
  3.2 0.7 pad_maximum_fusion.12
  4.0 0.7 constant_dynamic-update-slice_fusion.22
  4.7 7.9 %collective-permute-start.1 = (f32[20480]{0:T(1024)S(1)}, f32[20480]{0:T(1024)S(1)}, u32[]{:S(2)}, u32[]{:S(2)}) collective-permute-start(f32[20480]{0:T(1024)S(1)} %constant_dynamic-update-slice_fusion.19), channel_id=1, source_target_pairs={{8,0},{16,8},{24,16},{32,24},{40,32},{48,40},{56,48},{64,56},{72,6... | collective-permute-start | bytes 245768 | tf_op jit(solution)/shard_map/ppermute | solution.py:272
  12.7 1.9 %collective-permute-start = (f32[20480]{0:T(1024)S(1)}, f32[20480]{0:T(1024)S(1)}, u32[]{:S(2)}, u32[]{:S(2)}) collective-permute-start(f32[20480]{0:T(1024)S(1)} %constant_dynamic-update-slice_fusion.18), channel_id=1, source_target_pairs={{0,8},{8,16},{16,24},{24,32},{32,40},{40,48},{48,56},{56,64},{64,7... | collective-permute-start | bytes 245768 | tf_op jit(solution)/shard_map/ppermute | solution.py:271
  14.6 0.8 convert_bitcast_fusion
  15.4 0.8 multiply_bitcast_fusion
  16.2 0.8 fusion.98
  17.0 1.3 %and_select_fusion = (s32[1,2048]{1,0:T(1,128)}, s32[1,2048]{1,0:T(1,128)S(1)}) fusion(s32[1,1,2048]{2,1,0:T(1,128)} %param.24), kind=kLoop, calls=%fused_computation.235 | loop fusion | flops 22528 | bytes 24576 | tf_op jit(solution)/shard_map/jit(remainder)/select_n | solution.py:387
  19.0 0.6 fusion.101.rows_ref
  19.7 0.7 bitcast_select_fusion.index_ref
  20.4 0.7 collective-permute-done
  21.3 0.2 fusion.108
  21.6 0.4 reshape.584
  22.0 0.4 reshape.587
  22.3 0.1 pad_maximum_fusion.9
  22.4 3.5 %collective-permute-start.3 = (f32[13152]{0:T(1024)S(1)}, f32[13152]{0:T(1024)S(1)}, u32[]{:S(2)}, u32[]{:S(2)}) collective-permute-start(f32[13152]{0:T(1024)S(1)} %get-tuple-element.140), channel_id=1, source_target_pairs={{1,0},{2,1},{3,2},{4,3},{5,4},{6,5},{7,6},{128,7},{129,128},{130,1... | collective-permute-start | bytes 157832 | tf_op jit(solution)/shard_map/ppermute | solution.py:272
  25.9 1.9 %collective-permute-start.2 = (f32[13152]{0:T(1024)S(1)}, f32[13152]{0:T(1024)S(1)}, u32[]{:S(2)}, u32[]{:S(2)}) collective-permute-start(f32[13152]{0:T(1024)S(1)} %get-tuple-element.139), channel_id=1, source_target_pairs={{0,1},{1,2},{2,3},{3,4},{4,5},{5,6},{6,7},{7,128},{128,129},{129,1... | collective-permute-start | bytes 157832 | tf_op jit(solution)/shard_map/ppermute | solution.py:271
  27.9 0.7 pad_maximum_fusion.3.window_ref
  28.5 2.7 %shard_map.148.wind_ref = f32[2,2048]{1,0:T(2,128)} custom-call(f32[2,128,128]{2,1,0:T(8,128)} %pad_maximum_fusion.3.window_ref, s32[1,2048]{1,0:T(1,128)} %fusion.101.rows_ref, s32[1,2048]{1,0:T(1,128)} %get-tuple-element.57.cols_ref), custom_call_target="tpu_custom_call" | custom-call | tf_op jit(solution)/shard_map/pallas_call | solution.py:133
  31.2 0.7 reshape.588
  31.9 3.1 %collective-permute-done.2 = f32[13152]{0:T(1024)S(1)} collective-permute-done((f32[13152]{0:T(1024)S(1)}, f32[13152]{0:T(1024)S(1)}, u32[]{:S(2)}, u32[]{:S(2)}) %collective-permute-start.2) | collective-permute-done | bytes 52640 | tf_op jit(solution)/shard_map/ppermute | solution.py:271
  35.0 0.7 reshape.586
  35.7 0.1 fusion.99
  35.9 0.7 pad_maximum_fusion
  36.6 0.1 maximum_bitcast_fusion
  36.9 0.1 broadcast_multiply_fusion
  37.0 0.1 slice_multiply_fusion.5
  37.1 0.1 subtract_multiply_fusion.12
  37.2 1.1 %fusion.84 = f32[2,8,72,136]{3,2,1,0:T(8,128)S(1)} fusion(f32[2,1,72,136]{3,2,1,0:T(8,128)S(1)} %fusion.99, f32[1,8,72,136]{3,2,1,0:T(8,128)S(1)} %get-tuple-element.108, f32[1,8,72,136]{3,2,1,0:T(8,128)S(1)} %get-tuple-element.107, f32[2,7,72,136]{3,2,1,0:T(8,128)S(1)} %subtract_multiply_fusion.12, f32[2,8,72,136]{3,2,1,0:T(8,128)S(1)} %broadcast_multiply_fusion, ...), kind=kLoop, calls=%fused_computation.160 | loop fusion | flops 2036736 | bytes 2820128 | tf_op jit(solution)/shard_map/mul | solution.py:55
  38.3 0.1 slice_multiply_fusion.3
  38.4 0.1 fusion.88
  38.5 1.1 %fusion.85 = f32[2,8,72,136]{3,2,1,0:T(8,128)S(1)} fusion(f32[2,1,72,136]{3,2,1,0:T(8,128)S(1)} %fusion.99, f32[1,8,72,136]{3,2,1,0:T(8,128)S(1)} %get-tuple-element.106, f32[1,8,72,136]{3,2,1,0:T(8,128)S(1)} %get-tuple-element.105, f32[2,7,72,136]{3,2,1,0:T(8,128)S(1)} %fusion.88, f32[2,8,72,136]{3,2,1,0:T(8,128)S(1)} %fusion.84, ...), kind=kLoop, calls=%fused_computation.161 | loop fusion | flops 2036736 | bytes 2820128 | tf_op jit(solution)/shard_map/mul | solution.py:55
  39.6 0.1 slice_multiply_fusion.1
  39.7 0.1 fusion.87
  39.9 1.1 %fusion.86 = f32[2,8,72,136]{3,2,1,0:T(8,128)S(1)} fusion(f32[2,1,72,136]{3,2,1,0:T(8,128)S(1)} %fusion.99, f32[1,8,72,136]{3,2,1,0:T(8,128)S(1)} %get-tuple-element.104, f32[1,8,72,136]{3,2,1,0:T(8,128)S(1)} %get-tuple-element.103, f32[2,7,72,136]{3,2,1,0:T(8,128)S(1)} %fusion.87, f32[2,8,72,136]{3,2,1,0:T(8,128)S(1)} %fusion.85, ...), kind=kLoop, calls=%fused_computation.162 | loop fusion | flops 2036736 | bytes 2820128 | tf_op jit(solution)/shard_map/mul | solution.py:55
  40.9 0.2 slice_multiply_fusion.8
  41.1 0.3 fusion.97
  41.5 0.8 fusion.96
  42.3 5.1 %collective-permute-start.5 = (f32[2,32,128]{2,1,0:T(8,128)S(1)}, f32[2,32,128]{2,1,0:T(8,128)S(1)}, u32[]{:S(2)}, u32[]{:S(2)}) collective-permute-start(f32[2,32,128]{2,1,0:T(8,128)S(1)} %get-tuple-element.124), channel_id=1, source_target_pairs={{8,0},{16,8},{24,16},{32,24},{40,32},{48,40},{56,48},{64,56},{72,6... | collective-permute-start | bytes 98312 | tf_op jit(solution)/shard_map/ppermute | solution.py:272
  47.4 1.9 %collective-permute-start.4 = (f32[2,32,128]{2,1,0:T(8,128)S(1)}, f32[2,32,128]{2,1,0:T(8,128)S(1)}, u32[]{:S(2)}, u32[]{:S(2)}) collective-permute-start(f32[2,32,128]{2,1,0:T(8,128)S(1)} %get-tuple-element.123), channel_id=1, source_target_pairs={{0,8},{8,16},{16,24},{24,32},{32,40},{40,48},{48,56},{56,64},{64,7... | collective-permute-start | bytes 98312 | tf_op jit(solution)/shard_map/ppermute | solution.py:271
  49.4 0.1 fusion.118
  49.5 0.1 fusion.117
  49.8 5.9 %conditional.1 = (f32[16,2,128]{2,0,1:T(8,128)S(1)}) conditional(s32[]{:T(128)} %clamp.3, (s32[3,64]{1,0:T(4,128)S(1)}, s32[]{:T(128)}, f32[48,5,128]{2,1,0:T(8,128)S(1)}) %tuple.86, (s32[3,64]{1,0:T(4,128)S(1)}, s32[]{:T(128)}, f32[48,5,128]{2,1,0:T(8,128)S(1)}) %tuple.87, (s32[3,64]{1,0:T(4,128)S(1)}, s32[]{:T(128)}, ...), branch_computations={%region_0.3_spmd, %region_3.6_spmd, %region_6.9_spmd} | conditional | flops 31477696 | bytes 1797260 | solution.py:424
  49.8 0.6 gather_fusion.3
  50.5 0.6 gather_fusion.2
  51.2 3.5 %multiply_reduce_fusion.3 = (f32[32,128]{1,0:T(8,128)S(1)}, f32[32,128]{1,0:T(8,128)S(1)}) fusion(f32[32,128]{1,0:T(8,128)S(1)} %bitcast.212, f32[32,128]{1,0:T(8,128)S(1)} %bitcast.217, f32[32,128]{1,0:T(8,128)S(1)} %bitcast.213, f32[32,128]{1,0:T(8,128)S(1)} %bitcast.218, f32[32,128]{1,0:T(8,128)S(1)} %bitcast.210, f32[32,128]{1,0:T(8,128)S(1)} %bitcast.215, ...), kind=kLoop, calls=%fused_computation.57 | loop fusion | flops 14147584 | bytes 196608 | tf_op jit(solution)/shard_map/cond/branch_1_fun/reduce_sum | solution.py:73
  54.7 0.7 iota_compare_fusion.3
  55.4 0.2 fusion.25
  55.6 0.6 copy.23
  56.3 0.7 pad_maximum_fusion.4.window_ref
  56.9 4.3 %shard_map.149 = (f32[4,2048]{1,0:T(4,128)}, f32[8,38,128]{2,1,0:T(8,128)}) custom-call(f32[2,128,128]{2,1,0:T(8,128)} %pad_maximum_fusion.4.window_ref, s32[1,2048]{1,0:T(1,128)} %fusion.101.rows_ref, s32[1,2048]{1,0:T(1,128)} %get-tuple-element.57.cols_ref, f32[2,2048]{1,0:T(2,128)} %bitcast.183, f32[2,2048]{1,0:T(2,128)} %bitcast.180, ...), custom_call_target="tpu_custom_call" | custom-call | tf_op jit(solution)/shard_map/pallas_call | solution.py:253
  61.2 0.9 fusion.111
  62.1 1.9 %collective-permute-start.7 = (f32[3,38,128]{2,1,0:T(8,128)S(1)}, f32[3,38,128]{2,1,0:T(8,128)S(1)}, u32[]{:S(2)}, u32[]{:S(2)}) collective-permute-start(f32[3,38,128]{2,1,0:T(8,128)S(1)} %get-tuple-element.118), channel_id=1, source_target_pairs={{0,8},{8,16},{16,24},{24,32},{32,40},{40,48},{48,56},{56,64},{64,7... | collective-permute-start | bytes 175112 | tf_op jit(solution)/shard_map/ppermute | solution.py:271
  64.0 0.8 fusion.110
  64.8 6.0 %collective-permute-start.6 = (f32[3,38,128]{2,1,0:T(8,128)S(1)}, f32[3,38,128]{2,1,0:T(8,128)S(1)}, u32[]{:S(2)}, u32[]{:S(2)}) collective-permute-start(f32[3,38,128]{2,1,0:T(8,128)S(1)} %get-tuple-element.117), channel_id=1, source_target_pairs={{8,0},{16,8},{24,16},{32,24},{40,32},{48,40},{56,48},{64,56},{72,6... | collective-permute-start | bytes 175112 | tf_op jit(solution)/shard_map/ppermute | solution.py:272
  70.9 1.8 %collective-permute-done.6 = f32[3,38,128]{2,1,0:T(8,128)S(1)} collective-permute-done((f32[3,38,128]{2,1,0:T(8,128)S(1)}, f32[3,38,128]{2,1,0:T(8,128)S(1)}, u32[]{:S(2)}, u32[]{:S(2)}) %collective-permute-start.6) | collective-permute-done | bytes 58400 | tf_op jit(solution)/shard_map/ppermute | solution.py:272
  72.7 7.2 %collective-permute-start.8 = (f32[3,38,128]{2,1,0:T(8,128)S(1)}, f32[3,38,128]{2,1,0:T(8,128)S(1)}, u32[]{:S(2)}, u32[]{:S(2)}) collective-permute-start(f32[3,38,128]{2,1,0:T(8,128)S(1)} %pad_maximum_fusion.6), channel_id=1, source_target_pairs={{1,0},{2,1},{3,2},{4,3},{5,4},{6,5},{7,6},{128,7},{129,128},{130,1... | collective-permute-start | bytes 175112 | tf_op jit(solution)/shard_map/ppermute | solution.py:272
  79.9 1.8 %collective-permute-done.8 = f32[3,38,128]{2,1,0:T(8,128)S(1)} collective-permute-done((f32[3,38,128]{2,1,0:T(8,128)S(1)}, f32[3,38,128]{2,1,0:T(8,128)S(1)}, u32[]{:S(2)}, u32[]{:S(2)}) %collective-permute-start.8) | collective-permute-done | bytes 58400 | tf_op jit(solution)/shard_map/ppermute | solution.py:272
  81.7 1.9 %collective-permute-start.9 = (f32[3,38,128]{2,1,0:T(8,128)S(1)}, f32[3,38,128]{2,1,0:T(8,128)S(1)}, u32[]{:S(2)}, u32[]{:S(2)}) collective-permute-start(f32[3,38,128]{2,1,0:T(8,128)S(1)} %pad_maximum_fusion.7), channel_id=1, source_target_pairs={{0,1},{1,2},{2,3},{3,4},{4,5},{5,6},{6,7},{7,128},{128,129},{129,1... | collective-permute-start | bytes 175112 | tf_op jit(solution)/shard_map/ppermute | solution.py:271
  83.7 7.3 %collective-permute-done.9 = f32[3,38,128]{2,1,0:T(8,128)S(1)} collective-permute-done((f32[3,38,128]{2,1,0:T(8,128)S(1)}, f32[3,38,128]{2,1,0:T(8,128)S(1)}, u32[]{:S(2)}, u32[]{:S(2)}) %collective-permute-start.9) | collective-permute-done | bytes 58400 | tf_op jit(solution)/shard_map/ppermute | solution.py:271
  91.0 0.7 copy.18
  (91 shorter events, 0.8 us)
Async XLA Ops:
  0.6 20.6 %copy-start.1 = (f32[2,64,128]{2,1,0:T(8,128)S(1)}, f32[2,64,128]{2,1,0:T(8,128)}, u32[]{:S(2)}) copy-start(f32[2,64,128]{2,1,0:T(8,128)} %param.17) | copy-start | bytes 196612
  0.6 20.6 %copy-start = (f32[2,8,64,128]{3,2,1,0:T(8,128)S(1)}, f32[2,8,64,128]{3,2,1,0:T(8,128)}, u32[]{:S(2)}) copy-start(f32[2,8,64,128]{3,2,1,0:T(8,128)} %param.16) | copy-start | bytes 1572868
  0.7 19.7 %copy-start.5 = (f32[1,1,2048]{2,1,0:T(1,128)S(1)}, f32[1,1,2048]{2,1,0:T(1,128)}, u32[]{:S(2)}) copy-start(f32[1,1,2048]{2,1,0:T(1,128)} %param.21) | copy-start | bytes 24580
  0.7 19.7 %copy-start.3 = (f32[1,1,2,2048]{3,2,1,0:T(2,128)S(1)}, f32[1,1,2,2048]{3,2,1,0:T(2,128)}, u32[]{:S(2)}) copy-start(f32[1,1,2,2048]{3,2,1,0:T(2,128)} %param.20) | copy-start | bytes 49156
  0.7 19.7 %copy-start.4 = (f32[1,1,2,2048]{3,2,1,0:T(2,128)S(1)}, f32[1,1,2,2048]{3,2,1,0:T(2,128)}, u32[]{:S(2)}) copy-start(f32[1,1,2,2048]{3,2,1,0:T(2,128)} %param.19) | copy-start | bytes 49156
  0.7 18.4 %copy-start.6 = (s32[1,1,2048]{2,1,0:T(1,128)S(1)}, s32[1,1,2048]{2,1,0:T(1,128)}, u32[]{:S(2)}) copy-start(s32[1,1,2048]{2,1,0:T(1,128)} %param.24) | copy-start | bytes 24580
  0.7 18.3 %copy-start.8 = (s32[1,1,3,64]{3,1,2,0:T(1,128)S(1)}, s32[1,1,3,64]{3,1,2,0:T(1,128)}, u32[]{:S(2)}) copy-start(s32[1,1,3,64]{3,1,2,0:T(1,128)} %param.26) | copy-start | bytes 2308
  0.7 19.0 %copy-start.7 = (s32[1,1,8,128]{3,2,1,0:T(8,128)S(1)}, s32[1,1,8,128]{3,2,1,0:T(8,128)}, u32[]{:S(2)}) copy-start(s32[1,1,8,128]{3,2,1,0:T(8,128)} %param.27) | copy-start | bytes 12292
  0.7 19.0 %copy-start.9 = (s32[1,1,8]{2,1,0:T(1,128)S(1)}, s32[1,1,8]{2,1,0:T(1,128)}, u32[]{:S(2)}) copy-start(s32[1,1,8]{2,1,0:T(1,128)} %param.28) | copy-start | bytes 100
  4.7 15.7 %collective-permute-start.1 = (f32[20480]{0:T(1024)S(1)}, f32[20480]{0:T(1024)S(1)}, u32[]{:S(2)}, u32[]{:S(2)}) collective-permute-start(f32[20480]{0:T(1024)S(1)} %constant_dynamic-update-slice_fusion.19), channel_id=1, source_target_pairs={{8,0},{16,8},{24,16},{32,24},{40,32},{48,40},{56,48},{64,56},{72,6... | collective-permute-start | bytes 245768 | tf_op jit(solution)/shard_map/ppermute | solution.py:272
  12.7 8.4 %collective-permute-start = (f32[20480]{0:T(1024)S(1)}, f32[20480]{0:T(1024)S(1)}, u32[]{:S(2)}, u32[]{:S(2)}) collective-permute-start(f32[20480]{0:T(1024)S(1)} %constant_dynamic-update-slice_fusion.18), channel_id=1, source_target_pairs={{0,8},{8,16},{16,24},{24,32},{32,40},{40,48},{48,56},{56,64},{64,7... | collective-permute-start | bytes 245768 | tf_op jit(solution)/shard_map/ppermute | solution.py:271
  22.4 8.8 %collective-permute-start.3 = (f32[13152]{0:T(1024)S(1)}, f32[13152]{0:T(1024)S(1)}, u32[]{:S(2)}, u32[]{:S(2)}) collective-permute-start(f32[13152]{0:T(1024)S(1)} %get-tuple-element.140), channel_id=1, source_target_pairs={{1,0},{2,1},{3,2},{4,3},{5,4},{6,5},{7,6},{128,7},{129,128},{130,1... | collective-permute-start | bytes 157832 | tf_op jit(solution)/shard_map/ppermute | solution.py:272
  25.9 9.1 %collective-permute-start.2 = (f32[13152]{0:T(1024)S(1)}, f32[13152]{0:T(1024)S(1)}, u32[]{:S(2)}, u32[]{:S(2)}) collective-permute-start(f32[13152]{0:T(1024)S(1)} %get-tuple-element.139), channel_id=1, source_target_pairs={{0,1},{1,2},{2,3},{3,4},{4,5},{5,6},{6,7},{7,128},{128,129},{129,1... | collective-permute-start | bytes 157832 | tf_op jit(solution)/shard_map/ppermute | solution.py:271
  42.2 7.5 %copy-start.2 = (f32[2,8,64,128]{3,2,1,0:T(8,128)}, f32[2,8,64,128]{3,2,1,0:T(8,128)S(1)}, u32[]{:S(2)}) copy-start(f32[2,8,64,128]{3,2,1,0:T(8,128)S(1)} %fusion.96) | copy-start | bytes 1572868
  42.3 14.0 %collective-permute-start.5 = (f32[2,32,128]{2,1,0:T(8,128)S(1)}, f32[2,32,128]{2,1,0:T(8,128)S(1)}, u32[]{:S(2)}, u32[]{:S(2)}) collective-permute-start(f32[2,32,128]{2,1,0:T(8,128)S(1)} %get-tuple-element.124), channel_id=1, source_target_pairs={{8,0},{16,8},{24,16},{32,24},{40,32},{48,40},{56,48},{64,56},{72,6... | collective-permute-start | bytes 98312 | tf_op jit(solution)/shard_map/ppermute | solution.py:272
  47.4 8.8 %collective-permute-start.4 = (f32[2,32,128]{2,1,0:T(8,128)S(1)}, f32[2,32,128]{2,1,0:T(8,128)S(1)}, u32[]{:S(2)}, u32[]{:S(2)}) collective-permute-start(f32[2,32,128]{2,1,0:T(8,128)S(1)} %get-tuple-element.123), channel_id=1, source_target_pairs={{0,8},{8,16},{16,24},{24,32},{32,40},{40,48},{48,56},{56,64},{64,7... | collective-permute-start | bytes 98312 | tf_op jit(solution)/shard_map/ppermute | solution.py:271
  62.1 8.7 %collective-permute-start.7 = (f32[3,38,128]{2,1,0:T(8,128)S(1)}, f32[3,38,128]{2,1,0:T(8,128)S(1)}, u32[]{:S(2)}, u32[]{:S(2)}) collective-permute-start(f32[3,38,128]{2,1,0:T(8,128)S(1)} %get-tuple-element.118), channel_id=1, source_target_pairs={{0,8},{8,16},{16,24},{24,32},{32,40},{40,48},{48,56},{56,64},{64,7... | collective-permute-start | bytes 175112 | tf_op jit(solution)/shard_map/ppermute | solution.py:271
  64.8 7.9 %collective-permute-start.6 = (f32[3,38,128]{2,1,0:T(8,128)S(1)}, f32[3,38,128]{2,1,0:T(8,128)S(1)}, u32[]{:S(2)}, u32[]{:S(2)}) collective-permute-start(f32[3,38,128]{2,1,0:T(8,128)S(1)} %get-tuple-element.117), channel_id=1, source_target_pairs={{8,0},{16,8},{24,16},{32,24},{40,32},{48,40},{56,48},{64,56},{72,6... | collective-permute-start | bytes 175112 | tf_op jit(solution)/shard_map/ppermute | solution.py:272
  72.7 9.0 %collective-permute-start.8 = (f32[3,38,128]{2,1,0:T(8,128)S(1)}, f32[3,38,128]{2,1,0:T(8,128)S(1)}, u32[]{:S(2)}, u32[]{:S(2)}) collective-permute-start(f32[3,38,128]{2,1,0:T(8,128)S(1)} %pad_maximum_fusion.6), channel_id=1, source_target_pairs={{1,0},{2,1},{3,2},{4,3},{5,4},{6,5},{7,6},{128,7},{129,128},{130,1... | collective-permute-start | bytes 175112 | tf_op jit(solution)/shard_map/ppermute | solution.py:272
  81.7 9.2 %collective-permute-start.9 = (f32[3,38,128]{2,1,0:T(8,128)S(1)}, f32[3,38,128]{2,1,0:T(8,128)S(1)}, u32[]{:S(2)}, u32[]{:S(2)}) collective-permute-start(f32[3,38,128]{2,1,0:T(8,128)S(1)} %pad_maximum_fusion.7), channel_id=1, source_target_pairs={{0,1},{1,2},{2,3},{3,4},{4,5},{5,6},{6,7},{7,128},{128,129},{129,1... | collective-permute-start | bytes 175112 | tf_op jit(solution)/shard_map/ppermute | solution.py:271

commit v6 on v5

--- a/solution.py
+++ b/solution.py
@@ -217,7 +217,7 @@
     ]
     velocity = velocity_ref[...]
     position = position_ref[...]
-    contact = contact_ref[...]
+    contact = jnp.concatenate([contact_ref[block] for block in range(contact_ref.shape[0])], axis=1)
     wind = wind_ref[...]
     radius = radius_ref[...]
     mass = mass_ref[...]
@@ -422,7 +422,6 @@
 
     which = sum((count > size).astype(jnp.int32) for size in sizes[:-1])
     contact = lax.switch(which, [pass_over(size) for size in sizes], lists, count)
-    contact = contact.transpose(1, 0, 2).reshape(2, floes)
     floe_next, outgoing = sample_update_gather(
         near, floe_rows, floe_cols, position, velocity, radius[None], mass[None], contact,
         sampled_wind, floe_polygon[0, 0], chosen,

time: 90.8 us -> 90.7 us (level); the launches traced: 91.7 us -> 89.8 us
  other arithmetic: 18.6 us -> 16.8 us
  waiting for transfers between devices: 14.7 us -> 16.1 us
  starting transfers between devices: 39.4 us -> 38.4 us
    reduce_sum x1, other arithmetic: 3.51 us -> 1.77 us  [pair_forces(): jnp.sum(magnitude * normal_x, axis=1)]
    ppermute x5, waiting for transfers between devices: 11 us -> 12.5 us  [exchange(): from_previous = lax.ppermute(high, axis, up)]
    ppermute x5, starting transfers between devices: 29.8 us -> 28.8 us  [exchange(): from_next = lax.ppermute(low, axis, down)]
  transfers between devices with their start and end apart: 10 -> 10, of which waited for: 5 -> 6; matrix products, arithmetic and copies ran while one was open for 15% -> 13% of each run, Pallas kernels for 3% -> 3%
where the time goes in v6:
time: 90.7 us; the launch traced here: 89.8 us
  starting transfers between devices  38.4 us (42%)
  other arithmetic  16.8 us (19%)
  waiting for transfers between devices  16.1 us (18%)
  local copies, waits for them, and re-layouts  8.93 us (10%)
  Pallas kernels  7.05 us (8%)
  between operations  2.01 us (2%)
    ppermute x5, starting transfers between devices, exchange(): from_next = lax.ppermute(low, axis, down)  28.8 us
    ppermute x5, waiting for transfers between devices, exchange(): from_previous = lax.ppermute(high, axis, up)  12.5 us
    ppermute x5, starting transfers between devices, exchange(): from_previous = lax.ppermute(high, axis, up)  9.6 us
    pallas_call x1, Pallas kernels, sample_update_gather(): pl.pallas_call(tail_kernel, out_shape=(jax.ShapeDtypeStruct((4, floes), j...  4.39 us
    mul x4, other arithmetic, ocean_substep(): return (flow + horizontal * lap + vert + turning + surface) * wet[None]  3.99 us
    ppermute x5, waiting for transfers between devices, exchange(): from_next = lax.ppermute(low, axis, down)  3.67 us
    pallas_call x1, Pallas kernels, sample_surface(): pl.pallas_call(sample_kernel, out_shape=jax.ShapeDtypeStruct((window.shap...  2.67 us
  transfers between devices with their start and end apart: 10, of which 6 were waited for; matrix products, arithmetic and copies ran while one was open for 13% of the time, Pallas kernels for 3%

profile of v6, /device:TPU:24, one launch (start us, length us, event | category | flops | bytes accessed | tf_op | source)
XLA Modules:
  0.0 89.8 jit_solution(1885680257217437336)
XLA Ops:
  0.7 0.8 fusion.114
  1.5 0.8 fusion.113
  2.3 0.9 fusion.109
  3.2 0.7 pad_maximum_fusion.12
  4.0 0.7 constant_dynamic-update-slice_fusion.22
  4.7 7.9 %collective-permute-start.1 = (f32[20480]{0:T(1024)S(1)}, f32[20480]{0:T(1024)S(1)}, u32[]{:S(2)}, u32[]{:S(2)}) collective-permute-start(f32[20480]{0:T(1024)S(1)} %constant_dynamic-update-slice_fusion.19), channel_id=1, source_target_pairs={{8,0},{16,8},{24,16},{32,24},{40,32},{48,40},{56,48},{64,56},{72,6... | collective-permute-start | bytes 245768 | tf_op jit(solution)/shard_map/ppermute | solution.py:272
  12.7 1.9 %collective-permute-start = (f32[20480]{0:T(1024)S(1)}, f32[20480]{0:T(1024)S(1)}, u32[]{:S(2)}, u32[]{:S(2)}) collective-permute-start(f32[20480]{0:T(1024)S(1)} %constant_dynamic-update-slice_fusion.18), channel_id=1, source_target_pairs={{0,8},{8,16},{16,24},{24,32},{32,40},{40,48},{48,56},{56,64},{64,7... | collective-permute-start | bytes 245768 | tf_op jit(solution)/shard_map/ppermute | solution.py:271
  14.6 0.8 convert_bitcast_fusion
  15.4 0.8 multiply_bitcast_fusion
  16.2 0.8 fusion.98
  17.0 1.3 %and_select_fusion = (s32[1,2048]{1,0:T(1,128)}, s32[1,2048]{1,0:T(1,128)S(1)}) fusion(s32[1,1,2048]{2,1,0:T(1,128)} %param.24), kind=kLoop, calls=%fused_computation.238 | loop fusion | flops 22528 | bytes 24576 | tf_op jit(solution)/shard_map/jit(remainder)/select_n | solution.py:387
  19.0 0.6 fusion.101.rows_ref
  19.6 0.7 bitcast_select_fusion.index_ref
  20.4 0.7 collective-permute-done
  21.3 0.2 fusion.108
  21.6 0.4 reshape.581
  21.9 0.4 reshape.584
  22.3 0.1 pad_maximum_fusion.9
  22.4 3.5 %collective-permute-start.3 = (f32[13152]{0:T(1024)S(1)}, f32[13152]{0:T(1024)S(1)}, u32[]{:S(2)}, u32[]{:S(2)}) collective-permute-start(f32[13152]{0:T(1024)S(1)} %get-tuple-element.144), channel_id=1, source_target_pairs={{1,0},{2,1},{3,2},{4,3},{5,4},{6,5},{7,6},{128,7},{129,128},{130,1... | collective-permute-start | bytes 157832 | tf_op jit(solution)/shard_map/ppermute | solution.py:272
  25.9 1.9 %collective-permute-start.2 = (f32[13152]{0:T(1024)S(1)}, f32[13152]{0:T(1024)S(1)}, u32[]{:S(2)}, u32[]{:S(2)}) collective-permute-start(f32[13152]{0:T(1024)S(1)} %get-tuple-element.143), channel_id=1, source_target_pairs={{0,1},{1,2},{2,3},{3,4},{4,5},{5,6},{6,7},{7,128},{128,129},{129,1... | collective-permute-start | bytes 157832 | tf_op jit(solution)/shard_map/ppermute | solution.py:271
  27.8 0.7 pad_maximum_fusion.3.window_ref
  28.5 2.7 %shard_map.148.wind_ref = f32[2,2048]{1,0:T(2,128)} custom-call(f32[2,128,128]{2,1,0:T(8,128)} %pad_maximum_fusion.3.window_ref, s32[1,2048]{1,0:T(1,128)} %fusion.101.rows_ref, s32[1,2048]{1,0:T(1,128)} %get-tuple-element.61.cols_ref), custom_call_target="tpu_custom_call" | custom-call | tf_op jit(solution)/shard_map/pallas_call | solution.py:133
  31.2 0.7 reshape.585
  31.9 3.0 %collective-permute-done.2 = f32[13152]{0:T(1024)S(1)} collective-permute-done((f32[13152]{0:T(1024)S(1)}, f32[13152]{0:T(1024)S(1)}, u32[]{:S(2)}, u32[]{:S(2)}) %collective-permute-start.2) | collective-permute-done | bytes 52640 | tf_op jit(solution)/shard_map/ppermute | solution.py:271
  34.9 0.7 reshape.583
  35.7 0.1 fusion.99
  35.8 0.7 pad_maximum_fusion
  36.5 0.1 maximum_bitcast_fusion
  36.8 0.1 broadcast_multiply_fusion
  37.0 0.1 slice_multiply_fusion.5
  37.1 0.1 subtract_multiply_fusion.12
  37.2 1.1 %fusion.84 = f32[2,8,72,136]{3,2,1,0:T(8,128)S(1)} fusion(f32[2,1,72,136]{3,2,1,0:T(8,128)S(1)} %fusion.99, f32[1,8,72,136]{3,2,1,0:T(8,128)S(1)} %get-tuple-element.112, f32[1,8,72,136]{3,2,1,0:T(8,128)S(1)} %get-tuple-element.111, f32[2,7,72,136]{3,2,1,0:T(8,128)S(1)} %subtract_multiply_fusion.12, f32[2,8,72,136]{3,2,1,0:T(8,128)S(1)} %broadcast_multiply_fusion, ...), kind=kLoop, calls=%fused_computation.163 | loop fusion | flops 2036736 | bytes 2820128 | tf_op jit(solution)/shard_map/mul | solution.py:55
  38.3 0.1 slice_multiply_fusion.3
  38.4 0.1 fusion.88
  38.5 1.1 %fusion.85 = f32[2,8,72,136]{3,2,1,0:T(8,128)S(1)} fusion(f32[2,1,72,136]{3,2,1,0:T(8,128)S(1)} %fusion.99, f32[1,8,72,136]{3,2,1,0:T(8,128)S(1)} %get-tuple-element.110, f32[1,8,72,136]{3,2,1,0:T(8,128)S(1)} %get-tuple-element.109, f32[2,7,72,136]{3,2,1,0:T(8,128)S(1)} %fusion.88, f32[2,8,72,136]{3,2,1,0:T(8,128)S(1)} %fusion.84, ...), kind=kLoop, calls=%fused_computation.164 | loop fusion | flops 2036736 | bytes 2820128 | tf_op jit(solution)/shard_map/mul | solution.py:55
  39.6 0.1 slice_multiply_fusion.1
  39.7 0.1 fusion.87
  39.8 1.1 %fusion.86 = f32[2,8,72,136]{3,2,1,0:T(8,128)S(1)} fusion(f32[2,1,72,136]{3,2,1,0:T(8,128)S(1)} %fusion.99, f32[1,8,72,136]{3,2,1,0:T(8,128)S(1)} %get-tuple-element.108, f32[1,8,72,136]{3,2,1,0:T(8,128)S(1)} %get-tuple-element.107, f32[2,7,72,136]{3,2,1,0:T(8,128)S(1)} %fusion.87, f32[2,8,72,136]{3,2,1,0:T(8,128)S(1)} %fusion.85, ...), kind=kLoop, calls=%fused_computation.165 | loop fusion | flops 2036736 | bytes 2820128 | tf_op jit(solution)/shard_map/mul | solution.py:55
  40.9 0.2 slice_multiply_fusion.8
  41.1 0.3 fusion.97
  41.4 0.8 fusion.96
  42.2 5.1 %collective-permute-start.5 = (f32[2,32,128]{2,1,0:T(8,128)S(1)}, f32[2,32,128]{2,1,0:T(8,128)S(1)}, u32[]{:S(2)}, u32[]{:S(2)}) collective-permute-start(f32[2,32,128]{2,1,0:T(8,128)S(1)} %get-tuple-element.128), channel_id=1, source_target_pairs={{8,0},{16,8},{24,16},{32,24},{40,32},{48,40},{56,48},{64,56},{72,6... | collective-permute-start | bytes 98312 | tf_op jit(solution)/shard_map/ppermute | solution.py:272
  47.4 1.9 %collective-permute-start.4 = (f32[2,32,128]{2,1,0:T(8,128)S(1)}, f32[2,32,128]{2,1,0:T(8,128)S(1)}, u32[]{:S(2)}, u32[]{:S(2)}) collective-permute-start(f32[2,32,128]{2,1,0:T(8,128)S(1)} %get-tuple-element.127), channel_id=1, source_target_pairs={{0,8},{8,16},{16,24},{24,32},{32,40},{40,48},{48,56},{56,64},{64,7... | collective-permute-start | bytes 98312 | tf_op jit(solution)/shard_map/ppermute | solution.py:271
  49.3 0.1 fusion.118
  49.4 0.1 fusion.117
  49.8 4.1 %conditional.1 = (f32[16,2,128]{2,1,0:T(2,128)S(1)}) conditional(s32[]{:T(128)} %clamp.3, (s32[1,1,3,64]{3,1,2,0:T(1,128)S(1)}, s32[]{:T(128)}, f32[48,5,128]{2,1,0:T(8,128)S(1)}) %tuple.89, (s32[1,1,3,64]{3,1,2,0:T(1,128)S(1)}, s32[]{:T(128)}, f32[48,5,128]{2,1,0:T(8,128)S(1)}) %tuple.90, (s32[1,1,3,64]{3,1,2,0:T(1,128)S(1)}, ...), branch_computations={%region_0.3_spmd, %region_3.6_spmd, %region_6.9_spmd} | conditional | flops 31477696 | bytes 1831564 | solution.py:424
  49.8 0.6 gather_fusion.1
  50.4 0.6 gather_fusion
  51.1 1.8 %multiply_reduce_fusion.1 = (f32[16,128]{1,0:T(8,128)S(1)}, f32[16,128]{1,0:T(8,128)S(1)}) fusion(f32[16,128]{1,0:T(8,128)S(1)} %bitcast.222, f32[16,128]{1,0:T(8,128)S(1)} %bitcast.227, f32[16,128]{1,0:T(8,128)S(1)} %bitcast.223, f32[16,128]{1,0:T(8,128)S(1)} %bitcast.228, f32[16,128]{1,0:T(8,128)S(1)} %bitcast.220, f32[16,128]{1,0:T(8,128)S(1)} %bitcast.225, ...), kind=kLoop, calls=%fused_computation.19 | loop fusion | flops 7073792 | bytes 98304 | tf_op jit(solution)/shard_map/cond/branch_0_fun/reduce_sum | solution.py:73
  52.8 0.7 iota_compare_fusion.1
  53.5 0.2 fusion.5
  53.9 1.4 %collective-permute-done.4 = f32[2,32,128]{2,1,0:T(8,128)S(1)} collective-permute-done((f32[2,32,128]{2,1,0:T(8,128)S(1)}, f32[2,32,128]{2,1,0:T(8,128)S(1)}, u32[]{:S(2)}, u32[]{:S(2)}) %collective-permute-start.4) | collective-permute-done | bytes 32800 | tf_op jit(solution)/shard_map/ppermute | solution.py:271
  55.3 0.7 pad_maximum_fusion.4.window_ref
  56.0 4.4 %shard_map.149 = (f32[4,2048]{1,0:T(4,128)}, f32[8,38,128]{2,1,0:T(8,128)}) custom-call(f32[2,128,128]{2,1,0:T(8,128)} %pad_maximum_fusion.4.window_ref, s32[1,2048]{1,0:T(1,128)} %fusion.101.rows_ref, s32[1,2048]{1,0:T(1,128)} %get-tuple-element.61.cols_ref, f32[2,2048]{1,0:T(2,128)} %bitcast.184, f32[2,2048]{1,0:T(2,128)} %bitcast.181, ...), custom_call_target="tpu_custom_call" | custom-call | tf_op jit(solution)/shard_map/pallas_call | solution.py:253
  60.4 0.9 fusion.111
  61.2 1.9 %collective-permute-start.7 = (f32[3,38,128]{2,1,0:T(8,128)S(1)}, f32[3,38,128]{2,1,0:T(8,128)S(1)}, u32[]{:S(2)}, u32[]{:S(2)}) collective-permute-start(f32[3,38,128]{2,1,0:T(8,128)S(1)} %get-tuple-element.122), channel_id=1, source_target_pairs={{0,8},{8,16},{16,24},{24,32},{32,40},{40,48},{48,56},{56,64},{64,7... | collective-permute-start | bytes 175112 | tf_op jit(solution)/shard_map/ppermute | solution.py:271
  63.2 0.8 fusion.110
  63.9 10.3 %collective-permute-start.6 = (f32[3,38,128]{2,1,0:T(8,128)S(1)}, f32[3,38,128]{2,1,0:T(8,128)S(1)}, u32[]{:S(2)}, u32[]{:S(2)}) collective-permute-start(f32[3,38,128]{2,1,0:T(8,128)S(1)} %get-tuple-element.121), channel_id=1, source_target_pairs={{8,0},{16,8},{24,16},{32,24},{40,32},{48,40},{56,48},{64,56},{72,6... | collective-permute-start | bytes 175112 | tf_op jit(solution)/shard_map/ppermute | solution.py:272
  74.2 1.8 %collective-permute-done.6 = f32[3,38,128]{2,1,0:T(8,128)S(1)} collective-permute-done((f32[3,38,128]{2,1,0:T(8,128)S(1)}, f32[3,38,128]{2,1,0:T(8,128)S(1)}, u32[]{:S(2)}, u32[]{:S(2)}) %collective-permute-start.6) | collective-permute-done | bytes 58400 | tf_op jit(solution)/shard_map/ppermute | solution.py:272
  76.0 1.9 %collective-permute-start.8 = (f32[3,38,128]{2,1,0:T(8,128)S(1)}, f32[3,38,128]{2,1,0:T(8,128)S(1)}, u32[]{:S(2)}, u32[]{:S(2)}) collective-permute-start(f32[3,38,128]{2,1,0:T(8,128)S(1)} %pad_maximum_fusion.6), channel_id=1, source_target_pairs={{1,0},{2,1},{3,2},{4,3},{5,4},{6,5},{7,6},{128,7},{129,128},{130,1... | collective-permute-start | bytes 175112 | tf_op jit(solution)/shard_map/ppermute | solution.py:272
  78.0 1.8 %collective-permute-done.8 = f32[3,38,128]{2,1,0:T(8,128)S(1)} collective-permute-done((f32[3,38,128]{2,1,0:T(8,128)S(1)}, f32[3,38,128]{2,1,0:T(8,128)S(1)}, u32[]{:S(2)}, u32[]{:S(2)}) %collective-permute-start.8) | collective-permute-done | bytes 58400 | tf_op jit(solution)/shard_map/ppermute | solution.py:272
  79.8 1.9 %collective-permute-start.9 = (f32[3,38,128]{2,1,0:T(8,128)S(1)}, f32[3,38,128]{2,1,0:T(8,128)S(1)}, u32[]{:S(2)}, u32[]{:S(2)}) collective-permute-start(f32[3,38,128]{2,1,0:T(8,128)S(1)} %pad_maximum_fusion.7), channel_id=1, source_target_pairs={{0,1},{1,2},{2,3},{3,4},{4,5},{5,6},{6,7},{7,128},{128,129},{129,1... | collective-permute-start | bytes 175112 | tf_op jit(solution)/shard_map/ppermute | solution.py:271
  81.8 7.3 %collective-permute-done.9 = f32[3,38,128]{2,1,0:T(8,128)S(1)} collective-permute-done((f32[3,38,128]{2,1,0:T(8,128)S(1)}, f32[3,38,128]{2,1,0:T(8,128)S(1)}, u32[]{:S(2)}, u32[]{:S(2)}) %collective-permute-start.9) | collective-permute-done | bytes 58400 | tf_op jit(solution)/shard_map/ppermute | solution.py:271
  89.1 0.7 copy.21
  (91 shorter events, 0.8 us)
Async XLA Ops:
  0.6 20.6 %copy-start.1 = (f32[2,64,128]{2,1,0:T(8,128)S(1)}, f32[2,64,128]{2,1,0:T(8,128)}, u32[]{:S(2)}) copy-start(f32[2,64,128]{2,1,0:T(8,128)} %param.17) | copy-start | bytes 196612
  0.6 20.6 %copy-start = (f32[2,8,64,128]{3,2,1,0:T(8,128)S(1)}, f32[2,8,64,128]{3,2,1,0:T(8,128)}, u32[]{:S(2)}) copy-start(f32[2,8,64,128]{3,2,1,0:T(8,128)} %param.16) | copy-start | bytes 1572868
  0.7 19.7 %copy-start.5 = (f32[1,1,2048]{2,1,0:T(1,128)S(1)}, f32[1,1,2048]{2,1,0:T(1,128)}, u32[]{:S(2)}) copy-start(f32[1,1,2048]{2,1,0:T(1,128)} %param.21) | copy-start | bytes 24580
  0.7 19.6 %copy-start.3 = (f32[1,1,2,2048]{3,2,1,0:T(2,128)S(1)}, f32[1,1,2,2048]{3,2,1,0:T(2,128)}, u32[]{:S(2)}) copy-start(f32[1,1,2,2048]{3,2,1,0:T(2,128)} %param.20) | copy-start | bytes 49156
  0.7 19.6 %copy-start.4 = (f32[1,1,2,2048]{3,2,1,0:T(2,128)S(1)}, f32[1,1,2,2048]{3,2,1,0:T(2,128)}, u32[]{:S(2)}) copy-start(f32[1,1,2,2048]{3,2,1,0:T(2,128)} %param.19) | copy-start | bytes 49156
  0.7 18.3 %copy-start.6 = (s32[1,1,2048]{2,1,0:T(1,128)S(1)}, s32[1,1,2048]{2,1,0:T(1,128)}, u32[]{:S(2)}) copy-start(s32[1,1,2048]{2,1,0:T(1,128)} %param.24) | copy-start | bytes 24580
  0.7 18.9 %copy-start.8 = (s32[1,1,8,128]{3,2,1,0:T(8,128)S(1)}, s32[1,1,8,128]{3,2,1,0:T(8,128)}, u32[]{:S(2)}) copy-start(s32[1,1,8,128]{3,2,1,0:T(8,128)} %param.27) | copy-start | bytes 12292
  0.7 18.9 %copy-start.9 = (s32[1,1,8]{2,1,0:T(1,128)S(1)}, s32[1,1,8]{2,1,0:T(1,128)}, u32[]{:S(2)}) copy-start(s32[1,1,8]{2,1,0:T(1,128)} %param.28) | copy-start | bytes 100
  4.7 15.6 %collective-permute-start.1 = (f32[20480]{0:T(1024)S(1)}, f32[20480]{0:T(1024)S(1)}, u32[]{:S(2)}, u32[]{:S(2)}) collective-permute-start(f32[20480]{0:T(1024)S(1)} %constant_dynamic-update-slice_fusion.19), channel_id=1, source_target_pairs={{8,0},{16,8},{24,16},{32,24},{40,32},{48,40},{56,48},{64,56},{72,6... | collective-permute-start | bytes 245768 | tf_op jit(solution)/shard_map/ppermute | solution.py:272
  12.7 8.4 %collective-permute-start = (f32[20480]{0:T(1024)S(1)}, f32[20480]{0:T(1024)S(1)}, u32[]{:S(2)}, u32[]{:S(2)}) collective-permute-start(f32[20480]{0:T(1024)S(1)} %constant_dynamic-update-slice_fusion.18), channel_id=1, source_target_pairs={{0,8},{8,16},{16,24},{24,32},{32,40},{40,48},{48,56},{56,64},{64,7... | collective-permute-start | bytes 245768 | tf_op jit(solution)/shard_map/ppermute | solution.py:271
  22.4 8.8 %collective-permute-start.3 = (f32[13152]{0:T(1024)S(1)}, f32[13152]{0:T(1024)S(1)}, u32[]{:S(2)}, u32[]{:S(2)}) collective-permute-start(f32[13152]{0:T(1024)S(1)} %get-tuple-element.144), channel_id=1, source_target_pairs={{1,0},{2,1},{3,2},{4,3},{5,4},{6,5},{7,6},{128,7},{129,128},{130,1... | collective-permute-start | bytes 157832 | tf_op jit(solution)/shard_map/ppermute | solution.py:272
  25.9 9.1 %collective-permute-start.2 = (f32[13152]{0:T(1024)S(1)}, f32[13152]{0:T(1024)S(1)}, u32[]{:S(2)}, u32[]{:S(2)}) collective-permute-start(f32[13152]{0:T(1024)S(1)} %get-tuple-element.143), channel_id=1, source_target_pairs={{0,1},{1,2},{2,3},{3,4},{4,5},{5,6},{6,7},{7,128},{128,129},{129,1... | collective-permute-start | bytes 157832 | tf_op jit(solution)/shard_map/ppermute | solution.py:271
  42.2 7.6 %copy-start.2 = (f32[2,8,64,128]{3,2,1,0:T(8,128)}, f32[2,8,64,128]{3,2,1,0:T(8,128)S(1)}, u32[]{:S(2)}) copy-start(f32[2,8,64,128]{3,2,1,0:T(8,128)S(1)} %fusion.96) | copy-start | bytes 1572868
  42.2 7.5 %copy-start.7 = (s32[1,1,3,64]{3,1,2,0:T(1,128)S(1)}, s32[1,1,3,64]{3,1,2,0:T(1,128)}, u32[]{:S(2)}) copy-start(s32[1,1,3,64]{3,1,2,0:T(1,128)} %param.26) | copy-start | bytes 2308
  42.2 11.7 %collective-permute-start.5 = (f32[2,32,128]{2,1,0:T(8,128)S(1)}, f32[2,32,128]{2,1,0:T(8,128)S(1)}, u32[]{:S(2)}, u32[]{:S(2)}) collective-permute-start(f32[2,32,128]{2,1,0:T(8,128)S(1)} %get-tuple-element.128), channel_id=1, source_target_pairs={{8,0},{16,8},{24,16},{32,24},{40,32},{48,40},{56,48},{64,56},{72,6... | collective-permute-start | bytes 98312 | tf_op jit(solution)/shard_map/ppermute | solution.py:272
  47.4 7.9 %collective-permute-start.4 = (f32[2,32,128]{2,1,0:T(8,128)S(1)}, f32[2,32,128]{2,1,0:T(8,128)S(1)}, u32[]{:S(2)}, u32[]{:S(2)}) collective-permute-start(f32[2,32,128]{2,1,0:T(8,128)S(1)} %get-tuple-element.127), channel_id=1, source_target_pairs={{0,8},{8,16},{16,24},{24,32},{32,40},{40,48},{48,56},{56,64},{64,7... | collective-permute-start | bytes 98312 | tf_op jit(solution)/shard_map/ppermute | solution.py:271
  61.2 12.9 %collective-permute-start.7 = (f32[3,38,128]{2,1,0:T(8,128)S(1)}, f32[3,38,128]{2,1,0:T(8,128)S(1)}, u32[]{:S(2)}, u32[]{:S(2)}) collective-permute-start(f32[3,38,128]{2,1,0:T(8,128)S(1)} %get-tuple-element.122), channel_id=1, source_target_pairs={{0,8},{8,16},{16,24},{24,32},{32,40},{40,48},{48,56},{56,64},{64,7... | collective-permute-start | bytes 175112 | tf_op jit(solution)/shard_map/ppermute | solution.py:271
  63.9 12.1 %collective-permute-start.6 = (f32[3,38,128]{2,1,0:T(8,128)S(1)}, f32[3,38,128]{2,1,0:T(8,128)S(1)}, u32[]{:S(2)}, u32[]{:S(2)}) collective-permute-start(f32[3,38,128]{2,1,0:T(8,128)S(1)} %get-tuple-element.121), channel_id=1, source_target_pairs={{8,0},{16,8},{24,16},{32,24},{40,32},{48,40},{56,48},{64,56},{72,6... | collective-permute-start | bytes 175112 | tf_op jit(solution)/shard_map/ppermute | solution.py:272
  76.0 3.8 %collective-permute-start.8 = (f32[3,38,128]{2,1,0:T(8,128)S(1)}, f32[3,38,128]{2,1,0:T(8,128)S(1)}, u32[]{:S(2)}, u32[]{:S(2)}) collective-permute-start(f32[3,38,128]{2,1,0:T(8,128)S(1)} %pad_maximum_fusion.6), channel_id=1, source_target_pairs={{1,0},{2,1},{3,2},{4,3},{5,4},{6,5},{7,6},{128,7},{129,128},{130,1... | collective-permute-start | bytes 175112 | tf_op jit(solution)/shard_map/ppermute | solution.py:272
  79.8 9.2 %collective-permute-start.9 = (f32[3,38,128]{2,1,0:T(8,128)S(1)}, f32[3,38,128]{2,1,0:T(8,128)S(1)}, u32[]{:S(2)}, u32[]{:S(2)}) collective-permute-start(f32[3,38,128]{2,1,0:T(8,128)S(1)} %pad_maximum_fusion.7), channel_id=1, source_target_pairs={{0,1},{1,2},{2,3},{3,4},{4,5},{5,6},{6,7},{7,128},{128,129},{129,1... | collective-permute-start | bytes 175112 | tf_op jit(solution)/shard_map/ppermute | solution.py:271

commit v7 on v5

--- a/solution.py
+++ b/solution.py
@@ -232,8 +232,7 @@
         next_ref[2 + axis : 3 + axis, :] = new_velocity
         next_ref[axis : axis + 1, :] = position[axis : axis + 1] + ICE_STEP * new_velocity
     width = out_ref.shape[1]
-    record_ref[...] = jnp.zeros_like(record_ref)
-    stack_ref[...] = jnp.zeros_like(stack_ref)
+    record_ref[width:, :] = jnp.zeros((record_ref.shape[0] - width, floes), jnp.float32)
     record_ref[0:4, :] = next_ref[...]
     record_ref[4:5, :] = radius
     record_ref[5:6, :] = mass

time: 90.8 us -> 88.9 us (0.979)
  the two profiles are of different devices: /device:TPU:24 before, /device:TPU:120 now
where the time goes in v7:
time: 88.9 us; the launch traced here: 87.8 us
  starting transfers between devices  35.9 us (40%)
  other arithmetic  16.8 us (19%)
  waiting for transfers between devices  16.1 us (18%)
  local copies, waits for them, and re-layouts  9.53 us (11%)
  Pallas kernels  6.97 us (8%)
  between operations  2.04 us (2%)
    ppermute x5, starting transfers between devices, exchange(): from_next = lax.ppermute(low, axis, down)  19.5 us
    ppermute x5, starting transfers between devices, exchange(): from_previous = lax.ppermute(high, axis, up)  16.4 us
    ppermute x5, waiting for transfers between devices, exchange(): from_previous = lax.ppermute(high, axis, up)  10.3 us
    ppermute x5, waiting for transfers between devices, exchange(): from_next = lax.ppermute(low, axis, down)  5.74 us
    pallas_call x1, Pallas kernels, sample_update_gather(): pl.pallas_call(tail_kernel, out_shape=(jax.ShapeDtypeStruct((4, floes), j...  4.31 us
    mul x4, other arithmetic, ocean_substep(): return (flow + horizontal * lap + vert + turning + surface) * wet[None]  3.99 us
    pallas_call x1, Pallas kernels, sample_surface(): pl.pallas_call(sample_kernel, out_shape=jax.ShapeDtypeStruct((window.shap...  2.65 us
  transfers between devices with their start and end apart: 10, of which 4 were waited for; matrix products, arithmetic and copies ran while one was open for 14% of the time, Pallas kernels for 3%

profile of v7, /device:TPU:120, one launch (start us, length us, event | category | flops | bytes accessed | tf_op | source)
XLA Modules:
  0.0 87.8 jit_solution(6160890869665057417)
XLA Ops:
  0.7 0.8 fusion.114
  1.5 0.8 fusion.113
  2.3 0.9 %fusion.109 = (f32[2,8,4,128]{3,2,1,0:T(4,128)S(1)}, f32[2,8,4,128]{3,2,1,0:T(4,128)S(1)}) fusion(f32[2,8,64,128]{3,2,1,0:T(8,128)} %param.16), kind=kLoop, calls=%fused_computation.264 | loop fusion | bytes 131072 | tf_op jit(solution)/shard_map/slice | solution.py:318
  3.2 0.7 pad_maximum_fusion.12
  4.0 0.7 constant_dynamic-update-slice_fusion.22
  4.7 2.0 %collective-permute-start.1 = (f32[20480]{0:T(1024)S(1)}, f32[20480]{0:T(1024)S(1)}, u32[]{:S(2)}, u32[]{:S(2)}) collective-permute-start(f32[20480]{0:T(1024)S(1)} %constant_dynamic-update-slice_fusion.19), channel_id=1, source_target_pairs={{8,0},{16,8},{24,16},{32,24},{40,32},{48,40},{56,48},{64,56},{72,6... | collective-permute-start | bytes 245768 | tf_op jit(solution)/shard_map/ppermute | solution.py:271
  6.8 5.0 %collective-permute-start = (f32[20480]{0:T(1024)S(1)}, f32[20480]{0:T(1024)S(1)}, u32[]{:S(2)}, u32[]{:S(2)}) collective-permute-start(f32[20480]{0:T(1024)S(1)} %constant_dynamic-update-slice_fusion.18), channel_id=1, source_target_pairs={{0,8},{8,16},{16,24},{24,32},{32,40},{40,48},{48,56},{56,64},{64,7... | collective-permute-start | bytes 245768 | tf_op jit(solution)/shard_map/ppermute | solution.py:270
  11.8 0.8 convert_bitcast_fusion
  12.6 0.8 multiply_bitcast_fusion
  13.4 0.8 fusion.98
  14.2 1.3 %and_select_fusion = (s32[1,2048]{1,0:T(1,128)}, s32[1,2048]{1,0:T(1,128)S(1)}) fusion(s32[1,1,2048]{2,1,0:T(1,128)} %param.24), kind=kLoop, calls=%fused_computation.235 | loop fusion | flops 22528 | bytes 24576 | tf_op jit(solution)/shard_map/jit(remainder)/select_n | solution.py:386
  16.2 0.6 fusion.101.rows_ref
  16.9 0.7 bitcast_select_fusion.index_ref
  17.8 0.2 fusion.108
  18.1 0.4 reshape.584
  18.5 0.4 reshape.587
  18.8 0.1 pad_maximum_fusion.9
  18.9 4.4 %collective-permute-start.3 = (f32[13152]{0:T(1024)S(1)}, f32[13152]{0:T(1024)S(1)}, u32[]{:S(2)}, u32[]{:S(2)}) collective-permute-start(f32[13152]{0:T(1024)S(1)} %get-tuple-element.140), channel_id=1, source_target_pairs={{1,0},{2,1},{3,2},{4,3},{5,4},{6,5},{7,6},{128,7},{129,128},{130,1... | collective-permute-start | bytes 157832 | tf_op jit(solution)/shard_map/ppermute | solution.py:271
  23.3 1.9 %collective-permute-start.2 = (f32[13152]{0:T(1024)S(1)}, f32[13152]{0:T(1024)S(1)}, u32[]{:S(2)}, u32[]{:S(2)}) collective-permute-start(f32[13152]{0:T(1024)S(1)} %get-tuple-element.139), channel_id=1, source_target_pairs={{0,1},{1,2},{2,3},{3,4},{4,5},{5,6},{6,7},{7,128},{128,129},{129,1... | collective-permute-start | bytes 157832 | tf_op jit(solution)/shard_map/ppermute | solution.py:270
  25.3 0.7 pad_maximum_fusion.3.window_ref
  25.9 2.7 %shard_map.148.wind_ref = f32[2,2048]{1,0:T(2,128)} custom-call(f32[2,128,128]{2,1,0:T(8,128)} %pad_maximum_fusion.3.window_ref, s32[1,2048]{1,0:T(1,128)} %fusion.101.rows_ref, s32[1,2048]{1,0:T(1,128)} %get-tuple-element.57.cols_ref), custom_call_target="tpu_custom_call" | custom-call | tf_op jit(solution)/shard_map/pallas_call | solution.py:133
  28.6 0.7 reshape.588
  29.3 3.1 %collective-permute-done.2 = f32[13152]{0:T(1024)S(1)} collective-permute-done((f32[13152]{0:T(1024)S(1)}, f32[13152]{0:T(1024)S(1)}, u32[]{:S(2)}, u32[]{:S(2)}) %collective-permute-start.2) | collective-permute-done | bytes 52640 | tf_op jit(solution)/shard_map/ppermute | solution.py:270
  32.4 0.7 reshape.586
  33.1 0.1 fusion.99
  33.2 0.7 pad_maximum_fusion
  33.9 0.1 maximum_bitcast_fusion
  34.1 0.1 slice.634
  34.2 0.1 broadcast_multiply_fusion
  34.4 0.1 slice_multiply_fusion.5
  34.5 0.1 subtract_multiply_fusion.12
  34.6 1.1 %fusion.84 = f32[2,8,72,136]{3,2,1,0:T(8,128)S(1)} fusion(f32[2,1,72,136]{3,2,1,0:T(8,128)S(1)} %fusion.99, f32[1,8,72,136]{3,2,1,0:T(8,128)S(1)} %get-tuple-element.108, f32[1,8,72,136]{3,2,1,0:T(8,128)S(1)} %get-tuple-element.107, f32[2,7,72,136]{3,2,1,0:T(8,128)S(1)} %subtract_multiply_fusion.12, f32[2,8,72,136]{3,2,1,0:T(8,128)S(1)} %broadcast_multiply_fusion, ...), kind=kLoop, calls=%fused_computation.160 | loop fusion | flops 2036736 | bytes 2820128 | tf_op jit(solution)/shard_map/mul | solution.py:55
  35.7 0.1 slice_multiply_fusion.3
  35.8 0.1 fusion.88
  35.9 1.1 %fusion.85 = f32[2,8,72,136]{3,2,1,0:T(8,128)S(1)} fusion(f32[2,1,72,136]{3,2,1,0:T(8,128)S(1)} %fusion.99, f32[1,8,72,136]{3,2,1,0:T(8,128)S(1)} %get-tuple-element.106, f32[1,8,72,136]{3,2,1,0:T(8,128)S(1)} %get-tuple-element.105, f32[2,7,72,136]{3,2,1,0:T(8,128)S(1)} %fusion.88, f32[2,8,72,136]{3,2,1,0:T(8,128)S(1)} %fusion.84, ...), kind=kLoop, calls=%fused_computation.161 | loop fusion | flops 2036736 | bytes 2820128 | tf_op jit(solution)/shard_map/mul | solution.py:55
  37.0 0.1 slice_multiply_fusion.1
  37.1 0.1 fusion.87
  37.2 1.1 %fusion.86 = f32[2,8,72,136]{3,2,1,0:T(8,128)S(1)} fusion(f32[2,1,72,136]{3,2,1,0:T(8,128)S(1)} %fusion.99, f32[1,8,72,136]{3,2,1,0:T(8,128)S(1)} %get-tuple-element.104, f32[1,8,72,136]{3,2,1,0:T(8,128)S(1)} %get-tuple-element.103, f32[2,7,72,136]{3,2,1,0:T(8,128)S(1)} %fusion.87, f32[2,8,72,136]{3,2,1,0:T(8,128)S(1)} %fusion.85, ...), kind=kLoop, calls=%fused_computation.162 | loop fusion | flops 2036736 | bytes 2820128 | tf_op jit(solution)/shard_map/mul | solution.py:55
  38.3 0.2 slice_multiply_fusion.8
  38.5 0.3 fusion.97
  38.8 0.8 fusion.96
  39.7 1.9 %collective-permute-start.5 = (f32[2,32,128]{2,1,0:T(8,128)S(1)}, f32[2,32,128]{2,1,0:T(8,128)S(1)}, u32[]{:S(2)}, u32[]{:S(2)}) collective-permute-start(f32[2,32,128]{2,1,0:T(8,128)S(1)} %get-tuple-element.124), channel_id=1, source_target_pairs={{8,0},{16,8},{24,16},{32,24},{40,32},{48,40},{56,48},{64,56},{72,6... | collective-permute-start | bytes 98312 | tf_op jit(solution)/shard_map/ppermute | solution.py:271
  41.6 5.1 %collective-permute-start.4 = (f32[2,32,128]{2,1,0:T(8,128)S(1)}, f32[2,32,128]{2,1,0:T(8,128)S(1)}, u32[]{:S(2)}, u32[]{:S(2)}) collective-permute-start(f32[2,32,128]{2,1,0:T(8,128)S(1)} %get-tuple-element.123), channel_id=1, source_target_pairs={{0,8},{8,16},{16,24},{24,32},{32,40},{40,48},{48,56},{56,64},{64,7... | collective-permute-start | bytes 98312 | tf_op jit(solution)/shard_map/ppermute | solution.py:270
  46.7 0.1 fusion.118
  46.8 0.1 fusion.117
  47.2 4.1 %conditional.1 = (f32[16,2,128]{2,0,1:T(8,128)S(1)}) conditional(s32[]{:T(128)} %clamp.3, (s32[3,64]{1,0:T(4,128)S(1)}, s32[]{:T(128)}, f32[48,5,128]{2,1,0:T(8,128)S(1)}) %tuple.86, (s32[3,64]{1,0:T(4,128)S(1)}, s32[]{:T(128)}, f32[48,5,128]{2,1,0:T(8,128)S(1)}) %tuple.87, (s32[3,64]{1,0:T(4,128)S(1)}, s32[]{:T(128)}, ...), branch_computations={%region_0.3_spmd, %region_3.6_spmd, %region_6.9_spmd} | conditional | flops 31477696 | bytes 1797260 | solution.py:423
  47.2 0.6 gather_fusion.1
  47.8 0.6 gather_fusion
  48.4 1.8 %multiply_reduce_fusion.1 = (f32[16,128]{1,0:T(8,128)S(1)}, f32[16,128]{1,0:T(8,128)S(1)}) fusion(f32[16,128]{1,0:T(8,128)S(1)} %bitcast.226, f32[16,128]{1,0:T(8,128)S(1)} %bitcast.231, f32[16,128]{1,0:T(8,128)S(1)} %bitcast.227, f32[16,128]{1,0:T(8,128)S(1)} %bitcast.232, f32[16,128]{1,0:T(8,128)S(1)} %bitcast.224, f32[16,128]{1,0:T(8,128)S(1)} %bitcast.229, ...), kind=kLoop, calls=%fused_computation.19 | loop fusion | flops 7073792 | bytes 98304 | tf_op jit(solution)/shard_map/cond/branch_0_fun/reduce_sum | solution.py:73
  50.2 0.7 iota_compare_fusion.1
  50.9 0.2 fusion.5
  51.2 0.6 copy.23
  51.9 0.7 pad_maximum_fusion.4.window_ref
  52.5 4.3 %shard_map.149 = (f32[4,2048]{1,0:T(4,128)}, f32[8,38,128]{2,1,0:T(8,128)}) custom-call(f32[2,128,128]{2,1,0:T(8,128)} %pad_maximum_fusion.4.window_ref, s32[1,2048]{1,0:T(1,128)} %fusion.101.rows_ref, s32[1,2048]{1,0:T(1,128)} %get-tuple-element.57.cols_ref, f32[2,2048]{1,0:T(2,128)} %bitcast.183, f32[2,2048]{1,0:T(2,128)} %bitcast.180, ...), custom_call_target="tpu_custom_call" | custom-call | tf_op jit(solution)/shard_map/pallas_call | solution.py:252
  56.8 0.9 fusion.111
  57.7 2.4 %collective-permute-start.7 = (f32[3,38,128]{2,1,0:T(8,128)S(1)}, f32[3,38,128]{2,1,0:T(8,128)S(1)}, u32[]{:S(2)}, u32[]{:S(2)}) collective-permute-start(f32[3,38,128]{2,1,0:T(8,128)S(1)} %get-tuple-element.118), channel_id=1, source_target_pairs={{0,8},{8,16},{16,24},{24,32},{32,40},{40,48},{48,56},{56,64},{64,7... | collective-permute-start | bytes 175112 | tf_op jit(solution)/shard_map/ppermute | solution.py:270
  60.1 0.8 fusion.110
  60.9 3.4 %collective-permute-start.6 = (f32[3,38,128]{2,1,0:T(8,128)S(1)}, f32[3,38,128]{2,1,0:T(8,128)S(1)}, u32[]{:S(2)}, u32[]{:S(2)}) collective-permute-start(f32[3,38,128]{2,1,0:T(8,128)S(1)} %get-tuple-element.117), channel_id=1, source_target_pairs={{8,0},{16,8},{24,16},{32,24},{40,32},{48,40},{56,48},{64,56},{72,6... | collective-permute-start | bytes 175112 | tf_op jit(solution)/shard_map/ppermute | solution.py:271
  64.3 3.9 %collective-permute-done.6 = f32[3,38,128]{2,1,0:T(8,128)S(1)} collective-permute-done((f32[3,38,128]{2,1,0:T(8,128)S(1)}, f32[3,38,128]{2,1,0:T(8,128)S(1)}, u32[]{:S(2)}, u32[]{:S(2)}) %collective-permute-start.6) | collective-permute-done | bytes 58400 | tf_op jit(solution)/shard_map/ppermute | solution.py:271
  68.2 7.8 %collective-permute-start.8 = (f32[3,38,128]{2,1,0:T(8,128)S(1)}, f32[3,38,128]{2,1,0:T(8,128)S(1)}, u32[]{:S(2)}, u32[]{:S(2)}) collective-permute-start(f32[3,38,128]{2,1,0:T(8,128)S(1)} %pad_maximum_fusion.6), channel_id=1, source_target_pairs={{1,0},{2,1},{3,2},{4,3},{5,4},{6,5},{7,6},{128,7},{129,128},{130,1... | collective-permute-start | bytes 175112 | tf_op jit(solution)/shard_map/ppermute | solution.py:271
  76.0 1.8 %collective-permute-done.8 = f32[3,38,128]{2,1,0:T(8,128)S(1)} collective-permute-done((f32[3,38,128]{2,1,0:T(8,128)S(1)}, f32[3,38,128]{2,1,0:T(8,128)S(1)}, u32[]{:S(2)}, u32[]{:S(2)}) %collective-permute-start.8) | collective-permute-done | bytes 58400 | tf_op jit(solution)/shard_map/ppermute | solution.py:271
  77.9 1.9 %collective-permute-start.9 = (f32[3,38,128]{2,1,0:T(8,128)S(1)}, f32[3,38,128]{2,1,0:T(8,128)S(1)}, u32[]{:S(2)}, u32[]{:S(2)}) collective-permute-start(f32[3,38,128]{2,1,0:T(8,128)S(1)} %pad_maximum_fusion.7), channel_id=1, source_target_pairs={{0,1},{1,2},{2,3},{3,4},{4,5},{5,6},{6,7},{7,128},{128,129},{129,1... | collective-permute-start | bytes 175112 | tf_op jit(solution)/shard_map/ppermute | solution.py:270
  79.8 7.3 %collective-permute-done.9 = f32[3,38,128]{2,1,0:T(8,128)S(1)} collective-permute-done((f32[3,38,128]{2,1,0:T(8,128)S(1)}, f32[3,38,128]{2,1,0:T(8,128)S(1)}, u32[]{:S(2)}, u32[]{:S(2)}) %collective-permute-start.9) | collective-permute-done | bytes 58400 | tf_op jit(solution)/shard_map/ppermute | solution.py:270
  87.1 0.7 copy.18
  (91 shorter events, 0.7 us)
Async XLA Ops:
  0.6 17.1 %copy-start.1 = (f32[2,64,128]{2,1,0:T(8,128)S(1)}, f32[2,64,128]{2,1,0:T(8,128)}, u32[]{:S(2)}) copy-start(f32[2,64,128]{2,1,0:T(8,128)} %param.17) | copy-start | bytes 196612
  0.6 17.1 %copy-start = (f32[2,8,64,128]{3,2,1,0:T(8,128)S(1)}, f32[2,8,64,128]{3,2,1,0:T(8,128)}, u32[]{:S(2)}) copy-start(f32[2,8,64,128]{3,2,1,0:T(8,128)} %param.16) | copy-start | bytes 1572868
  0.7 16.9 %copy-start.5 = (f32[1,1,2048]{2,1,0:T(1,128)S(1)}, f32[1,1,2048]{2,1,0:T(1,128)}, u32[]{:S(2)}) copy-start(f32[1,1,2048]{2,1,0:T(1,128)} %param.21) | copy-start | bytes 24580
  0.7 16.9 %copy-start.3 = (f32[1,1,2,2048]{3,2,1,0:T(2,128)S(1)}, f32[1,1,2,2048]{3,2,1,0:T(2,128)}, u32[]{:S(2)}) copy-start(f32[1,1,2,2048]{3,2,1,0:T(2,128)} %param.20) | copy-start | bytes 49156
  0.7 16.9 %copy-start.4 = (f32[1,1,2,2048]{3,2,1,0:T(2,128)S(1)}, f32[1,1,2,2048]{3,2,1,0:T(2,128)}, u32[]{:S(2)}) copy-start(f32[1,1,2,2048]{3,2,1,0:T(2,128)} %param.19) | copy-start | bytes 49156
  0.7 15.5 %copy-start.6 = (s32[1,1,2048]{2,1,0:T(1,128)S(1)}, s32[1,1,2048]{2,1,0:T(1,128)}, u32[]{:S(2)}) copy-start(s32[1,1,2048]{2,1,0:T(1,128)} %param.24) | copy-start | bytes 24580
  0.7 15.5 %copy-start.8 = (s32[1,1,3,64]{3,1,2,0:T(1,128)S(1)}, s32[1,1,3,64]{3,1,2,0:T(1,128)}, u32[]{:S(2)}) copy-start(s32[1,1,3,64]{3,1,2,0:T(1,128)} %param.26) | copy-start | bytes 2308
  0.7 16.2 %copy-start.7 = (s32[1,1,8,128]{3,2,1,0:T(8,128)S(1)}, s32[1,1,8,128]{3,2,1,0:T(8,128)}, u32[]{:S(2)}) copy-start(s32[1,1,8,128]{3,2,1,0:T(8,128)} %param.27) | copy-start | bytes 12292
  0.7 16.2 %copy-start.9 = (s32[1,1,8]{2,1,0:T(1,128)S(1)}, s32[1,1,8]{2,1,0:T(1,128)}, u32[]{:S(2)}) copy-start(s32[1,1,8]{2,1,0:T(1,128)} %param.28) | copy-start | bytes 100
  4.7 12.9 %collective-permute-start.1 = (f32[20480]{0:T(1024)S(1)}, f32[20480]{0:T(1024)S(1)}, u32[]{:S(2)}, u32[]{:S(2)}) collective-permute-start(f32[20480]{0:T(1024)S(1)} %constant_dynamic-update-slice_fusion.19), channel_id=1, source_target_pairs={{8,0},{16,8},{24,16},{32,24},{40,32},{48,40},{56,48},{64,56},{72,6... | collective-permute-start | bytes 245768 | tf_op jit(solution)/shard_map/ppermute | solution.py:271
  6.8 10.9 %collective-permute-start = (f32[20480]{0:T(1024)S(1)}, f32[20480]{0:T(1024)S(1)}, u32[]{:S(2)}, u32[]{:S(2)}) collective-permute-start(f32[20480]{0:T(1024)S(1)} %constant_dynamic-update-slice_fusion.18), channel_id=1, source_target_pairs={{0,8},{8,16},{16,24},{24,32},{32,40},{40,48},{48,56},{56,64},{64,7... | collective-permute-start | bytes 245768 | tf_op jit(solution)/shard_map/ppermute | solution.py:270
  18.9 9.7 %collective-permute-start.3 = (f32[13152]{0:T(1024)S(1)}, f32[13152]{0:T(1024)S(1)}, u32[]{:S(2)}, u32[]{:S(2)}) collective-permute-start(f32[13152]{0:T(1024)S(1)} %get-tuple-element.140), channel_id=1, source_target_pairs={{1,0},{2,1},{3,2},{4,3},{5,4},{6,5},{7,6},{128,7},{129,128},{130,1... | collective-permute-start | bytes 157832 | tf_op jit(solution)/shard_map/ppermute | solution.py:271
  23.3 9.1 %collective-permute-start.2 = (f32[13152]{0:T(1024)S(1)}, f32[13152]{0:T(1024)S(1)}, u32[]{:S(2)}, u32[]{:S(2)}) collective-permute-start(f32[13152]{0:T(1024)S(1)} %get-tuple-element.139), channel_id=1, source_target_pairs={{0,1},{1,2},{2,3},{3,4},{4,5},{5,6},{6,7},{7,128},{128,129},{129,1... | collective-permute-start | bytes 157832 | tf_op jit(solution)/shard_map/ppermute | solution.py:270
  39.6 7.5 %copy-start.2 = (f32[2,8,64,128]{3,2,1,0:T(8,128)}, f32[2,8,64,128]{3,2,1,0:T(8,128)S(1)}, u32[]{:S(2)}) copy-start(f32[2,8,64,128]{3,2,1,0:T(8,128)S(1)} %fusion.96) | copy-start | bytes 1572868
  39.7 12.2 %collective-permute-start.5 = (f32[2,32,128]{2,1,0:T(8,128)S(1)}, f32[2,32,128]{2,1,0:T(8,128)S(1)}, u32[]{:S(2)}, u32[]{:S(2)}) collective-permute-start(f32[2,32,128]{2,1,0:T(8,128)S(1)} %get-tuple-element.124), channel_id=1, source_target_pairs={{8,0},{16,8},{24,16},{32,24},{40,32},{48,40},{56,48},{64,56},{72,6... | collective-permute-start | bytes 98312 | tf_op jit(solution)/shard_map/ppermute | solution.py:271
  41.6 10.3 %collective-permute-start.4 = (f32[2,32,128]{2,1,0:T(8,128)S(1)}, f32[2,32,128]{2,1,0:T(8,128)S(1)}, u32[]{:S(2)}, u32[]{:S(2)}) collective-permute-start(f32[2,32,128]{2,1,0:T(8,128)S(1)} %get-tuple-element.123), channel_id=1, source_target_pairs={{0,8},{8,16},{16,24},{24,32},{32,40},{40,48},{48,56},{56,64},{64,7... | collective-permute-start | bytes 98312 | tf_op jit(solution)/shard_map/ppermute | solution.py:270
  57.7 6.6 %collective-permute-start.7 = (f32[3,38,128]{2,1,0:T(8,128)S(1)}, f32[3,38,128]{2,1,0:T(8,128)S(1)}, u32[]{:S(2)}, u32[]{:S(2)}) collective-permute-start(f32[3,38,128]{2,1,0:T(8,128)S(1)} %get-tuple-element.118), channel_id=1, source_target_pairs={{0,8},{8,16},{16,24},{24,32},{32,40},{40,48},{48,56},{56,64},{64,7... | collective-permute-start | bytes 175112 | tf_op jit(solution)/shard_map/ppermute | solution.py:270
  60.9 7.3 %collective-permute-start.6 = (f32[3,38,128]{2,1,0:T(8,128)S(1)}, f32[3,38,128]{2,1,0:T(8,128)S(1)}, u32[]{:S(2)}, u32[]{:S(2)}) collective-permute-start(f32[3,38,128]{2,1,0:T(8,128)S(1)} %get-tuple-element.117), channel_id=1, source_target_pairs={{8,0},{16,8},{24,16},{32,24},{40,32},{48,40},{56,48},{64,56},{72,6... | collective-permute-start | bytes 175112 | tf_op jit(solution)/shard_map/ppermute | solution.py:271
  68.2 9.6 %collective-permute-start.8 = (f32[3,38,128]{2,1,0:T(8,128)S(1)}, f32[3,38,128]{2,1,0:T(8,128)S(1)}, u32[]{:S(2)}, u32[]{:S(2)}) collective-permute-start(f32[3,38,128]{2,1,0:T(8,128)S(1)} %pad_maximum_fusion.6), channel_id=1, source_target_pairs={{1,0},{2,1},{3,2},{4,3},{5,4},{6,5},{7,6},{128,7},{129,128},{130,1... | collective-permute-start | bytes 175112 | tf_op jit(solution)/shard_map/ppermute | solution.py:271
  77.9 9.2 %collective-permute-start.9 = (f32[3,38,128]{2,1,0:T(8,128)S(1)}, f32[3,38,128]{2,1,0:T(8,128)S(1)}, u32[]{:S(2)}, u32[]{:S(2)}) collective-permute-start(f32[3,38,128]{2,1,0:T(8,128)S(1)} %pad_maximum_fusion.7), channel_id=1, source_target_pairs={{0,1},{1,2},{2,3},{3,4},{4,5},{5,6},{6,7},{7,128},{128,129},{129,1... | collective-permute-start | bytes 175112 | tf_op jit(solution)/shard_map/ppermute | solution.py:270
